TPU v7x, 256 devices: a whole 4x4x8 slice. The times are simulated.
256 devices in a mesh: pipe: 4 (over y_lo, core), seq: 64 (over y_hi, z, x).
Axes of the slice: x: 4, y: 4 (y_hi: 2, y_lo: 2; y = y_hi * 2 + y_lo), z: 8, core: 2. Of those that a mesh axis runs over, the one named last changes fastest.
Arguments:
- query_act: bfloat16 [4, 24576, 2048], P('pipe', 'seq'), may hold values from -6 to 6
- key_act: bfloat16 [4, 24576, 2048], P('pipe', 'seq'), may hold values from -6 to 6
- value_act: bfloat16 [4, 24576, 2048], P('pipe', 'seq'), may hold values from -6 to 6
- out_grad: bfloat16 [4, 24576, 2048], P('pipe', 'seq'), may hold values from -6 to 6
- local_lists: int32 [192, 5], P('seq'), may hold values from 0 to 191, as said below
- strided_lists: int32 [192, 2], P('seq'), may hold values from 0 to 191, as said below
Outputs:
- handed_query: bfloat16 [4, 24576, 2048], P('pipe', 'seq')
- handed_key: bfloat16 [4, 24576, 2048], P('pipe', 'seq')
- handed_value: bfloat16 [4, 24576, 2048], P('pipe', 'seq')
Inputs may be any that keep to these rules, and one draw needn't show every extreme that they name: `local_lists`: each list names the query block itself, two different blocks 1 to 3 before it and two different blocks 1 to 3 after it, counted round the sequence. `strided_lists`: each list names the query block itself and one other block of the same aligned run of 3 blocks.
All inputs are finite; a program needn't handle non-finite values.
Results may differ from a plain program's by a relative error of at most 0.012.
Values may be sent and summed in bfloat16 or wider, within the bound.
No kernel may reach another device: no remote copies, remote signals or barrier semaphores. Data moves between devices by JAX's collectives and lax.ppermute only.
A program may use at most 192 MiB of HBM per device.

v0:
```python
import jax
import jax.numpy as jnp
from jax import lax
from jax.sharding import PartitionSpec as P

HEADS_ROW = 8
HEADS_COL = 8
HEAD_DIM = 128
COLS = 1024
BLOCK = 128
REACH = 3


def with_halo(block, sides, width):
    for axis, dim in sides:
        count = lax.axis_size(axis)
        forward = [(i, i + 1) for i in range(count - 1)]
        forward.append((count - 1, 0))
        backward = [(target, source) for source, target in forward]
        low = lax.ppermute(
            lax.slice_in_dim(block, block.shape[dim] - width, None, axis=dim), axis, forward
        )
        high = lax.ppermute(lax.slice_in_dim(block, 0, width, axis=dim), axis, backward)
        block = jnp.concatenate([low, block, high], axis=dim)
    return block


def passed_along(value, axis, steps):
    count = lax.axis_size(axis)
    pairs = [(source, (source + steps) % count) for source in range(count)]
    return lax.ppermute(value, axis, pairs)


def gather_lists(index, key_blocks, value_blocks):
    block_count, list_count = (index.shape[0], index.shape[1])
    block_rows, head_count, head_width = (
        key_blocks.shape[1],
        key_blocks.shape[2],
        key_blocks.shape[3],
    )
    flat_index = index.reshape(-1)
    key_list = jnp.take(key_blocks, flat_index, axis=0, mode="clip").reshape(
        block_count, list_count * block_rows, head_count, head_width
    )
    value_list = jnp.take(value_blocks, flat_index, axis=0, mode="clip").reshape(
        block_count, list_count * block_rows, head_count, head_width
    )
    return (key_list, value_list)


def spread_back(index, grad_klist, grad_vlist, block_rows, total):
    block_count, list_count = (index.shape[0], index.shape[1])
    head_count, head_width = (grad_klist.shape[2], grad_klist.shape[3])
    flat_index = index.reshape(-1)
    empty = jnp.zeros((total, block_rows, head_count, head_width), jnp.float32)
    grad_key = empty.at[flat_index].add(
        grad_klist.reshape(block_count * list_count, block_rows, head_count, head_width),
        mode="drop",
    )
    grad_value = empty.at[flat_index].add(
        grad_vlist.reshape(block_count * list_count, block_rows, head_count, head_width),
        mode="drop",
    )
    return (grad_key, grad_value)


def block_grads(query_blocks, key_blocks, value_blocks, grad_blocks, index):
    block_rows, head_width = (query_blocks.shape[1], query_blocks.shape[3])
    inverse_root = head_width ** (-0.5)
    key_list, value_list = gather_lists(index, key_blocks, value_blocks)
    scores = (
        jnp.einsum("nqhd,nkhd->nhqk", query_blocks, key_list, preferred_element_type=jnp.float32)
        * inverse_root
    )
    largest = jnp.max(scores, axis=-1, keepdims=True)
    raised = jnp.exp(scores - largest)
    totals = jnp.sum(raised, axis=-1, keepdims=True)
    softmax = raised / totals
    softmax_low = softmax.astype(jnp.bfloat16)
    attended = jnp.einsum(
        "nhqk,nkhd->nqhd", softmax_low, value_list, preferred_element_type=jnp.float32
    )
    row_delta = jnp.einsum("nqhd,nqhd->nhq", grad_blocks.astype(jnp.float32), attended)
    grad_softmax = jnp.einsum(
        "nqhd,nkhd->nhqk", grad_blocks, value_list, preferred_element_type=jnp.float32
    )
    grad_scores = (inverse_root * softmax * (grad_softmax - row_delta[..., None])).astype(
        jnp.bfloat16
    )
    grad_query = jnp.einsum(
        "nhqk,nkhd->nqhd", grad_scores, key_list, preferred_element_type=jnp.float32
    )
    grad_klist = jnp.einsum(
        "nhqk,nqhd->nkhd", grad_scores, query_blocks, preferred_element_type=jnp.float32
    )
    grad_vlist = jnp.einsum(
        "nhqk,nqhd->nkhd", softmax_low, grad_blocks, preferred_element_type=jnp.float32
    )
    grad_key, grad_value = spread_back(
        index, grad_klist, grad_vlist, block_rows, key_blocks.shape[0]
    )
    row_stats = jnp.stack([largest[..., 0], totals[..., 0], row_delta])
    return (grad_query, grad_key, grad_value, row_stats)


def body(query_act, key_act, value_act, out_grad, local_lists, strided_lists):
    devices = lax.axis_size("seq")
    position = lax.axis_index("seq")
    query_now = query_act[0]
    key_now = key_act[0]
    value_now = value_act[0]
    grad_now = out_grad[0]
    tokens = query_now.shape[0]
    block_count = tokens // BLOCK
    row_width = HEADS_ROW * HEAD_DIM
    col_width = HEADS_COL * HEAD_DIM
    rim_rows = REACH * BLOCK
    near = with_halo(
        jnp.stack([key_now[:, :row_width], value_now[:, :row_width]]), (("seq", 1),), rim_rows
    )
    local_index = (local_lists - (position * block_count - REACH)) % (block_count * devices)
    row_query, row_key, row_value, row_stats = block_grads(
        query_now[:, :row_width].reshape(block_count, BLOCK, HEADS_ROW, HEAD_DIM),
        near[0].reshape(-1, BLOCK, HEADS_ROW, HEAD_DIM),
        near[1].reshape(-1, BLOCK, HEADS_ROW, HEAD_DIM),
        grad_now[:, :row_width].reshape(block_count, BLOCK, HEADS_ROW, HEAD_DIM),
        local_index,
    )
    extended = jnp.stack([row_key, row_value]).reshape(2, -1, row_width)
    from_before = passed_along(extended[:, -rim_rows:].astype(jnp.bfloat16), "seq", 1).astype(
        jnp.float32
    )
    from_after = passed_along(extended[:, :rim_rows].astype(jnp.bfloat16), "seq", -1).astype(
        jnp.float32
    )
    middle = extended[:, rim_rows:-rim_rows]
    middle = middle.at[:, :rim_rows].add(from_before).at[:, -rim_rows:].add(from_after)
    own_key = middle[0]
    own_value = middle[1]
    row_grads = (
        row_query.reshape(tokens, row_width).astype(jnp.bfloat16),
        own_key.astype(jnp.bfloat16),
        own_value.astype(jnp.bfloat16),
    )
    share = tokens // devices
    grid_rows = tokens * devices // COLS
    group_cols = COLS // devices
    col_index = strided_lists - position * block_count

    def column_layout(array):
        return (
            array.reshape(grid_rows, group_cols, array.shape[2], HEAD_DIM)
            .transpose(1, 0, 2, 3)
            .reshape(block_count, BLOCK, array.shape[2], HEAD_DIM)
        )

    sent = [
        item[:, row_width:].reshape(share, devices, HEADS_COL, HEAD_DIM)
        for item in (query_now, key_now, value_now, grad_now)
    ]
    received = (
        lax.all_to_all(sent[0], "seq", split_axis=1, concat_axis=0, tiled=True),
        lax.all_to_all(sent[1], "seq", split_axis=1, concat_axis=0, tiled=True),
        lax.all_to_all(sent[2], "seq", split_axis=1, concat_axis=0, tiled=True),
        lax.all_to_all(sent[3], "seq", split_axis=1, concat_axis=0, tiled=True),
    )
    head_count = received[0].shape[2]
    results = block_grads(
        column_layout(received[0]),
        column_layout(received[1]),
        column_layout(received[2]),
        column_layout(received[3]),
        col_index,
    )[:3]
    col_result = tuple(
        (
            item.astype(jnp.bfloat16).reshape(group_cols, grid_rows, head_count, HEAD_DIM)
            for item in results
        )
    )
    head_count = col_result[0].shape[2]
    sectioned = [
        item.transpose(1, 0, 2, 3).reshape(devices, share, 1, head_count, HEAD_DIM)
        for item in col_result
    ]
    returned = (
        lax.all_to_all(sectioned[0], "seq", split_axis=0, concat_axis=2, tiled=True),
        lax.all_to_all(sectioned[1], "seq", split_axis=0, concat_axis=2, tiled=True),
        lax.all_to_all(sectioned[2], "seq", split_axis=0, concat_axis=2, tiled=True),
    )
    col_result = tuple((item.reshape(share, devices, head_count, HEAD_DIM) for item in returned))
    joined = [
        jnp.concatenate([row_grads[number], col_result[number].reshape(tokens, col_width)], axis=1)
        for number in range(3)
    ]
    handed = passed_along((joined[0], joined[1], joined[2]), "pipe", -1)
    return (handed[0][None], handed[1][None], handed[2][None])


def solution(mesh):
    in_specs = (
        P("pipe", "seq", None),
        P("pipe", "seq", None),
        P("pipe", "seq", None),
        P("pipe", "seq", None),
        P("seq", None),
        P("seq", None),
    )
    out_specs = (P("pipe", "seq", None), P("pipe", "seq", None), P("pipe", "seq", None))
    return jax.shard_map(body, mesh=mesh, in_specs=in_specs, out_specs=out_specs, check_vma=False)
```

profile of v0, /device:TPU:1, one launch (start us, length us, event | category | flops | bytes accessed | tf_op | source)
XLA Modules:
  0.0 452.8 jit_solution(4151343370061425844)
XLA Ops:
  4.2 15.1 %all-to-all-start.2 = ((bf16[6,64,8,128]{3,2,0,1:T(8,128)(2,1)}), bf16[6,64,8,128]{3,2,0,1:T(8,128)(2,1)S(1)}, u32[]{:S(2)}, u32[]{:S(2)}) async-start(bf16[6,64,8,128]{3,2,0,1:T(8,128)(2,1)} %copy.102), calls=%async_computation.2 | async-start | bytes 1572864 | tf_op jit(solution)/shard_map/all_to_all | solution.py:164
  20.5 21.5 %all-to-all-done.2 = bf16[6,64,8,128]{3,2,0,1:T(8,128)(2,1)S(1)} async-done(((bf16[6,64,8,128]{3,2,0,1:T(8,128)(2,1)}), bf16[6,64,8,128]{3,2,0,1:T(8,128)(2,1)S(1)}, u32[]{:S(2)}, u32[]{:S(2)}) %all-to-all-start.2) | async-done | bytes 786464 | tf_op jit(solution)/shard_map/all_to_all | solution.py:164
  42.0 7.2 %all-to-all-start = ((bf16[6,64,8,128]{3,2,0,1:T(8,128)(2,1)}), bf16[6,64,8,128]{3,2,0,1:T(8,128)(2,1)S(1)}, u32[]{:S(2)}, u32[]{:S(2)}) async-start(bf16[6,64,8,128]{3,2,0,1:T(8,128)(2,1)} %copy.95), calls=%async_computation | async-start | bytes 1572864 | tf_op jit(solution)/shard_map/all_to_all | solution.py:163
  52.9 18.4 %all-to-all-done = bf16[6,64,8,128]{3,2,0,1:T(8,128)(2,1)S(1)} async-done(((bf16[6,64,8,128]{3,2,0,1:T(8,128)(2,1)}), bf16[6,64,8,128]{3,2,0,1:T(8,128)(2,1)S(1)}, u32[]{:S(2)}, u32[]{:S(2)}) %all-to-all-start) | async-done | bytes 786464 | tf_op jit(solution)/shard_map/all_to_all | solution.py:163
  71.3 7.5 %all-to-all-start.1 = ((bf16[6,64,8,128]{3,2,0,1:T(8,128)(2,1)}), bf16[6,64,8,128]{3,2,0,1:T(8,128)(2,1)S(1)}, u32[]{:S(2)}, u32[]{:S(2)}) async-start(bf16[6,64,8,128]{3,2,0,1:T(8,128)(2,1)} %copy.98), calls=%async_computation.1 | async-start | bytes 1572864 | tf_op jit(solution)/shard_map/all_to_all | solution.py:162
  80.1 7.0 %collective-permute-start.1 = (bf16[2,384,1024]{2,1,0:T(8,128)(2,1)}, bf16[2,384,1024]{2,1,0:T(8,128)(2,1)}, u32[]{:S(2)}, u32[]{:S(2)}) collective-permute-start(bf16[2,384,1024]{2,1,0:T(8,128)(2,1)} %pad_maximum_fusion.1), channel_id=1, source_target_pairs={{1,0},{2,1},{3,2},{4,3},{5,4},{6,5},{7,6},{8,7},{9,8},{10,9},{11,1... | collective-permute-start | bytes 4718600 | tf_op jit(solution)/shard_map/ppermute | solution.py:23
  91.1 9.4 %all-to-all-done.1 = bf16[6,64,8,128]{3,2,0,1:T(8,128)(2,1)S(1)} async-done(((bf16[6,64,8,128]{3,2,0,1:T(8,128)(2,1)}), bf16[6,64,8,128]{3,2,0,1:T(8,128)(2,1)S(1)}, u32[]{:S(2)}, u32[]{:S(2)}) %all-to-all-start.1) | async-done | bytes 786464 | tf_op jit(solution)/shard_map/all_to_all | solution.py:162
  100.5 8.1 %all-to-all-start.3 = ((bf16[6,64,8,128]{3,2,0,1:T(8,128)(2,1)}), bf16[6,64,8,128]{3,2,0,1:T(8,128)(2,1)}, u32[]{:S(2)}, u32[]{:S(2)}) async-start(bf16[6,64,8,128]{3,2,0,1:T(8,128)(2,1)} %copy.104), calls=%async_computation.3 | async-start | bytes 1572864 | tf_op jit(solution)/shard_map/all_to_all | solution.py:165
  130.8 25.1 %all-to-all-done.3 = bf16[6,64,8,128]{3,2,0,1:T(8,128)(2,1)} async-done(((bf16[6,64,8,128]{3,2,0,1:T(8,128)(2,1)}), bf16[6,64,8,128]{3,2,0,1:T(8,128)(2,1)}, u32[]{:S(2)}, u32[]{:S(2)}) %all-to-all-start.3) | async-done | bytes 786464 | tf_op jit(solution)/shard_map/all_to_all | solution.py:165
  166.1 9.8 %all-to-all-start.4 = ((bf16[64,6,1,8,128]{4,3,1,2,0:T(8,128)(2,1)}), bf16[64,6,1,8,128]{4,3,1,2,0:T(8,128)(2,1)}, u32[]{:S(2)}, u32[]{:S(2)}) async-start(bf16[64,6,1,8,128]{4,3,1,2,0:T(8,128)(2,1)} %bitcast.48), calls=%async_computation.4 | async-start | bytes 1572864 | tf_op jit(solution)/shard_map/all_to_all | solution.py:187
  181.5 5.3 %scatter_fusion.2 = f32[3,128,8,128]{3,2,1,0:T(8,128)S(1)} fusion(f32[3,128,8,128]{3,2,1,0:T(8,128)S(1)} %broadcast_in_dim.39.clone, s32[6]{0:T(128)S(1)} %fusion.37, f32[6,128,8,128]{3,2,1,0:T(8,128)} %bitcast.226), kind=kCustom, calls=%fused_computation.6 | custom fusion | flops 786432 | bytes 9437208 | tf_op jit(solution)/shard_map/scatter-add | solution.py:56
  196.5 6.6 %copy.92 = bf16[3,640,8,128]{1,3,2,0:T(8,128)(2,1)} copy(bf16[3,640,8,128]{3,2,1,0:T(8,128)(2,1)} %bitcast.222) | data formatting | bytes 7864320 | tf_op jit(solution)/shard_map/reshape | solution.py:42
  208.3 6.5 %copy.90 = bf16[3,640,8,128]{1,3,2,0:T(8,128)(2,1)} copy(bf16[3,640,8,128]{3,2,1,0:T(8,128)(2,1)} %bitcast.221) | data formatting | bytes 7864320 | tf_op jit(solution)/shard_map/reshape | solution.py:45
  218.2 5.0 %fusion.44 = (f32[3,8,128]{2,1,0:T(8,128)S(1)}, f32[3,8,128,640]{2,3,1,0:T(8,128)S(1)}) fusion(f32[3,8,640,128]{3,2,1,0:T(8,128)S(1)} %fusion.34), kind=kOutput, calls=%fused_computation.93 | output fusion | flops 7864959 | bytes 15740928 | tf_op jit(solution)/shard_map/sub | solution.py:76
  234.0 6.6 %fusion.2 = bf16[3,8,128,640]{2,3,1,0:T(8,128)(2,1)S(1)} fusion(f32[3,8,128]{2,1,0:T(8,128)S(1)} %copy.138, f32[3,8,128,640]{2,3,1,0:T(8,128)} %copy-done.2, f32[3,8,128]{2,1,0:T(8,128)S(1)} %get-tuple-element.59, bf16[3,640,8,128]{1,3,2,0:T(8,128)(2,1)} %copy.90, bf16[3,128,8,128]{3,2,1,0:T(8,128)(2,1)S(1)} %bitcast.230), kind=kOutput, calls=%fused_computation.11 | convolution fusion | flops 513146880 | bytes 16539648 | tf_op jit(solution)/shard_map/nqhd,nkhd->nhqk/dot_general | solution.py:84
  242.5 7.6 %copy.117 = f32[3,640,8,128]{3,2,1,0:T(8,128)} copy(f32[3,640,8,128]{3,1,2,0:T(8,128)S(1)} %convolution_bitcast_fusion.1) | data formatting | bytes 15728640 | tf_op jit(solution)/shard_map/nhqk,nqhd->nkhd/transpose | solution.py:93
  252.6 18.1 %scatter_fusion = f32[9,128,8,128]{3,2,1,0:T(8,128)} fusion(f32[9,128,8,128]{3,2,1,0:T(8,128)} %broadcast_in_dim.38.clone, s32[15]{0:T(128)S(1)} %fusion.36, f32[15,128,8,128]{3,2,1,0:T(8,128)} %bitcast.216), kind=kCustom, calls=%fused_computation.4 | custom fusion | flops 1966080 | bytes 23593020 | tf_op jit(solution)/shard_map/scatter-add | solution.py:56
  270.7 6.0 %stack.21 = f32[1,1152,1024]{2,1,0:T(8,128)} reshape(f32[9,128,8,128]{3,2,1,0:T(8,128)} %scatter_fusion) | data formatting | bytes 9437184 | tf_op jit(solution)/shard_map/stack | solution.py:129
  279.9 7.6 %copy.119 = f32[3,640,8,128]{3,2,1,0:T(8,128)} copy(f32[3,640,8,128]{3,1,2,0:T(8,128)S(1)} %convolution_bitcast_fusion) | data formatting | bytes 15728640 | tf_op jit(solution)/shard_map/nhqk,nqhd->nkhd/transpose | solution.py:96
  290.0 17.9 %scatter_fusion.1 = f32[9,128,8,128]{3,2,1,0:T(8,128)} fusion(f32[9,128,8,128]{3,2,1,0:T(8,128)} %broadcast_in_dim.38.clone.1, s32[15]{0:T(128)S(1)} %fusion.36, f32[15,128,8,128]{3,2,1,0:T(8,128)} %bitcast.215), kind=kCustom, calls=%fused_computation.5 | custom fusion | flops 1966080 | bytes 23593020 | tf_op jit(solution)/shard_map/scatter-add | solution.py:60
  307.9 6.0 %stack.22 = f32[1,1152,1024]{2,1,0:T(8,128)} reshape(f32[9,128,8,128]{3,2,1,0:T(8,128)} %scatter_fusion.1) | data formatting | bytes 9437184 | tf_op jit(solution)/shard_map/stack | solution.py:129
  313.9 12.4 %all-to-all-start.5 = ((bf16[64,6,1,8,128]{4,3,1,2,0:T(8,128)(2,1)}), bf16[64,6,1,8,128]{4,3,1,2,0:T(8,128)(2,1)S(1)}, u32[]{:S(2)}, u32[]{:S(2)}) async-start(bf16[64,6,1,8,128]{4,3,1,2,0:T(8,128)(2,1)} %bitcast.64), calls=%async_computation.5 | async-start | bytes 1572864 | tf_op jit(solution)/shard_map/all_to_all | solution.py:188
  335.9 7.0 %collective-permute-start.4 = (bf16[2,384,1024]{2,1,0:T(8,128)(2,1)}, bf16[2,384,1024]{2,1,0:T(8,128)(2,1)}, u32[]{:S(2)}, u32[]{:S(2)}) collective-permute-start(bf16[2,384,1024]{2,1,0:T(8,128)(2,1)} %get-tuple-element.44), channel_id=1, source_target_pairs={{0,63},{1,0},{2,1},{3,2},{4,3},{5,4},{6,5},{7,6},{8,7},{9,8},{10,9... | collective-permute-start | bytes 4718600 | tf_op jit(solution)/shard_map/ppermute | solution.py:31
  347.4 5.3 %scatter_fusion.3 = f32[3,128,8,128]{3,2,1,0:T(8,128)S(1)} fusion(f32[3,128,8,128]{3,2,1,0:T(8,128)S(1)} %broadcast_in_dim.39.clone.1, s32[6]{0:T(128)S(1)} %fusion.37, f32[6,128,8,128]{3,2,1,0:T(8,128)} %bitcast.225), kind=kCustom, calls=%fused_computation.7 | custom fusion | flops 786432 | bytes 9437208 | tf_op jit(solution)/shard_map/scatter-add | solution.py:60
  354.0 9.4 %all-to-all-start.6 = ((bf16[64,6,1,8,128]{4,3,1,2,0:T(8,128)(2,1)}), bf16[64,6,1,8,128]{4,3,1,2,0:T(8,128)(2,1)S(1)}, u32[]{:S(2)}, u32[]{:S(2)}) async-start(bf16[64,6,1,8,128]{4,3,1,2,0:T(8,128)(2,1)} %bitcast.74), calls=%async_computation.6 | async-start | bytes 1572864 | tf_op jit(solution)/shard_map/all_to_all | solution.py:189
  363.5 4.5 fusion.25
  371.3 3.9 collective-permute-start.2
  375.5 28.3 %all-to-all-done.6 = bf16[64,6,1,8,128]{4,3,1,2,0:T(8,128)(2,1)S(1)} async-done(((bf16[64,6,1,8,128]{4,3,1,2,0:T(8,128)(2,1)}), bf16[64,6,1,8,128]{4,3,1,2,0:T(8,128)(2,1)S(1)}, u32[]{:S(2)}, u32[]{:S(2)}) %all-to-all-start.6) | async-done | bytes 786464 | tf_op jit(solution)/shard_map/all_to_all | solution.py:189
  404.1 3.7 fusion.11
  408.0 4.1 collective-permute-start.5
  412.4 18.1 %collective-permute-done.5 = bf16[384,2048]{1,0:T(8,128)(2,1)S(1)} collective-permute-done((bf16[384,2048]{1,0:T(8,128)(2,1)S(1)}, bf16[384,2048]{1,0:T(8,128)(2,1)S(1)}, u32[]{:S(2)}, u32[]{:S(2)}) %collective-permute-start.5) | collective-permute-done | bytes 1572896 | tf_op jit(solution)/shard_map/ppermute | solution.py:31
  430.5 16.9 %collective-permute-done.6 = bf16[384,2048]{1,0:T(8,128)(2,1)S(1)} collective-permute-done((bf16[384,2048]{1,0:T(8,128)(2,1)S(1)}, bf16[384,2048]{1,0:T(8,128)(2,1)S(1)}, u32[]{:S(2)}, u32[]{:S(2)}) %collective-permute-start.6) | collective-permute-done | bytes 1572896 | tf_op jit(solution)/shard_map/ppermute | solution.py:31
  (149 shorter events, 115.2 us)
Async XLA Ops:
  3.0 75.8 %copy-start.5 = (bf16[1,384,1024]{2,1,0:T(8,128)(2,1)}, bf16[1,384,1024]{2,1,0:T(8,128)(2,1)S(1)}, u32[]{:S(2)}) copy-start(bf16[1,384,1024]{2,1,0:T(8,128)(2,1)S(1)} %get-tuple-element.64) | copy-start | bytes 2359300
  4.2 37.8 %all-to-all-start.2 = ((bf16[6,64,8,128]{3,2,0,1:T(8,128)(2,1)}), bf16[6,64,8,128]{3,2,0,1:T(8,128)(2,1)S(1)}, u32[]{:S(2)}, u32[]{:S(2)}) async-start(bf16[6,64,8,128]{3,2,0,1:T(8,128)(2,1)} %copy.102), calls=%async_computation.2 | async-start | bytes 1572864 | tf_op jit(solution)/shard_map/all_to_all | solution.py:164
  42.0 9.8 %copy-start.11 = (bf16[6,64,8,128]{3,2,0,1:T(8,128)(2,1)}, bf16[6,64,8,128]{3,2,0,1:T(8,128)(2,1)S(1)}, u32[]{:S(2)}) copy-start(bf16[6,64,8,128]{3,2,0,1:T(8,128)(2,1)S(1)} %all-to-all-done.2) | copy-start | bytes 2359300
  42.0 29.2 %all-to-all-start = ((bf16[6,64,8,128]{3,2,0,1:T(8,128)(2,1)}), bf16[6,64,8,128]{3,2,0,1:T(8,128)(2,1)S(1)}, u32[]{:S(2)}, u32[]{:S(2)}) async-start(bf16[6,64,8,128]{3,2,0,1:T(8,128)(2,1)} %copy.95), calls=%async_computation | async-start | bytes 1572864 | tf_op jit(solution)/shard_map/all_to_all | solution.py:163
  51.8 35.3 %copy-start.23 = (s32[3,2]{0,1:T(2,128)S(1)}, s32[3,2]{0,1:T(2,128)}, u32[]{:S(2)}) copy-start(s32[3,2]{0,1:T(2,128)} %param.19) | copy-start | bytes 76
  51.8 35.6 %copy-start.22 = (s32[3,5]{1,0:T(4,128)S(1)}, s32[3,5]{1,0:T(4,128)}, u32[]{:S(2)}) copy-start(s32[3,5]{1,0:T(4,128)} %param.18) | copy-start | bytes 184
  71.3 18.6 %copy-start.13 = (bf16[6,64,8,128]{3,2,0,1:T(8,128)(2,1)}, bf16[6,64,8,128]{3,2,0,1:T(8,128)(2,1)S(1)}, u32[]{:S(2)}) copy-start(bf16[6,64,8,128]{3,2,0,1:T(8,128)(2,1)S(1)} %all-to-all-done) | copy-start | bytes 2359300
  71.3 29.2 %all-to-all-start.1 = ((bf16[6,64,8,128]{3,2,0,1:T(8,128)(2,1)}), bf16[6,64,8,128]{3,2,0,1:T(8,128)(2,1)S(1)}, u32[]{:S(2)}, u32[]{:S(2)}) async-start(bf16[6,64,8,128]{3,2,0,1:T(8,128)(2,1)} %copy.98), calls=%async_computation.1 | async-start | bytes 1572864 | tf_op jit(solution)/shard_map/all_to_all | solution.py:162
  80.1 108.0 %collective-permute-start.1 = (bf16[2,384,1024]{2,1,0:T(8,128)(2,1)}, bf16[2,384,1024]{2,1,0:T(8,128)(2,1)}, u32[]{:S(2)}, u32[]{:S(2)}) collective-permute-start(bf16[2,384,1024]{2,1,0:T(8,128)(2,1)} %pad_maximum_fusion.1), channel_id=1, source_target_pairs={{1,0},{2,1},{3,2},{4,3},{5,4},{6,5},{7,6},{8,7},{9,8},{10,9},{11,1... | collective-permute-start | bytes 4718600 | tf_op jit(solution)/shard_map/ppermute | solution.py:23
  87.1 101.0 %collective-permute-start = (bf16[2,384,1024]{2,1,0:T(8,128)(2,1)}, bf16[2,384,1024]{2,1,0:T(8,128)(2,1)}, u32[]{:S(2)}, u32[]{:S(2)}) collective-permute-start(bf16[2,384,1024]{2,1,0:T(8,128)(2,1)} %pad_maximum_fusion.1), channel_id=1, source_target_pairs={{0,1},{1,2},{2,3},{3,4},{4,5},{5,6},{6,7},{7,8},{8,9},{9,10},{10,1... | collective-permute-start | bytes 4718600 | tf_op jit(solution)/shard_map/ppermute | solution.py:20
  89.9 18.9 %copy-start.18 = (bf16[48,8,8,128]{3,1,2,0:T(8,128)(2,1)S(1)}, bf16[48,8,8,128]{3,1,2,0:T(8,128)(2,1)}, u32[]{:S(2)}) copy-start(bf16[48,8,8,128]{3,1,2,0:T(8,128)(2,1)} %get-tuple-element.51) | copy-start | bytes 2359300
  90.1 21.1 %copy-start.12 = (bf16[6,64,8,128]{3,2,0,1:T(8,128)(2,1)S(1)}, bf16[6,64,8,128]{3,2,0,1:T(8,128)(2,1)}, u32[]{:S(2)}) copy-start(bf16[6,64,8,128]{3,2,0,1:T(8,128)(2,1)} %copy-done.11) | copy-start | bytes 2359300
  100.5 8.2 %copy-start.15 = (bf16[6,64,8,128]{3,2,0,1:T(8,128)(2,1)}, bf16[6,64,8,128]{3,2,0,1:T(8,128)(2,1)S(1)}, u32[]{:S(2)}) copy-start(bf16[6,64,8,128]{3,2,0,1:T(8,128)(2,1)S(1)} %all-to-all-done.1) | copy-start | bytes 2359300
  100.5 55.4 %all-to-all-start.3 = ((bf16[6,64,8,128]{3,2,0,1:T(8,128)(2,1)}), bf16[6,64,8,128]{3,2,0,1:T(8,128)(2,1)}, u32[]{:S(2)}, u32[]{:S(2)}) async-start(bf16[6,64,8,128]{3,2,0,1:T(8,128)(2,1)} %copy.104), calls=%async_computation.3 | async-start | bytes 1572864 | tf_op jit(solution)/shard_map/all_to_all | solution.py:165
  111.4 4.8 %copy-start.14 = (bf16[6,64,8,128]{3,2,0,1:T(8,128)(2,1)S(1)}, bf16[6,64,8,128]{3,2,0,1:T(8,128)(2,1)}, u32[]{:S(2)}) copy-start(bf16[6,64,8,128]{3,2,0,1:T(8,128)(2,1)} %copy-done.13) | copy-start | bytes 2359300
  122.1 4.0 copy-start.21
  164.5 11.5 %copy-start.9 = (bf16[16,24,8,128]{3,2,1,0:T(8,128)(2,1)S(1)}, bf16[16,24,8,128]{3,2,1,0:T(8,128)(2,1)}, u32[]{:S(2)}) copy-start(bf16[16,24,8,128]{3,2,1,0:T(8,128)(2,1)} %copy-done.8) | copy-start | bytes 2359300
  166.1 147.7 %all-to-all-start.4 = ((bf16[64,6,1,8,128]{4,3,1,2,0:T(8,128)(2,1)}), bf16[64,6,1,8,128]{4,3,1,2,0:T(8,128)(2,1)}, u32[]{:S(2)}, u32[]{:S(2)}) async-start(bf16[64,6,1,8,128]{4,3,1,2,0:T(8,128)(2,1)} %bitcast.48), calls=%async_computation.4 | async-start | bytes 1572864 | tf_op jit(solution)/shard_map/all_to_all | solution.py:187
  223.1 4.0 copy-start.2
  223.2 5.9 %copy-start.3 = (bf16[3,640,8,128]{1,3,2,0:T(8,128)(2,1)S(1)}, bf16[3,640,8,128]{1,3,2,0:T(8,128)(2,1)}, u32[]{:S(2)}) copy-start(bf16[3,640,8,128]{1,3,2,0:T(8,128)(2,1)} %copy.90) | copy-start | bytes 11796484
  313.9 15.3 %slice-start = ((s8[4718592]{0:T(1024)(128)(4,1)}), s8[524288]{0:T(1024)(128)(4,1)S(1)}, s32[]{:S(2)}) async-start(s8[4718592]{0:T(1024)(128)(4,1)} %bitcast.217), calls=%async_computation.7 | async-start | bytes 1048576
  313.9 40.1 %all-to-all-start.5 = ((bf16[64,6,1,8,128]{4,3,1,2,0:T(8,128)(2,1)}), bf16[64,6,1,8,128]{4,3,1,2,0:T(8,128)(2,1)S(1)}, u32[]{:S(2)}, u32[]{:S(2)}) async-start(bf16[64,6,1,8,128]{4,3,1,2,0:T(8,128)(2,1)} %bitcast.64), calls=%async_computation.5 | async-start | bytes 1572864 | tf_op jit(solution)/shard_map/all_to_all | solution.py:188
  326.3 3.6 slice-start.1
  330.3 3.7 copy-start.1
  334.0 9.3 %copy-start.17 = (bf16[16,24,8,128]{3,2,1,0:T(8,128)(2,1)S(1)}, bf16[16,24,8,128]{3,2,1,0:T(8,128)(2,1)}, u32[]{:S(2)}) copy-start(bf16[16,24,8,128]{3,2,1,0:T(8,128)(2,1)} %copy-done.16) | copy-start | bytes 2359300
  334.0 9.3 %copy-start.20 = (f32[3,8,128,256]{2,3,1,0:T(8,128)S(1)}, f32[3,8,128,256]{2,3,1,0:T(8,128)}, u32[]{:S(2)}) copy-start(f32[3,8,128,256]{2,3,1,0:T(8,128)} %copy-done.19) | copy-start | bytes 9437188
  335.9 68.1 %collective-permute-start.4 = (bf16[2,384,1024]{2,1,0:T(8,128)(2,1)}, bf16[2,384,1024]{2,1,0:T(8,128)(2,1)}, u32[]{:S(2)}, u32[]{:S(2)}) collective-permute-start(bf16[2,384,1024]{2,1,0:T(8,128)(2,1)} %get-tuple-element.44), channel_id=1, source_target_pairs={{0,63},{1,0},{2,1},{3,2},{4,3},{5,4},{6,5},{7,6},{8,7},{9,8},{10,9... | collective-permute-start | bytes 4718600 | tf_op jit(solution)/shard_map/ppermute | solution.py:31
  343.0 61.1 %collective-permute-start.3 = (bf16[2,384,1024]{2,1,0:T(8,128)(2,1)}, bf16[2,384,1024]{2,1,0:T(8,128)(2,1)}, u32[]{:S(2)}, u32[]{:S(2)}) collective-permute-start(bf16[2,384,1024]{2,1,0:T(8,128)(2,1)} %get-tuple-element.43), channel_id=1, source_target_pairs={{0,1},{1,2},{2,3},{3,4},{4,5},{5,6},{6,7},{7,8},{8,9},{9,10},{10,1... | collective-permute-start | bytes 4718600 | tf_op jit(solution)/shard_map/ppermute | solution.py:31
  354.0 49.8 %all-to-all-start.6 = ((bf16[64,6,1,8,128]{4,3,1,2,0:T(8,128)(2,1)}), bf16[64,6,1,8,128]{4,3,1,2,0:T(8,128)(2,1)S(1)}, u32[]{:S(2)}, u32[]{:S(2)}) async-start(bf16[64,6,1,8,128]{4,3,1,2,0:T(8,128)(2,1)} %bitcast.74), calls=%async_computation.6 | async-start | bytes 1572864 | tf_op jit(solution)/shard_map/all_to_all | solution.py:189
  371.3 41.1 %collective-permute-start.2 = (bf16[384,2048]{1,0:T(8,128)(2,1)}, bf16[384,2048]{1,0:T(8,128)(2,1)}, u32[]{:S(2)}, u32[]{:S(2)}) collective-permute-start(bf16[384,2048]{1,0:T(8,128)(2,1)} %pad_maximum_fusion.2), channel_id=1, source_target_pairs={{0,192},{64,0},{128,64},{192,128},{1,193},{65,1},{129,65},{193,129... | collective-permute-start | bytes 4718600 | tf_op jit(solution)/shard_map/ppermute | solution.py:31
  408.0 22.5 %collective-permute-start.5 = (bf16[384,2048]{1,0:T(8,128)(2,1)S(1)}, bf16[384,2048]{1,0:T(8,128)(2,1)S(1)}, u32[]{:S(2)}, u32[]{:S(2)}) collective-permute-start(bf16[384,2048]{1,0:T(8,128)(2,1)S(1)} %pad_maximum_fusion.3), channel_id=1, source_target_pairs={{0,192},{64,0},{128,64},{192,128},{1,193},{65,1},{129,65},{193,129... | collective-permute-start | bytes 4718600 | tf_op jit(solution)/shard_map/ppermute | solution.py:31
  412.3 35.1 %collective-permute-start.6 = (bf16[384,2048]{1,0:T(8,128)(2,1)S(1)}, bf16[384,2048]{1,0:T(8,128)(2,1)S(1)}, u32[]{:S(2)}, u32[]{:S(2)}) collective-permute-start(bf16[384,2048]{1,0:T(8,128)(2,1)S(1)} %pad_maximum_fusion.4), channel_id=1, source_target_pairs={{0,192},{64,0},{128,64},{192,128},{1,193},{65,1},{129,65},{193,129... | collective-permute-start | bytes 4718600 | tf_op jit(solution)/shard_map/ppermute | solution.py:31
  (8 other events, 13.0 us)
where the time goes:
time: 460 us; the launch traced here: 453 us
  waiting for transfers between devices  138 us (30%)
  local copies, waits for them, and re-layouts  124 us (27%)
  starting transfers between devices  92 us (20%)
  other arithmetic  67.1 us (15%)
  matrix products  30.4 us (7%)
    scatter-add x4, other arithmetic, spread_back(): empty.at[flat_index]  46.7 us
    unnamed x73, local copies, waits for them, and re-layouts  39.8 us
    ppermute x5, waiting for transfers between devices, passed_along(): return lax.ppermute(value, axis, pairs)  35 us
    all_to_all x1, waiting for transfers between devices, body(): lax.all_to_all(sectioned[2], 'seq', split_axis=0, concat_axis=2, tiled=True)  28.3 us
    all_to_all x1, waiting for transfers between devices, body(): lax.all_to_all(sent[3], 'seq', split_axis=1, concat_axis=0, tiled=True)  25.1 us
    all_to_all x1, waiting for transfers between devices, body(): lax.all_to_all(sent[2], 'seq', split_axis=1, concat_axis=0, tiled=True)  21.5 us
    all_to_all x1, waiting for transfers between devices, body(): lax.all_to_all(sent[1], 'seq', split_axis=1, concat_axis=0, tiled=True)  18.4 us
    ppermute x5, starting transfers between devices, passed_along(): return lax.ppermute(value, axis, pairs)  15.3 us
  transfers between devices with their start and end apart: 14, of which 7 were waited for; matrix products, arithmetic and copies ran while one was open for 44% of the time, Pallas kernels for 0%

commit v1 on v0

v1 whole, which is shorter than its diff:
```python
import jax
import jax.numpy as jnp
from jax import lax
from jax.experimental import pallas as pl
from jax.experimental.pallas import tpu as pltpu
from jax.sharding import PartitionSpec as P

HEADS_ROW = 8
HEADS_COL = 8
HEAD_DIM = 128
COLS = 1024
BLOCK = 128
REACH = 3
GROUP_COLS = 16


def shifted(value, axis, steps):
    count = lax.axis_size(axis)
    pairs = [(source, (source + steps) % count) for source in range(count)]
    return lax.ppermute(value, axis, pairs)


def chunk_grads(q, do, k, v, keep, scale):
    scores = lax.dot_general(q, k, (((1,), (1,)), ((), ())), preferred_element_type=jnp.float32)
    scores = jnp.where(keep, scores * scale, -jnp.inf)
    largest = jnp.max(scores, axis=1, keepdims=True)
    raised = jnp.exp(scores - largest)
    softmax = raised / jnp.sum(raised, axis=1, keepdims=True)
    softmax_low = softmax.astype(jnp.bfloat16)
    attended = jnp.dot(softmax_low, v, preferred_element_type=jnp.float32)
    row_delta = jnp.sum(do.astype(jnp.float32) * attended, axis=1, keepdims=True)
    grad_softmax = lax.dot_general(
        do, v, (((1,), (1,)), ((), ())), preferred_element_type=jnp.float32
    )
    grad_scores = (scale * softmax * (grad_softmax - row_delta)).astype(jnp.bfloat16)
    grad_q = jnp.dot(grad_scores, k, preferred_element_type=jnp.float32)
    grad_k = lax.dot_general(
        grad_scores, q, (((0,), (0,)), ((), ())), preferred_element_type=jnp.float32
    )
    grad_v = lax.dot_general(
        softmax_low, do, (((0,), (0,)), ((), ())), preferred_element_type=jnp.float32
    )
    return grad_q, grad_k, grad_v


def row_kernel(
    q_ref, do_ref, kp_ref, ko_ref, kn_ref, vp_ref, vo_ref, vn_ref, keep_ref,
    dq_ref, dprev_ref, down_ref, dnext_ref, kwin, vwin, dkwin, dvwin,
):
    tokens = q_ref.shape[0]
    span = (2 * REACH + 1) * BLOCK
    scale = HEAD_DIM ** (-0.5)
    kwin[0:tokens, :] = kp_ref[...]
    kwin[tokens:2 * tokens, :] = ko_ref[...]
    kwin[2 * tokens:3 * tokens, :] = kn_ref[...]
    vwin[0:tokens, :] = vp_ref[...]
    vwin[tokens:2 * tokens, :] = vo_ref[...]
    vwin[2 * tokens:3 * tokens, :] = vn_ref[...]
    dkwin[...] = jnp.zeros_like(dkwin)
    dvwin[...] = jnp.zeros_like(dvwin)
    for i in range(tokens // BLOCK):
        rows = slice(i * BLOCK, (i + 1) * BLOCK)
        keys = slice(i * BLOCK, i * BLOCK + span)
        keep = keep_ref[i:i + 1, :] > 0.5
        grad_q, grad_k, grad_v = chunk_grads(
            q_ref[rows, :], do_ref[rows, :], kwin[keys, :], vwin[keys, :], keep, scale
        )
        dq_ref[rows, :] = grad_q.astype(dq_ref.dtype)
        dkwin[keys, :] += grad_k
        dvwin[keys, :] += grad_v
    dprev_ref[0] = dkwin[0:tokens, :].astype(dprev_ref.dtype)
    dprev_ref[1] = dvwin[0:tokens, :].astype(dprev_ref.dtype)
    down_ref[0] = dkwin[tokens:2 * tokens, :]
    down_ref[1] = dvwin[tokens:2 * tokens, :]
    dnext_ref[0] = dkwin[2 * tokens:3 * tokens, :].astype(dnext_ref.dtype)
    dnext_ref[1] = dvwin[2 * tokens:3 * tokens, :].astype(dnext_ref.dtype)


def col_kernel(q_ref, k_ref, v_ref, do_ref, keep_ref, dq_ref, dk_ref, dv_ref):
    scale = HEAD_DIM ** (-0.5)
    keep = keep_ref[...] > 0.5
    grad_q, grad_k, grad_v = chunk_grads(
        q_ref[0], do_ref[0], k_ref[0], v_ref[0], keep, scale
    )
    dq_ref[0] = grad_q.astype(dq_ref.dtype)
    dk_ref[0] = grad_k.astype(dk_ref.dtype)
    dv_ref[0] = grad_v.astype(dv_ref.dtype)


def row_side(query_now, key_now, value_now, grad_now, near_before, near_after, keep):
    tokens = query_now.shape[0]
    span = (2 * REACH + 1) * BLOCK
    head_block = lambda h: (0, h)
    stacked_block = lambda part: pl.BlockSpec((None, tokens, HEAD_DIM), lambda h: (part, 0, h))
    plain = pl.BlockSpec((tokens, HEAD_DIM), head_block)
    pair_out = pl.BlockSpec((2, tokens, HEAD_DIM), lambda h: (0, 0, h))
    return pl.pallas_call(
        row_kernel,
        grid=(HEADS_ROW,),
        in_specs=[
            plain, plain,
            stacked_block(0), plain, stacked_block(0),
            stacked_block(1), plain, stacked_block(1),
            pl.BlockSpec(keep.shape, lambda h: (0, 0)),
        ],
        out_specs=[plain, pair_out, pair_out, pair_out],
        out_shape=[
            jax.ShapeDtypeStruct((tokens, HEADS_ROW * HEAD_DIM), jnp.bfloat16),
            jax.ShapeDtypeStruct((2, tokens, HEADS_ROW * HEAD_DIM), jnp.bfloat16),
            jax.ShapeDtypeStruct((2, tokens, HEADS_ROW * HEAD_DIM), jnp.float32),
            jax.ShapeDtypeStruct((2, tokens, HEADS_ROW * HEAD_DIM), jnp.bfloat16),
        ],
        scratch_shapes=[
            pltpu.VMEM((3 * tokens, HEAD_DIM), jnp.bfloat16),
            pltpu.VMEM((3 * tokens, HEAD_DIM), jnp.bfloat16),
            pltpu.VMEM((3 * tokens, HEAD_DIM), jnp.float32),
            pltpu.VMEM((3 * tokens, HEAD_DIM), jnp.float32),
        ],
    )(
        query_now, grad_now,
        near_before, key_now, near_after,
        near_before, value_now, near_after,
        keep,
    )


def col_side(received, keep):
    tokens = received.shape[1]
    part_block = lambda part: pl.BlockSpec((1, tokens, HEAD_DIM), lambda h: (part, 0, h))
    out_block = pl.BlockSpec((1, tokens, HEAD_DIM), lambda h: (0, 0, h))
    out_struct = jax.ShapeDtypeStruct((1, tokens, HEADS_COL * HEAD_DIM), jnp.bfloat16)
    return pl.pallas_call(
        col_kernel,
        grid=(HEADS_COL,),
        in_specs=[
            part_block(0), part_block(1), part_block(2), part_block(3),
            pl.BlockSpec(keep.shape, lambda h: (0, 0)),
        ],
        out_specs=[out_block, out_block, out_block],
        out_shape=[out_struct, out_struct, out_struct],
    )(received, received, received, received, keep)


def body(query_act, key_act, value_act, out_grad, local_lists, strided_lists):
    devices = lax.axis_size("seq")
    position = lax.axis_index("seq")
    query_now = query_act[0]
    key_now = key_act[0]
    value_now = value_act[0]
    grad_now = out_grad[0]
    tokens = query_now.shape[0]
    block_count = tokens // BLOCK
    total_blocks = block_count * devices
    row_width = HEADS_ROW * HEAD_DIM
    share = tokens // devices

    sent = jnp.stack([item[:, row_width:] for item in (query_now, key_now, value_now, grad_now)])
    received = lax.all_to_all(
        sent.reshape(4, share, devices, COLS), "seq", split_axis=2, concat_axis=1, tiled=True
    ).reshape(4, tokens, COLS)

    near = jnp.stack([key_now[:, :row_width], value_now[:, :row_width]])
    near_before = shifted(near, "seq", 1)
    near_after = shifted(near, "seq", -1)

    own_blocks = position * block_count + jnp.arange(block_count, dtype=jnp.int32)
    offsets = jnp.arange(-REACH, REACH + 1, dtype=jnp.int32)
    wanted = (own_blocks[:, None] + offsets[None, :]) % total_blocks
    row_allowed = jnp.any(wanted[:, :, None] == local_lists[:, None, :], axis=2)
    row_keep = jnp.repeat(row_allowed.astype(jnp.float32), BLOCK, axis=1)

    dq_row, d_prev, d_own, d_next = row_side(
        query_now, key_now, value_now, grad_now, near_before, near_after, row_keep
    )
    from_after = shifted(d_prev, "seq", -1).astype(jnp.float32)
    from_before = shifted(d_next, "seq", 1).astype(jnp.float32)
    d_total = (d_own + from_before + from_after).astype(jnp.bfloat16)
    row_grads = jnp.concatenate([dq_row[None], d_total], axis=0)
    row_handed = shifted(row_grads, "pipe", -1)

    grid_rows = tokens * devices // COLS
    arrival = jnp.arange(tokens, dtype=jnp.int32)
    col_block = ((arrival % GROUP_COLS) * grid_rows + arrival // GROUP_COLS) // BLOCK
    local_strided = strided_lists - position * block_count
    col_allowed = jnp.any(
        local_strided[:, None, :] == jnp.arange(block_count, dtype=jnp.int32)[None, :, None], axis=2
    )
    col_keep = col_allowed[col_block][:, col_block].astype(jnp.float32)
    col_grads = jnp.concatenate(col_side(received, col_keep), axis=0)
    returned = lax.all_to_all(
        col_grads.reshape(3, devices, share, 1, COLS), "seq", split_axis=1, concat_axis=3, tiled=True
    ).reshape(3, tokens, COLS)
    col_handed = shifted(returned, "pipe", -1)

    handed = jnp.concatenate([row_handed, col_handed], axis=2)
    return (handed[0][None], handed[1][None], handed[2][None])


def solution(mesh):
    in_specs = (
        P("pipe", "seq", None),
        P("pipe", "seq", None),
        P("pipe", "seq", None),
        P("pipe", "seq", None),
        P("seq", None),
        P("seq", None),
    )
    out_specs = (P("pipe", "seq", None), P("pipe", "seq", None), P("pipe", "seq", None))
    return jax.shard_map(body, mesh=mesh, in_specs=in_specs, out_specs=out_specs, check_vma=False)
```

time: 460 us -> 371 us (0.81); the launches traced: 453 us -> 370 us
  waiting for transfers between devices: 138 us -> 246 us
  local copies, waits for them, and re-layouts: 124 us -> 26.6 us
  starting transfers between devices: 92 us -> 42.3 us
  other arithmetic: 67.1 us -> 20 us
  Pallas kernels: 0 us -> 34.7 us
  matrix products: 30.4 us -> 0 us
    ppermute x7 -> x6, waiting for transfers between devices: 35 us -> 180 us  [shifted(): return lax.ppermute(value, axis, pairs)]
    scatter-add x4 -> x0, other arithmetic: 46.7 us -> none  [spread_back(): empty.at[flat_index]]
    all_to_all x7 -> x2, starting transfers between devices: 69.6 us -> 25.8 us  [the longest x1 15.4 us: body(): lax.all_to_all(sent.reshape(4, share, devices, COLS), 'seq', split_axis=2...]
    all_to_all x7 -> x2, waiting for transfers between devices: 103 us -> 65.5 us  [the longest x1 65.5 us: body(): lax.all_to_all(sent.reshape(4, share, devices, COLS), 'seq', split_axis=2...]
    unnamed x73 -> x16, local copies, waits for them, and re-layouts: 39.8 us -> 3.26 us
    pallas_call x0 -> x2, Pallas kernels: none -> 34.7 us  [the longest x1 24.3 us: row_side(): pl.pallas_call(row_kernel, grid=(HEADS_ROW,), in_specs=[plain, plain, sta...]
    dot_general x12 -> x0, matrix products: 30.4 us -> none  [the longest x2 10.2 us: block_grads(): jnp.einsum('nqhd,nkhd->nhqk', grad_blocks, value_list, preferred_element_...]
    transpose x11 -> x0, local copies, waits for them, and re-layouts: 29.4 us -> none  [the longest x2 11.1 us: block_grads(): jnp.einsum('nhqk,nqhd->nkhd', softmax_low, grad_blocks, preferred_element...]
  transfers between devices with their start and end apart: 14 -> 8, of which waited for: 7 -> 6; matrix products, arithmetic and copies ran while one was open for 44% -> 4% of each run, Pallas kernels for 0% -> 7%
where the time goes in v1:
time: 371 us; the launch traced here: 370 us
  waiting for transfers between devices  246 us (66%)
  starting transfers between devices  42.3 us (11%)
  Pallas kernels  34.7 us (9%)
  local copies, waits for them, and re-layouts  26.6 us (7%)
  other arithmetic  20 us (5%)
    ppermute x6, waiting for transfers between devices, shifted(): return lax.ppermute(value, axis, pairs)  180 us
    all_to_all x1, waiting for transfers between devices, body(): lax.all_to_all(sent.reshape(4, share, devices, COLS), 'seq', split_axis=2...  65.5 us
    pallas_call x1, Pallas kernels, row_side(): pl.pallas_call(row_kernel, grid=(HEADS_ROW,), in_specs=[plain, plain, sta...  24.3 us
    ppermute x6, starting transfers between devices, shifted(): return lax.ppermute(value, axis, pairs)  16.5 us
    all_to_all x1, starting transfers between devices, body(): lax.all_to_all(sent.reshape(4, share, devices, COLS), 'seq', split_axis=2...  15.4 us
    all_to_all x1, starting transfers between devices, body(): lax.all_to_all(col_grads.reshape(3, devices, share, 1, COLS), 'seq', spli...  10.3 us
    pallas_call x1, Pallas kernels, col_side(): pl.pallas_call(col_kernel, grid=(HEADS_COL,), in_specs=[part_block(0), pa...  10.3 us
    another operation x1, other arithmetic, body(): jnp.stack([item[:, row_width:] for item in (query_now, key_now, value_now...  8.37 us
  transfers between devices with their start and end apart: 8, of which 6 were waited for; matrix products, arithmetic and copies ran while one was open for 4% of the time, Pallas kernels for 7%

profile of v1, /device:TPU:1, one launch (start us, length us, event | category | flops | bytes accessed | tf_op | source)
XLA Modules:
  0.0 369.9 jit_solution(2531242839694367131)
XLA Ops:
  0.6 1.3 slice.42
  1.9 1.2 copy.43
  3.3 1.2 copy.46
  5.1 1.5 fusion.8
  6.6 1.2 copy.44
  7.8 1.2 copy.45
  9.0 8.4 %pad_maximum_fusion = bf16[4,6,64,1024]{3,0,1,2:T(4,128)(2,1)} fusion(bf16[1,6,64,1024]{3,0,1,2:T(2,128)(2,1)S(1)} %copy.46, bf16[1,6,64,1024]{3,0,1,2:T(2,128)(2,1)S(1)} %copy.45, bf16[1,6,64,1024]{3,0,1,2:T(2,128)(2,1)S(1)} %copy.44, bf16[1,6,64,1024]{3,0,1,2:T(2,128)(2,1)S(1)} %copy.43), kind=kLoop, calls=%fused_computation.2 | loop fusion | flops 12582912 | bytes 6291456 | tf_op jit(solution)/shard_map/stack | solution.py:157
  17.4 15.4 %all-to-all-start = ((bf16[4,6,64,1024]{3,0,1,2:T(4,128)(2,1)}), bf16[4,6,64,1024]{3,0,1,2:T(4,128)(2,1)S(1)}, u32[]{:S(2)}, u32[]{:S(2)}) async-start(bf16[4,6,64,1024]{3,0,1,2:T(4,128)(2,1)} %pad_maximum_fusion), calls=%async_computation | async-start | bytes 6291456 | tf_op jit(solution)/shard_map/all_to_all | solution.py:158
  33.0 1.3 gather_fusion
  34.4 1.9 gather_fusion.1
  37.4 65.5 %all-to-all-done = bf16[4,6,64,1024]{3,0,1,2:T(4,128)(2,1)S(1)} async-done(((bf16[4,6,64,1024]{3,0,1,2:T(4,128)(2,1)}), bf16[4,6,64,1024]{3,0,1,2:T(4,128)(2,1)S(1)}, u32[]{:S(2)}, u32[]{:S(2)}) %all-to-all-start) | async-done | bytes 3145760 | tf_op jit(solution)/shard_map/all_to_all | solution.py:158
  103.0 2.6 copy.49.q_ref.k_ref.v_ref.do_ref
  105.6 10.3 %shard_map.86 = (bf16[1,384,1024]{2,1,0:T(8,128)(2,1)}, bf16[1,384,1024]{2,1,0:T(8,128)(2,1)}, bf16[1,384,1024]{2,1,0:T(8,128)(2,1)}) custom-call(bf16[4,384,1024]{2,1,0:T(8,128)(2,1)} %copy.49.q_ref.k_ref.v_ref.do_ref, bf16[4,384,1024]{2,1,0:T(8,128)(2,1)} %copy.49.q_ref.k_ref.v_ref.do_ref, bf16[4,384,1024]{2,1,0:T(8,128)(2,1)} %copy.49.q_ref.k_ref.v_ref.do_ref, ...), custom_call_target="tpu_custom_call" | custom-call | tf_op jit(solution)/shard_map/pallas_call | solution.py:132
  115.9 3.3 pad_maximum_fusion.2
  119.2 3.6 reshape.183
  122.8 1.9 copy.53
  124.7 10.3 %all-to-all-start.1 = ((bf16[3,64,6,1,1024]{4,2,0,3,1:T(8,128)(2,1)}), bf16[3,64,6,1,1024]{4,2,0,3,1:T(8,128)(2,1)S(1)}, u32[]{:S(2)}, u32[]{:S(2)}) async-start(bf16[3,64,6,1,1024]{4,2,0,3,1:T(8,128)(2,1)} %copy.53), calls=%async_computation.1 | async-start | bytes 6291456 | tf_op jit(solution)/shard_map/all_to_all | solution.py:190
  135.1 2.7 pad_maximum_fusion.3
  137.7 7.0 %collective-permute-start.1 = (bf16[2,384,1024]{2,1,0:T(8,128)(2,1)}, bf16[2,384,1024]{2,1,0:T(8,128)(2,1)}, u32[]{:S(2)}, u32[]{:S(2)}) collective-permute-start(bf16[2,384,1024]{2,1,0:T(8,128)(2,1)} %pad_maximum_fusion.3), channel_id=1, source_target_pairs={{0,63},{1,0},{2,1},{3,2},{4,3},{5,4},{6,5},{7,6},{8,7},{9,8},{10,9... | collective-permute-start | bytes 4718600 | tf_op jit(solution)/shard_map/ppermute | solution.py:20
  145.7 90.2 %collective-permute-done.1.kn_ref.vn_ref = bf16[2,384,1024]{2,1,0:T(8,128)(2,1)} collective-permute-done((bf16[2,384,1024]{2,1,0:T(8,128)(2,1)}, bf16[2,384,1024]{2,1,0:T(8,128)(2,1)}, u32[]{:S(2)}, u32[]{:S(2)}) %collective-permute-start.1) | collective-permute-done | bytes 1572896 | tf_op jit(solution)/shard_map/ppermute | solution.py:20
  236.0 7.5 %collective-permute-done.kp_ref.vp_ref = bf16[2,384,1024]{2,1,0:T(8,128)(2,1)} collective-permute-done((bf16[2,384,1024]{2,1,0:T(8,128)(2,1)}, bf16[2,384,1024]{2,1,0:T(8,128)(2,1)}, u32[]{:S(2)}, u32[]{:S(2)}) %collective-permute-start) | collective-permute-done | bytes 1572896 | tf_op jit(solution)/shard_map/ppermute | solution.py:20
  243.4 24.3 %shard_map.85 = (bf16[384,1024]{1,0:T(8,128)(2,1)}, bf16[2,384,1024]{2,1,0:T(8,128)(2,1)}, f32[2,384,1024]{2,1,0:T(8,128)}, bf16[2,384,1024]{2,1,0:T(8,128)(2,1)}) custom-call(bf16[384,2048]{1,0:T(8,128)(2,1)} %bitcast.36, bf16[384,2048]{1,0:T(8,128)(2,1)} %bitcast.37, bf16[2,384,1024]{2,1,0:T(8,128)(2,1)} %collective-permute-done.kp_ref.vp_ref, ...), custom_call_target="tpu_custom_call" | custom-call | tf_op jit(solution)/shard_map/pallas_call | solution.py:97
  267.9 7.2 %collective-permute-start.3 = (bf16[2,384,1024]{2,1,0:T(8,128)(2,1)}, bf16[2,384,1024]{2,1,0:T(8,128)(2,1)S(1)}, u32[]{:S(2)}, u32[]{:S(2)}) collective-permute-start(bf16[2,384,1024]{2,1,0:T(8,128)(2,1)} %get-tuple-element.13), channel_id=1, source_target_pairs={{0,63},{1,0},{2,1},{3,2},{4,3},{5,4},{6,5},{7,6},{8,7},{9,8},{10,9... | collective-permute-start | bytes 4718600 | tf_op jit(solution)/shard_map/ppermute | solution.py:20
  275.0 33.4 %collective-permute-done.2 = bf16[2,384,1024]{2,1,0:T(8,128)(2,1)S(1)} collective-permute-done((bf16[2,384,1024]{2,1,0:T(8,128)(2,1)}, bf16[2,384,1024]{2,1,0:T(8,128)(2,1)S(1)}, u32[]{:S(2)}, u32[]{:S(2)}) %collective-permute-start.2) | collective-permute-done | bytes 1572896 | tf_op jit(solution)/shard_map/ppermute | solution.py:20
  308.5 2.8 add_convert_fusion
  311.3 1.7 pad_maximum_fusion.1
  313.0 2.2 collective-permute-start.4
  315.1 1.3 copy.54
  316.5 25.7 %collective-permute-done.4 = bf16[3,384,1024]{2,1,0:T(8,128)(2,1)} collective-permute-done((bf16[3,384,1024]{2,1,0:T(8,128)(2,1)}, bf16[3,384,1024]{2,1,0:T(8,128)(2,1)}, u32[]{:S(2)}, u32[]{:S(2)}) %collective-permute-start.4) | collective-permute-done | bytes 2359328 | tf_op jit(solution)/shard_map/ppermute | solution.py:20
  342.2 1.9 constant_dynamic-update-slice_fusion.1
  344.1 23.3 %collective-permute-done.5 = bf16[3,384,1024]{2,1,0:T(8,128)(2,1)S(1)} collective-permute-done((bf16[3,384,1024]{2,1,0:T(8,128)(2,1)S(1)}, bf16[3,384,1024]{2,1,0:T(8,128)(2,1)S(1)}, u32[]{:S(2)}, u32[]{:S(2)}) %collective-permute-start.5) | collective-permute-done | bytes 2359328 | tf_op jit(solution)/shard_map/ppermute | solution.py:20
  367.6 2.4 fusion.7
  (34 shorter events, 3.4 us)
Async XLA Ops:
  0.6 2.6 copy-start.2
  3.2 1.4 copy-start
  3.2 1.9 copy-start.1
  17.4 15.5 %copy-start.5 = (s32[3,2]{0,1:T(2,128)S(1)}, s32[3,2]{0,1:T(2,128)}, u32[]{:S(2)}) copy-start(s32[3,2]{0,1:T(2,128)} %param.11) | copy-start | bytes 76
  17.4 85.5 %all-to-all-start = ((bf16[4,6,64,1024]{3,0,1,2:T(4,128)(2,1)}), bf16[4,6,64,1024]{3,0,1,2:T(4,128)(2,1)S(1)}, u32[]{:S(2)}, u32[]{:S(2)}) async-start(bf16[4,6,64,1024]{3,0,1,2:T(4,128)(2,1)} %pad_maximum_fusion), calls=%async_computation | async-start | bytes 6291456 | tf_op jit(solution)/shard_map/all_to_all | solution.py:158
  124.7 190.4 %all-to-all-start.1 = ((bf16[3,64,6,1,1024]{4,2,0,3,1:T(8,128)(2,1)}), bf16[3,64,6,1,1024]{4,2,0,3,1:T(8,128)(2,1)S(1)}, u32[]{:S(2)}, u32[]{:S(2)}) async-start(bf16[3,64,6,1,1024]{4,2,0,3,1:T(8,128)(2,1)} %copy.53), calls=%async_computation.1 | async-start | bytes 6291456 | tf_op jit(solution)/shard_map/all_to_all | solution.py:190
  135.0 9.7 %copy-start.4 = (s32[3,5]{1,0:T(4,128)S(1)}, s32[3,5]{1,0:T(4,128)}, u32[]{:S(2)}) copy-start(s32[3,5]{1,0:T(4,128)} %param.10) | copy-start | bytes 184
  137.7 98.2 %collective-permute-start.1 = (bf16[2,384,1024]{2,1,0:T(8,128)(2,1)}, bf16[2,384,1024]{2,1,0:T(8,128)(2,1)}, u32[]{:S(2)}, u32[]{:S(2)}) collective-permute-start(bf16[2,384,1024]{2,1,0:T(8,128)(2,1)} %pad_maximum_fusion.3), channel_id=1, source_target_pairs={{0,63},{1,0},{2,1},{3,2},{4,3},{5,4},{6,5},{7,6},{8,7},{9,8},{10,9... | collective-permute-start | bytes 4718600 | tf_op jit(solution)/shard_map/ppermute | solution.py:20
  144.8 98.7 %collective-permute-start = (bf16[2,384,1024]{2,1,0:T(8,128)(2,1)}, bf16[2,384,1024]{2,1,0:T(8,128)(2,1)}, u32[]{:S(2)}, u32[]{:S(2)}) collective-permute-start(bf16[2,384,1024]{2,1,0:T(8,128)(2,1)} %pad_maximum_fusion.3), channel_id=1, source_target_pairs={{0,1},{1,2},{2,3},{3,4},{4,5},{5,6},{6,7},{7,8},{8,9},{9,10},{10,1... | collective-permute-start | bytes 4718600 | tf_op jit(solution)/shard_map/ppermute | solution.py:20
  267.8 40.7 %collective-permute-start.2 = (bf16[2,384,1024]{2,1,0:T(8,128)(2,1)}, bf16[2,384,1024]{2,1,0:T(8,128)(2,1)S(1)}, u32[]{:S(2)}, u32[]{:S(2)}) collective-permute-start(bf16[2,384,1024]{2,1,0:T(8,128)(2,1)} %get-tuple-element.12), channel_id=1, source_target_pairs={{0,1},{1,2},{2,3},{3,4},{4,5},{5,6},{6,7},{7,8},{8,9},{9,10},{10,1... | collective-permute-start | bytes 4718600 | tf_op jit(solution)/shard_map/ppermute | solution.py:20
  267.9 40.6 %collective-permute-start.3 = (bf16[2,384,1024]{2,1,0:T(8,128)(2,1)}, bf16[2,384,1024]{2,1,0:T(8,128)(2,1)S(1)}, u32[]{:S(2)}, u32[]{:S(2)}) collective-permute-start(bf16[2,384,1024]{2,1,0:T(8,128)(2,1)} %get-tuple-element.13), channel_id=1, source_target_pairs={{0,63},{1,0},{2,1},{3,2},{4,3},{5,4},{6,5},{7,6},{8,7},{9,8},{10,9... | collective-permute-start | bytes 4718600 | tf_op jit(solution)/shard_map/ppermute | solution.py:20
  308.4 2.8 copy-start.3
  313.0 29.2 %collective-permute-start.4 = (bf16[3,384,1024]{2,1,0:T(8,128)(2,1)}, bf16[3,384,1024]{2,1,0:T(8,128)(2,1)}, u32[]{:S(2)}, u32[]{:S(2)}) collective-permute-start(bf16[3,384,1024]{2,1,0:T(8,128)(2,1)} %pad_maximum_fusion.1), channel_id=1, source_target_pairs={{0,192},{64,0},{128,64},{192,128},{1,193},{65,1},{129,65},{193,129... | collective-permute-start | bytes 7077896 | tf_op jit(solution)/shard_map/ppermute | solution.py:20
  316.4 50.9 %collective-permute-start.5 = (bf16[3,384,1024]{2,1,0:T(8,128)(2,1)S(1)}, bf16[3,384,1024]{2,1,0:T(8,128)(2,1)S(1)}, u32[]{:S(2)}, u32[]{:S(2)}) collective-permute-start(bf16[3,384,1024]{2,1,0:T(8,128)(2,1)S(1)} %bitcast.43), channel_id=1, source_target_pairs={{0,192},{64,0},{128,64},{192,128},{1,193},{65,1},{129,65},{193,129... | collective-permute-start | bytes 7077896 | tf_op jit(solution)/shard_map/ppermute | solution.py:20

commit v2 on v1

--- a/solution.py
+++ b/solution.py
@@ -154,14 +154,15 @@
     row_width = HEADS_ROW * HEAD_DIM
     share = tokens // devices
 
+    near = jnp.stack([key_now[:, :row_width], value_now[:, :row_width]])
+    near_before = shifted(near, "seq", 1)
+    near_after = shifted(near, "seq", -1)
+
     sent = jnp.stack([item[:, row_width:] for item in (query_now, key_now, value_now, grad_now)])
+    sent, near_before, near_after = lax.optimization_barrier((sent, near_before, near_after))
     received = lax.all_to_all(
         sent.reshape(4, share, devices, COLS), "seq", split_axis=2, concat_axis=1, tiled=True
     ).reshape(4, tokens, COLS)
-
-    near = jnp.stack([key_now[:, :row_width], value_now[:, :row_width]])
-    near_before = shifted(near, "seq", 1)
-    near_after = shifted(near, "seq", -1)
 
     own_blocks = position * block_count + jnp.arange(block_count, dtype=jnp.int32)
     offsets = jnp.arange(-REACH, REACH + 1, dtype=jnp.int32)

time: 371 us -> 336 us (0.906)
  waiting for transfers between devices: 246 us -> 231 us
  other arithmetic: 20 us -> 9.54 us
  starting transfers between devices: 42.3 us -> 35.1 us
    ppermute x6, waiting for transfers between devices: 180 us -> 165 us  [shifted(): return lax.ppermute(value, axis, pairs)]
    all_to_all x1, starting transfers between devices: 15.4 us -> 4.87 us  [body(): lax.all_to_all(sent.reshape(4, share, devices, COLS), 'seq', split_axis=2...]
    another operation x1, other arithmetic: 8.37 us -> 0.44 us  [body(): jnp.stack([item[:, row_width:] for item in (query_now, key_now, value_now...]
    another operation x4 -> x1, local copies, waits for them, and re-layouts: 4.86 us -> 0.12 us  [body(): jnp.stack([item[:, row_width:] for item in (query_now, key_now, value_now...]
    reshape x0 -> x1, local copies, waits for them, and re-layouts: none -> 4.05 us  [body(): sent.reshape(4, share, devices, COLS)]
where the time goes in v2:
time: 336 us
  waiting for transfers between devices  231 us (69%)
  starting transfers between devices  35.1 us (10%)
  Pallas kernels  34.6 us (10%)
  local copies, waits for them, and re-layouts  24.6 us (7%)
  other arithmetic  9.54 us (3%)
    ppermute x6, waiting for transfers between devices, shifted(): return lax.ppermute(value, axis, pairs)  165 us
    all_to_all x1, waiting for transfers between devices, body(): lax.all_to_all(sent.reshape(4, share, devices, COLS), 'seq', split_axis=2...  65.9 us
    pallas_call x1, Pallas kernels, row_side(): pl.pallas_call(row_kernel, grid=(HEADS_ROW,), in_specs=[plain, plain, sta...  24.3 us
    ppermute x6, starting transfers between devices, shifted(): return lax.ppermute(value, axis, pairs)  20 us
    pallas_call x1, Pallas kernels, col_side(): pl.pallas_call(col_kernel, grid=(HEADS_COL,), in_specs=[part_block(0), pa...  10.3 us
    all_to_all x1, starting transfers between devices, body(): lax.all_to_all(col_grads.reshape(3, devices, share, 1, COLS), 'seq', spli...  10.3 us
  transfers between devices with their start and end apart: 8, of which 6 were waited for; matrix products, arithmetic and copies ran while one was open for 4% of the time, Pallas kernels for 7%

profile of v2, /device:TPU:1, one launch (start us, length us, event | category | flops | bytes accessed | tf_op | source)
XLA Modules:
  0.0 335.5 jit_solution(5215332897039530384)
XLA Ops:
  0.6 2.2 slice_bitcast_fusion
  3.0 11.3 %collective-permute-start.1 = (bf16[2,384,1024]{2,1,0:T(8,128)(2,1)S(1)}, bf16[2,384,1024]{2,1,0:T(8,128)(2,1)}, u32[]{:S(2)}, u32[]{:S(2)}) collective-permute-start(bf16[2,384,1024]{2,1,0:T(8,128)(2,1)S(1)} %pad_maximum_fusion.3), channel_id=1, source_target_pairs={{0,63},{1,0},{2,1},{3,2},{4,3},{5,4},{6,5},{7,6},{8,7},{9,8},{10,9... | collective-permute-start | bytes 4718600 | tf_op jit(solution)/shard_map/ppermute | solution.py:20
  14.4 0.4 pad_maximum_fusion
  14.9 32.5 %collective-permute-done.1.kn_ref.vn_ref = bf16[2,384,1024]{2,1,0:T(8,128)(2,1)} collective-permute-done((bf16[2,384,1024]{2,1,0:T(8,128)(2,1)S(1)}, bf16[2,384,1024]{2,1,0:T(8,128)(2,1)}, u32[]{:S(2)}, u32[]{:S(2)}) %collective-permute-start.1) | collective-permute-done | bytes 1572896 | tf_op jit(solution)/shard_map/ppermute | solution.py:20
  47.3 7.7 %collective-permute-done.kp_ref.vp_ref = bf16[2,384,1024]{2,1,0:T(8,128)(2,1)} collective-permute-done((bf16[2,384,1024]{2,1,0:T(8,128)(2,1)S(1)}, bf16[2,384,1024]{2,1,0:T(8,128)(2,1)}, u32[]{:S(2)}, u32[]{:S(2)}) %collective-permute-start) | collective-permute-done | bytes 1572896 | tf_op jit(solution)/shard_map/ppermute | solution.py:20
  55.1 4.1 %copy.34 = bf16[4,6,64,1024]{3,0,1,2:T(4,128)(2,1)} copy(bf16[4,6,64,1024]{3,2,1,0:T(8,128)(2,1)S(1)} %bitcast.35) | data formatting | bytes 6291456 | tf_op jit(solution)/shard_map/reshape | solution.py:164
  59.1 4.9 %all-to-all-start = ((bf16[4,6,64,1024]{3,0,1,2:T(4,128)(2,1)}), bf16[4,6,64,1024]{3,0,1,2:T(4,128)(2,1)S(1)}, u32[]{:S(2)}, u32[]{:S(2)}) async-start(bf16[4,6,64,1024]{3,0,1,2:T(4,128)(2,1)} %copy.34), calls=%async_computation | async-start | bytes 6291456 | tf_op jit(solution)/shard_map/all_to_all | solution.py:163
  64.2 1.3 gather_fusion
  65.6 1.9 gather_fusion.1
  67.5 0.3 copy.36
  67.8 0.9 convert_bitcast_fusion.keep_ref
  68.6 65.9 %all-to-all-done = bf16[4,6,64,1024]{3,0,1,2:T(4,128)(2,1)S(1)} async-done(((bf16[4,6,64,1024]{3,0,1,2:T(4,128)(2,1)}), bf16[4,6,64,1024]{3,0,1,2:T(4,128)(2,1)S(1)}, u32[]{:S(2)}, u32[]{:S(2)}) %all-to-all-start) | async-done | bytes 3145760 | tf_op jit(solution)/shard_map/all_to_all | solution.py:163
  134.6 2.6 copy.37.q_ref.k_ref.v_ref.do_ref
  137.2 10.3 %shard_map.86 = (bf16[1,384,1024]{2,1,0:T(8,128)(2,1)}, bf16[1,384,1024]{2,1,0:T(8,128)(2,1)}, bf16[1,384,1024]{2,1,0:T(8,128)(2,1)}) custom-call(bf16[4,384,1024]{2,1,0:T(8,128)(2,1)} %copy.37.q_ref.k_ref.v_ref.do_ref, bf16[4,384,1024]{2,1,0:T(8,128)(2,1)} %copy.37.q_ref.k_ref.v_ref.do_ref, bf16[4,384,1024]{2,1,0:T(8,128)(2,1)} %copy.37.q_ref.k_ref.v_ref.do_ref, ...), custom_call_target="tpu_custom_call" | custom-call | tf_op jit(solution)/shard_map/pallas_call | solution.py:132
  147.5 3.3 pad_maximum_fusion.2
  150.8 3.6 %reshape.178 = bf16[3,64,6,1,1024]{4,2,1,0,3:T(8,128)(2,1)S(1)} reshape(bf16[3,384,1024]{2,1,0:T(8,128)(2,1)} %pad_maximum_fusion.2) | data formatting | bytes 4718592 | tf_op jit(solution)/shard_map/reshape | solution.py:192
  154.4 1.9 copy.41
  156.3 10.3 %all-to-all-start.1 = ((bf16[3,64,6,1,1024]{4,2,0,3,1:T(8,128)(2,1)}), bf16[3,64,6,1,1024]{4,2,0,3,1:T(8,128)(2,1)S(1)}, u32[]{:S(2)}, u32[]{:S(2)}) async-start(bf16[3,64,6,1,1024]{4,2,0,3,1:T(8,128)(2,1)} %copy.41), calls=%async_computation.1 | async-start | bytes 6291456 | tf_op jit(solution)/shard_map/all_to_all | solution.py:191
  166.9 0.6 copy.45
  167.5 24.3 %shard_map.85 = (bf16[384,1024]{1,0:T(8,128)(2,1)}, bf16[2,384,1024]{2,1,0:T(8,128)(2,1)}, f32[2,384,1024]{2,1,0:T(8,128)}, bf16[2,384,1024]{2,1,0:T(8,128)(2,1)}) custom-call(bf16[384,2048]{1,0:T(8,128)(2,1)} %bitcast.41, bf16[384,2048]{1,0:T(8,128)(2,1)} %bitcast.43, bf16[2,384,1024]{2,1,0:T(8,128)(2,1)} %collective-permute-done.kp_ref.vp_ref, ...), custom_call_target="tpu_custom_call" | custom-call | tf_op jit(solution)/shard_map/pallas_call | solution.py:97
  191.8 0.9 collective-permute-start.2
  192.7 6.4 %collective-permute-start.3 = (bf16[2,384,1024]{2,1,0:T(8,128)(2,1)}, bf16[2,384,1024]{2,1,0:T(8,128)(2,1)S(1)}, u32[]{:S(2)}, u32[]{:S(2)}) collective-permute-start(bf16[2,384,1024]{2,1,0:T(8,128)(2,1)} %get-tuple-element.18), channel_id=1, source_target_pairs={{0,63},{1,0},{2,1},{3,2},{4,3},{5,4},{6,5},{7,6},{8,7},{9,8},{10,9... | collective-permute-start | bytes 4718600 | tf_op jit(solution)/shard_map/ppermute | solution.py:20
  199.1 75.6 %collective-permute-done.2 = bf16[2,384,1024]{2,1,0:T(8,128)(2,1)S(1)} collective-permute-done((bf16[2,384,1024]{2,1,0:T(8,128)(2,1)}, bf16[2,384,1024]{2,1,0:T(8,128)(2,1)S(1)}, u32[]{:S(2)}, u32[]{:S(2)}) %collective-permute-start.2) | collective-permute-done | bytes 1572896 | tf_op jit(solution)/shard_map/ppermute | solution.py:20
  274.7 2.8 add_convert_fusion
  277.5 1.7 pad_maximum_fusion.1
  279.2 1.4 collective-permute-start.4
  280.5 1.3 copy.42
  281.9 25.8 %collective-permute-done.4 = bf16[3,384,1024]{2,1,0:T(8,128)(2,1)} collective-permute-done((bf16[3,384,1024]{2,1,0:T(8,128)(2,1)}, bf16[3,384,1024]{2,1,0:T(8,128)(2,1)}, u32[]{:S(2)}, u32[]{:S(2)}) %collective-permute-start.4) | collective-permute-done | bytes 2359328 | tf_op jit(solution)/shard_map/ppermute | solution.py:20
  307.8 1.9 constant_dynamic-update-slice_fusion.1
  309.7 23.3 %collective-permute-done.5 = bf16[3,384,1024]{2,1,0:T(8,128)(2,1)S(1)} collective-permute-done((bf16[3,384,1024]{2,1,0:T(8,128)(2,1)S(1)}, bf16[3,384,1024]{2,1,0:T(8,128)(2,1)S(1)}, u32[]{:S(2)}, u32[]{:S(2)}) %collective-permute-start.5) | collective-permute-done | bytes 2359328 | tf_op jit(solution)/shard_map/ppermute | solution.py:20
  332.9 0.2 constant_dynamic-update-slice_fusion
  333.1 2.4 fusion.7
  (28 shorter events, 1.0 us)
Async XLA Ops:
  2.8 11.5 %copy-start = (bf16[1,384,2048]{2,1,0:T(8,128)(2,1)S(1)}, bf16[1,384,2048]{2,1,0:T(8,128)(2,1)}, u32[]{:S(2)}) copy-start(bf16[1,384,2048]{2,1,0:T(8,128)(2,1)} %param.6) | copy-start | bytes 4718596
  2.8 11.5 %copy-start.1 = (bf16[1,384,2048]{2,1,0:T(8,128)(2,1)S(1)}, bf16[1,384,2048]{2,1,0:T(8,128)(2,1)}, u32[]{:S(2)}) copy-start(bf16[1,384,2048]{2,1,0:T(8,128)(2,1)} %param.9) | copy-start | bytes 4718596
  3.0 44.4 %collective-permute-start.1 = (bf16[2,384,1024]{2,1,0:T(8,128)(2,1)S(1)}, bf16[2,384,1024]{2,1,0:T(8,128)(2,1)}, u32[]{:S(2)}, u32[]{:S(2)}) collective-permute-start(bf16[2,384,1024]{2,1,0:T(8,128)(2,1)S(1)} %pad_maximum_fusion.3), channel_id=1, source_target_pairs={{0,63},{1,0},{2,1},{3,2},{4,3},{5,4},{6,5},{7,6},{8,7},{9,8},{10,9... | collective-permute-start | bytes 4718600 | tf_op jit(solution)/shard_map/ppermute | solution.py:20
  14.3 40.8 %collective-permute-start = (bf16[2,384,1024]{2,1,0:T(8,128)(2,1)S(1)}, bf16[2,384,1024]{2,1,0:T(8,128)(2,1)}, u32[]{:S(2)}, u32[]{:S(2)}) collective-permute-start(bf16[2,384,1024]{2,1,0:T(8,128)(2,1)S(1)} %pad_maximum_fusion.3), channel_id=1, source_target_pairs={{0,1},{1,2},{2,3},{3,4},{4,5},{5,6},{6,7},{7,8},{8,9},{9,10},{10,1... | collective-permute-start | bytes 4718600 | tf_op jit(solution)/shard_map/ppermute | solution.py:20
  59.1 4.9 %copy-start.4 = (s32[3,2]{0,1:T(2,128)S(1)}, s32[3,2]{0,1:T(2,128)}, u32[]{:S(2)}) copy-start(s32[3,2]{0,1:T(2,128)} %param.11) | copy-start | bytes 76
  59.1 75.4 %all-to-all-start = ((bf16[4,6,64,1024]{3,0,1,2:T(4,128)(2,1)}), bf16[4,6,64,1024]{3,0,1,2:T(4,128)(2,1)S(1)}, u32[]{:S(2)}, u32[]{:S(2)}) async-start(bf16[4,6,64,1024]{3,0,1,2:T(4,128)(2,1)} %copy.34), calls=%async_computation | async-start | bytes 6291456 | tf_op jit(solution)/shard_map/all_to_all | solution.py:163
  156.3 10.3 %copy-start.3 = (s32[3,5]{1,0:T(4,128)S(1)}, s32[3,5]{1,0:T(4,128)}, u32[]{:S(2)}) copy-start(s32[3,5]{1,0:T(4,128)} %param.10) | copy-start | bytes 184
  156.3 124.3 %all-to-all-start.1 = ((bf16[3,64,6,1,1024]{4,2,0,3,1:T(8,128)(2,1)}), bf16[3,64,6,1,1024]{4,2,0,3,1:T(8,128)(2,1)S(1)}, u32[]{:S(2)}, u32[]{:S(2)}) async-start(bf16[3,64,6,1,1024]{4,2,0,3,1:T(8,128)(2,1)} %copy.41), calls=%async_computation.1 | async-start | bytes 6291456 | tf_op jit(solution)/shard_map/all_to_all | solution.py:191
  191.8 82.8 %collective-permute-start.2 = (bf16[2,384,1024]{2,1,0:T(8,128)(2,1)}, bf16[2,384,1024]{2,1,0:T(8,128)(2,1)S(1)}, u32[]{:S(2)}, u32[]{:S(2)}) collective-permute-start(bf16[2,384,1024]{2,1,0:T(8,128)(2,1)} %get-tuple-element.17), channel_id=1, source_target_pairs={{0,1},{1,2},{2,3},{3,4},{4,5},{5,6},{6,7},{7,8},{8,9},{9,10},{10,1... | collective-permute-start | bytes 4718600 | tf_op jit(solution)/shard_map/ppermute | solution.py:20
  192.7 81.9 %collective-permute-start.3 = (bf16[2,384,1024]{2,1,0:T(8,128)(2,1)}, bf16[2,384,1024]{2,1,0:T(8,128)(2,1)S(1)}, u32[]{:S(2)}, u32[]{:S(2)}) collective-permute-start(bf16[2,384,1024]{2,1,0:T(8,128)(2,1)} %get-tuple-element.18), channel_id=1, source_target_pairs={{0,63},{1,0},{2,1},{3,2},{4,3},{5,4},{6,5},{7,6},{8,7},{9,8},{10,9... | collective-permute-start | bytes 4718600 | tf_op jit(solution)/shard_map/ppermute | solution.py:20
  274.7 2.8 copy-start.2
  279.2 28.6 %collective-permute-start.4 = (bf16[3,384,1024]{2,1,0:T(8,128)(2,1)}, bf16[3,384,1024]{2,1,0:T(8,128)(2,1)}, u32[]{:S(2)}, u32[]{:S(2)}) collective-permute-start(bf16[3,384,1024]{2,1,0:T(8,128)(2,1)} %pad_maximum_fusion.1), channel_id=1, source_target_pairs={{0,192},{64,0},{128,64},{192,128},{1,193},{65,1},{129,65},{193,129... | collective-permute-start | bytes 7077896 | tf_op jit(solution)/shard_map/ppermute | solution.py:20
  281.8 51.1 %collective-permute-start.5 = (bf16[3,384,1024]{2,1,0:T(8,128)(2,1)S(1)}, bf16[3,384,1024]{2,1,0:T(8,128)(2,1)S(1)}, u32[]{:S(2)}, u32[]{:S(2)}) collective-permute-start(bf16[3,384,1024]{2,1,0:T(8,128)(2,1)S(1)} %bitcast.45), channel_id=1, source_target_pairs={{0,192},{64,0},{128,64},{192,128},{1,193},{65,1},{129,65},{193,129... | collective-permute-start | bytes 7077896 | tf_op jit(solution)/shard_map/ppermute | solution.py:20

commit v3 on v2

--- a/solution.py
+++ b/solution.py
@@ -187,6 +187,9 @@
         local_strided[:, None, :] == jnp.arange(block_count, dtype=jnp.int32)[None, :, None], axis=2
     )
     col_keep = col_allowed[col_block][:, col_block].astype(jnp.float32)
+    received, dq_row, d_prev, d_own, d_next = lax.optimization_barrier(
+        (received, dq_row, d_prev, d_own, d_next)
+    )
     col_grads = jnp.concatenate(col_side(received, col_keep), axis=0)
     returned = lax.all_to_all(
         col_grads.reshape(3, devices, share, 1, COLS), "seq", split_axis=1, concat_axis=3, tiled=True

time: 336 us -> 334 us (level)
  waiting for transfers between devices: 231 us -> 224 us
  starting transfers between devices: 35.1 us -> 39.6 us
    all_to_all x1, waiting for transfers between devices: 65.9 us -> 40.5 us  [body(): lax.all_to_all(sent.reshape(4, share, devices, COLS), 'seq', split_axis=2...]
    ppermute x6, waiting for transfers between devices: 165 us -> 184 us  [shifted(): return lax.ppermute(value, axis, pairs)]
    all_to_all x1, starting transfers between devices: 4.87 us -> 9.59 us  [body(): lax.all_to_all(sent.reshape(4, share, devices, COLS), 'seq', split_axis=2...]
  transfers between devices with their start and end apart: 8 -> 8, of which waited for: 6 -> 5; matrix products, arithmetic and copies ran while one was open for 4% -> 4% of each run, Pallas kernels for 7% -> 7%
where the time goes in v3:
time: 334 us; the launch traced here: 333 us
  waiting for transfers between devices  224 us (67%)
  starting transfers between devices  39.6 us (12%)
  Pallas kernels  34.6 us (10%)
  local copies, waits for them, and re-layouts  24.7 us (7%)
  other arithmetic  9.47 us (3%)
    ppermute x6, waiting for transfers between devices, shifted(): return lax.ppermute(value, axis, pairs)  184 us
    all_to_all x1, waiting for transfers between devices, body(): lax.all_to_all(sent.reshape(4, share, devices, COLS), 'seq', split_axis=2...  40.5 us
    pallas_call x1, Pallas kernels, row_side(): pl.pallas_call(row_kernel, grid=(HEADS_ROW,), in_specs=[plain, plain, sta...  24.3 us
    ppermute x6, starting transfers between devices, shifted(): return lax.ppermute(value, axis, pairs)  20.1 us
    pallas_call x1, Pallas kernels, col_side(): pl.pallas_call(col_kernel, grid=(HEADS_COL,), in_specs=[part_block(0), pa...  10.4 us
    all_to_all x1, starting transfers between devices, body(): lax.all_to_all(col_grads.reshape(3, devices, share, 1, COLS), 'seq', spli...  9.95 us
    all_to_all x1, starting transfers between devices, body(): lax.all_to_all(sent.reshape(4, share, devices, COLS), 'seq', split_axis=2...  9.59 us
  transfers between devices with their start and end apart: 8, of which 5 were waited for; matrix products, arithmetic and copies ran while one was open for 4% of the time, Pallas kernels for 7%

profile of v3, /device:TPU:1, one launch (start us, length us, event | category | flops | bytes accessed | tf_op | source)
XLA Modules:
  0.0 333.4 jit_solution(6266124221183353561)
XLA Ops:
  0.6 2.2 slice_bitcast_fusion
  3.0 2.1 collective-permute-start
  5.1 9.3 %collective-permute-start.1 = (bf16[2,384,1024]{2,1,0:T(8,128)(2,1)S(1)}, bf16[2,384,1024]{2,1,0:T(8,128)(2,1)}, u32[]{:S(2)}, u32[]{:S(2)}) collective-permute-start(bf16[2,384,1024]{2,1,0:T(8,128)(2,1)S(1)} %pad_maximum_fusion.3), channel_id=1, source_target_pairs={{0,63},{1,0},{2,1},{3,2},{4,3},{5,4},{6,5},{7,6},{8,7},{9,8},{10,9... | collective-permute-start | bytes 4718600 | tf_op jit(solution)/shard_map/ppermute | solution.py:20
  14.5 0.4 pad_maximum_fusion
  14.9 33.5 %collective-permute-done.kp_ref.vp_ref = bf16[2,384,1024]{2,1,0:T(8,128)(2,1)} collective-permute-done((bf16[2,384,1024]{2,1,0:T(8,128)(2,1)S(1)}, bf16[2,384,1024]{2,1,0:T(8,128)(2,1)}, u32[]{:S(2)}, u32[]{:S(2)}) %collective-permute-start) | collective-permute-done | bytes 1572896 | tf_op jit(solution)/shard_map/ppermute | solution.py:20
  48.5 4.1 %copy.34 = bf16[4,6,64,1024]{3,0,1,2:T(4,128)(2,1)} copy(bf16[4,6,64,1024]{3,2,1,0:T(8,128)(2,1)S(1)} %bitcast.35) | data formatting | bytes 6291456 | tf_op jit(solution)/shard_map/reshape | solution.py:164
  52.6 9.6 %all-to-all-start = ((bf16[4,6,64,1024]{3,0,1,2:T(4,128)(2,1)}), bf16[4,6,64,1024]{3,0,1,2:T(4,128)(2,1)S(1)}, u32[]{:S(2)}, u32[]{:S(2)}) async-start(bf16[4,6,64,1024]{3,0,1,2:T(4,128)(2,1)} %copy.34), calls=%async_computation | async-start | bytes 6291456 | tf_op jit(solution)/shard_map/all_to_all | solution.py:163
  62.5 0.6 copy.45
  63.3 1.3 gather_fusion
  64.7 1.9 gather_fusion.1
  66.6 0.3 copy.36
  66.9 0.9 convert_bitcast_fusion.keep_ref
  67.8 24.3 %shard_map.85 = (bf16[384,1024]{1,0:T(8,128)(2,1)}, bf16[2,384,1024]{2,1,0:T(8,128)(2,1)}, f32[2,384,1024]{2,1,0:T(8,128)}, bf16[2,384,1024]{2,1,0:T(8,128)(2,1)}) custom-call(bf16[384,2048]{1,0:T(8,128)(2,1)} %bitcast.41, bf16[384,2048]{1,0:T(8,128)(2,1)} %bitcast.43, bf16[2,384,1024]{2,1,0:T(8,128)(2,1)} %collective-permute-done.kp_ref.vp_ref, ...), custom_call_target="tpu_custom_call" | custom-call | tf_op jit(solution)/shard_map/pallas_call | solution.py:97
  92.0 40.5 %all-to-all-done = bf16[4,6,64,1024]{3,0,1,2:T(4,128)(2,1)S(1)} async-done(((bf16[4,6,64,1024]{3,0,1,2:T(4,128)(2,1)}), bf16[4,6,64,1024]{3,0,1,2:T(4,128)(2,1)S(1)}, u32[]{:S(2)}, u32[]{:S(2)}) %all-to-all-start) | async-done | bytes 3145760 | tf_op jit(solution)/shard_map/all_to_all | solution.py:163
  132.6 2.7 copy.37.q_ref.k_ref.v_ref.do_ref
  135.2 10.4 %shard_map.86 = (bf16[1,384,1024]{2,1,0:T(8,128)(2,1)}, bf16[1,384,1024]{2,1,0:T(8,128)(2,1)}, bf16[1,384,1024]{2,1,0:T(8,128)(2,1)}) custom-call(bf16[4,384,1024]{2,1,0:T(8,128)(2,1)} %copy.37.q_ref.k_ref.v_ref.do_ref, bf16[4,384,1024]{2,1,0:T(8,128)(2,1)} %copy.37.q_ref.k_ref.v_ref.do_ref, bf16[4,384,1024]{2,1,0:T(8,128)(2,1)} %copy.37.q_ref.k_ref.v_ref.do_ref, ...), custom_call_target="tpu_custom_call" | custom-call | tf_op jit(solution)/shard_map/pallas_call | solution.py:132
  145.6 3.3 %pad_maximum_fusion.2 = bf16[3,384,1024]{2,1,0:T(8,128)(2,1)} fusion(bf16[1,384,1024]{2,1,0:T(8,128)(2,1)} %get-tuple-element.24, bf16[1,384,1024]{2,1,0:T(8,128)(2,1)} %get-tuple-element.23, bf16[1,384,1024]{2,1,0:T(8,128)(2,1)} %get-tuple-element.22), kind=kLoop, calls=%fused_computation.5 | loop fusion | flops 2359296 | bytes 4718592 | tf_op jit(solution)/shard_map/concatenate | solution.py:193
  148.9 3.6 %reshape.178 = bf16[3,64,6,1,1024]{4,2,1,0,3:T(8,128)(2,1)S(1)} reshape(bf16[3,384,1024]{2,1,0:T(8,128)(2,1)} %pad_maximum_fusion.2) | data formatting | bytes 4718592 | tf_op jit(solution)/shard_map/reshape | solution.py:195
  152.5 2.0 copy.41
  154.5 10.0 %all-to-all-start.1 = ((bf16[3,64,6,1,1024]{4,2,0,3,1:T(8,128)(2,1)}), bf16[3,64,6,1,1024]{4,2,0,3,1:T(8,128)(2,1)S(1)}, u32[]{:S(2)}, u32[]{:S(2)}) async-start(bf16[3,64,6,1,1024]{4,2,0,3,1:T(8,128)(2,1)} %copy.41), calls=%async_computation.1 | async-start | bytes 6291456 | tf_op jit(solution)/shard_map/all_to_all | solution.py:194
  164.5 1.1 collective-permute-start.2
  165.5 6.2 %collective-permute-start.3 = (bf16[2,384,1024]{2,1,0:T(8,128)(2,1)}, bf16[2,384,1024]{2,1,0:T(8,128)(2,1)S(1)}, u32[]{:S(2)}, u32[]{:S(2)}) collective-permute-start(bf16[2,384,1024]{2,1,0:T(8,128)(2,1)} %get-tuple-element.19), channel_id=1, source_target_pairs={{0,63},{1,0},{2,1},{3,2},{4,3},{5,4},{6,5},{7,6},{8,7},{9,8},{10,9... | collective-permute-start | bytes 4718600 | tf_op jit(solution)/shard_map/ppermute | solution.py:20
  171.7 101.0 %collective-permute-done.2 = bf16[2,384,1024]{2,1,0:T(8,128)(2,1)S(1)} collective-permute-done((bf16[2,384,1024]{2,1,0:T(8,128)(2,1)}, bf16[2,384,1024]{2,1,0:T(8,128)(2,1)S(1)}, u32[]{:S(2)}, u32[]{:S(2)}) %collective-permute-start.2) | collective-permute-done | bytes 1572896 | tf_op jit(solution)/shard_map/ppermute | solution.py:20
  272.7 2.7 add_convert_fusion
  275.5 1.6 pad_maximum_fusion.1
  277.1 1.4 collective-permute-start.4
  278.5 1.3 copy.42
  279.9 25.8 %collective-permute-done.4 = bf16[3,384,1024]{2,1,0:T(8,128)(2,1)} collective-permute-done((bf16[3,384,1024]{2,1,0:T(8,128)(2,1)}, bf16[3,384,1024]{2,1,0:T(8,128)(2,1)}, u32[]{:S(2)}, u32[]{:S(2)}) %collective-permute-start.4) | collective-permute-done | bytes 2359328 | tf_op jit(solution)/shard_map/ppermute | solution.py:20
  305.7 1.9 constant_dynamic-update-slice_fusion.1
  307.6 23.3 %collective-permute-done.5 = bf16[3,384,1024]{2,1,0:T(8,128)(2,1)S(1)} collective-permute-done((bf16[3,384,1024]{2,1,0:T(8,128)(2,1)S(1)}, bf16[3,384,1024]{2,1,0:T(8,128)(2,1)S(1)}, u32[]{:S(2)}, u32[]{:S(2)}) %collective-permute-start.5) | collective-permute-done | bytes 2359328 | tf_op jit(solution)/shard_map/ppermute | solution.py:20
  330.9 0.2 constant_dynamic-update-slice_fusion
  331.1 2.4 fusion.7
  (28 shorter events, 1.0 us)
Async XLA Ops:
  2.8 11.6 %copy-start = (bf16[1,384,2048]{2,1,0:T(8,128)(2,1)S(1)}, bf16[1,384,2048]{2,1,0:T(8,128)(2,1)}, u32[]{:S(2)}) copy-start(bf16[1,384,2048]{2,1,0:T(8,128)(2,1)} %param.6) | copy-start | bytes 4718596
  2.8 11.6 %copy-start.1 = (bf16[1,384,2048]{2,1,0:T(8,128)(2,1)S(1)}, bf16[1,384,2048]{2,1,0:T(8,128)(2,1)}, u32[]{:S(2)}) copy-start(bf16[1,384,2048]{2,1,0:T(8,128)(2,1)} %param.9) | copy-start | bytes 4718596
  3.0 45.5 %collective-permute-start = (bf16[2,384,1024]{2,1,0:T(8,128)(2,1)S(1)}, bf16[2,384,1024]{2,1,0:T(8,128)(2,1)}, u32[]{:S(2)}, u32[]{:S(2)}) collective-permute-start(bf16[2,384,1024]{2,1,0:T(8,128)(2,1)S(1)} %pad_maximum_fusion.3), channel_id=1, source_target_pairs={{0,1},{1,2},{2,3},{3,4},{4,5},{5,6},{6,7},{7,8},{8,9},{9,10},{10,1... | collective-permute-start | bytes 4718600 | tf_op jit(solution)/shard_map/ppermute | solution.py:20
  5.1 43.4 %collective-permute-start.1 = (bf16[2,384,1024]{2,1,0:T(8,128)(2,1)S(1)}, bf16[2,384,1024]{2,1,0:T(8,128)(2,1)}, u32[]{:S(2)}, u32[]{:S(2)}) collective-permute-start(bf16[2,384,1024]{2,1,0:T(8,128)(2,1)S(1)} %pad_maximum_fusion.3), channel_id=1, source_target_pairs={{0,63},{1,0},{2,1},{3,2},{4,3},{5,4},{6,5},{7,6},{8,7},{9,8},{10,9... | collective-permute-start | bytes 4718600 | tf_op jit(solution)/shard_map/ppermute | solution.py:20
  52.6 9.6 %copy-start.3 = (s32[3,5]{1,0:T(4,128)S(1)}, s32[3,5]{1,0:T(4,128)}, u32[]{:S(2)}) copy-start(s32[3,5]{1,0:T(4,128)} %param.10) | copy-start | bytes 184
  52.6 10.6 %copy-start.4 = (s32[3,2]{0,1:T(2,128)S(1)}, s32[3,2]{0,1:T(2,128)}, u32[]{:S(2)}) copy-start(s32[3,2]{0,1:T(2,128)} %param.11) | copy-start | bytes 76
  52.6 80.0 %all-to-all-start = ((bf16[4,6,64,1024]{3,0,1,2:T(4,128)(2,1)}), bf16[4,6,64,1024]{3,0,1,2:T(4,128)(2,1)S(1)}, u32[]{:S(2)}, u32[]{:S(2)}) async-start(bf16[4,6,64,1024]{3,0,1,2:T(4,128)(2,1)} %copy.34), calls=%async_computation | async-start | bytes 6291456 | tf_op jit(solution)/shard_map/all_to_all | solution.py:163
  154.5 124.0 %all-to-all-start.1 = ((bf16[3,64,6,1,1024]{4,2,0,3,1:T(8,128)(2,1)}), bf16[3,64,6,1,1024]{4,2,0,3,1:T(8,128)(2,1)S(1)}, u32[]{:S(2)}, u32[]{:S(2)}) async-start(bf16[3,64,6,1,1024]{4,2,0,3,1:T(8,128)(2,1)} %copy.41), calls=%async_computation.1 | async-start | bytes 6291456 | tf_op jit(solution)/shard_map/all_to_all | solution.py:194
  164.4 111.0 %copy-start.2 = (bf16[384,1024]{1,0:T(8,128)(2,1)S(1)}, bf16[384,1024]{1,0:T(8,128)(2,1)}, u32[]{:S(2)}) copy-start(bf16[384,1024]{1,0:T(8,128)(2,1)} %get-tuple-element.16) | copy-start | bytes 2359300
  164.5 108.3 %collective-permute-start.2 = (bf16[2,384,1024]{2,1,0:T(8,128)(2,1)}, bf16[2,384,1024]{2,1,0:T(8,128)(2,1)S(1)}, u32[]{:S(2)}, u32[]{:S(2)}) collective-permute-start(bf16[2,384,1024]{2,1,0:T(8,128)(2,1)} %get-tuple-element.18), channel_id=1, source_target_pairs={{0,1},{1,2},{2,3},{3,4},{4,5},{5,6},{6,7},{7,8},{8,9},{9,10},{10,1... | collective-permute-start | bytes 4718600 | tf_op jit(solution)/shard_map/ppermute | solution.py:20
  165.5 107.2 %collective-permute-start.3 = (bf16[2,384,1024]{2,1,0:T(8,128)(2,1)}, bf16[2,384,1024]{2,1,0:T(8,128)(2,1)S(1)}, u32[]{:S(2)}, u32[]{:S(2)}) collective-permute-start(bf16[2,384,1024]{2,1,0:T(8,128)(2,1)} %get-tuple-element.19), channel_id=1, source_target_pairs={{0,63},{1,0},{2,1},{3,2},{4,3},{5,4},{6,5},{7,6},{8,7},{9,8},{10,9... | collective-permute-start | bytes 4718600 | tf_op jit(solution)/shard_map/ppermute | solution.py:20
  277.1 28.6 %collective-permute-start.4 = (bf16[3,384,1024]{2,1,0:T(8,128)(2,1)}, bf16[3,384,1024]{2,1,0:T(8,128)(2,1)}, u32[]{:S(2)}, u32[]{:S(2)}) collective-permute-start(bf16[3,384,1024]{2,1,0:T(8,128)(2,1)} %pad_maximum_fusion.1), channel_id=1, source_target_pairs={{0,192},{64,0},{128,64},{192,128},{1,193},{65,1},{129,65},{193,129... | collective-permute-start | bytes 7077896 | tf_op jit(solution)/shard_map/ppermute | solution.py:20
  279.8 51.1 %collective-permute-start.5 = (bf16[3,384,1024]{2,1,0:T(8,128)(2,1)S(1)}, bf16[3,384,1024]{2,1,0:T(8,128)(2,1)S(1)}, u32[]{:S(2)}, u32[]{:S(2)}) collective-permute-start(bf16[3,384,1024]{2,1,0:T(8,128)(2,1)S(1)} %bitcast.45), channel_id=1, source_target_pairs={{0,192},{64,0},{128,64},{192,128},{1,193},{65,1},{129,65},{193,129... | collective-permute-start | bytes 7077896 | tf_op jit(solution)/shard_map/ppermute | solution.py:20

commit v4 on v2

--- a/solution.py
+++ b/solution.py
@@ -157,8 +157,9 @@
     near = jnp.stack([key_now[:, :row_width], value_now[:, :row_width]])
     near_before = shifted(near, "seq", 1)
     near_after = shifted(near, "seq", -1)
-
     sent = jnp.stack([item[:, row_width:] for item in (query_now, key_now, value_now, grad_now)])
+    sent = shifted(sent, "pipe", -1)
+
     sent, near_before, near_after = lax.optimization_barrier((sent, near_before, near_after))
     received = lax.all_to_all(
         sent.reshape(4, share, devices, COLS), "seq", split_axis=2, concat_axis=1, tiled=True
@@ -173,11 +174,12 @@
     dq_row, d_prev, d_own, d_next = row_side(
         query_now, key_now, value_now, grad_now, near_before, near_after, row_keep
     )
-    from_after = shifted(d_prev, "seq", -1).astype(jnp.float32)
-    from_before = shifted(d_next, "seq", 1).astype(jnp.float32)
-    d_total = (d_own + from_before + from_after).astype(jnp.bfloat16)
-    row_grads = jnp.concatenate([dq_row[None], d_total], axis=0)
-    row_handed = shifted(row_grads, "pipe", -1)
+
+    received, dq_row, d_prev, d_own, d_next = lax.optimization_barrier(
+        (received, dq_row, d_prev, d_own, d_next)
+    )
+    from_after = shifted(d_prev, "seq", -1)
+    from_before = shifted(d_next, "seq", 1)
 
     grid_rows = tokens * devices // COLS
     arrival = jnp.arange(tokens, dtype=jnp.int32)
@@ -188,10 +190,16 @@
     )
     col_keep = col_allowed[col_block][:, col_block].astype(jnp.float32)
     col_grads = jnp.concatenate(col_side(received, col_keep), axis=0)
-    returned = lax.all_to_all(
+
+    col_grads, from_after, from_before = lax.optimization_barrier((col_grads, from_after, from_before))
+    d_total = (d_own + from_before.astype(jnp.float32) + from_after.astype(jnp.float32)).astype(
+        jnp.bfloat16
+    )
+    row_grads = jnp.concatenate([dq_row[None], d_total], axis=0)
+    row_handed = shifted(row_grads, "pipe", -1)
+    col_handed = lax.all_to_all(
         col_grads.reshape(3, devices, share, 1, COLS), "seq", split_axis=1, concat_axis=3, tiled=True
     ).reshape(3, tokens, COLS)
-    col_handed = shifted(returned, "pipe", -1)
 
     handed = jnp.concatenate([row_handed, col_handed], axis=2)
     return (handed[0][None], handed[1][None], handed[2][None])

time: 336 us -> 301 us (0.90); the launches traced: 336 us -> 296 us
  waiting for transfers between devices: 231 us -> 189 us
  other arithmetic: 9.54 us -> 14 us
  local copies, waits for them, and re-layouts: 24.6 us -> 20.7 us
    ppermute x6, waiting for transfers between devices: 165 us -> 79.1 us  [shifted(): return lax.ppermute(value, axis, pairs)]
    all_to_all x1, waiting for transfers between devices: 0.01 us -> 63 us  [body(): lax.all_to_all(col_grads.reshape(3, devices, share, 1, COLS), 'seq', spli...]
    all_to_all x1, waiting for transfers between devices: 65.9 us -> 46.4 us  [body(): lax.all_to_all(sent.reshape(4, share, devices, COLS), 'seq', split_axis=2...]
    all_to_all x1, starting transfers between devices: 4.87 us -> 12.7 us  [body(): lax.all_to_all(sent.reshape(4, share, devices, COLS), 'seq', split_axis=2...]
    all_to_all x1, starting transfers between devices: 10.3 us -> 5.39 us  [body(): lax.all_to_all(col_grads.reshape(3, devices, share, 1, COLS), 'seq', spli...]
    concatenate x0 -> x1, other arithmetic: none -> 3.48 us  [body(): handed = jnp.concatenate([row_handed, col_handed], axis=2)]
  transfers between devices with their start and end apart: 8 -> 8, of which waited for: 6 -> 6; matrix products, arithmetic and copies ran while one was open for 4% -> 6% of each run, Pallas kernels for 7% -> 12%
where the time goes in v4:
time: 301 us; the launch traced here: 296 us
  waiting for transfers between devices  189 us (63%)
  starting transfers between devices  37.6 us (12%)
  Pallas kernels  34.7 us (12%)
  local copies, waits for them, and re-layouts  20.7 us (7%)
  other arithmetic  14 us (5%)
    ppermute x6, waiting for transfers between devices, shifted(): return lax.ppermute(value, axis, pairs)  79.1 us
    all_to_all x1, waiting for transfers between devices, body(): lax.all_to_all(col_grads.reshape(3, devices, share, 1, COLS), 'seq', spli...  63 us
    all_to_all x1, waiting for transfers between devices, body(): lax.all_to_all(sent.reshape(4, share, devices, COLS), 'seq', split_axis=2...  46.4 us
    pallas_call x1, Pallas kernels, row_side(): pl.pallas_call(row_kernel, grid=(HEADS_ROW,), in_specs=[plain, plain, sta...  24.3 us
    ppermute x6, starting transfers between devices, shifted(): return lax.ppermute(value, axis, pairs)  19.5 us
    all_to_all x1, starting transfers between devices, body(): lax.all_to_all(sent.reshape(4, share, devices, COLS), 'seq', split_axis=2...  12.7 us
    pallas_call x1, Pallas kernels, col_side(): pl.pallas_call(col_kernel, grid=(HEADS_COL,), in_specs=[part_block(0), pa...  10.3 us
  transfers between devices with their start and end apart: 8, of which 6 were waited for; matrix products, arithmetic and copies ran while one was open for 6% of the time, Pallas kernels for 12%

profile of v4, /device:TPU:1, one launch (start us, length us, event | category | flops | bytes accessed | tf_op | source)
XLA Modules:
  0.0 296.3 jit_solution(16330611189403540256)
XLA Ops:
  0.7 1.6 slice_bitcast_fusion.2
  2.5 0.5 copy-done.1
  3.0 0.4 slice_bitcast_fusion
  3.4 0.4 pad_maximum_fusion
  3.9 3.3 %collective-permute-start = (bf16[4,384,1024]{2,1,0:T(8,128)(2,1)S(1)}, bf16[4,384,1024]{2,1,0:T(8,128)(2,1)S(1)}, u32[]{:S(2)}, u32[]{:S(2)}) collective-permute-start(bf16[4,384,1024]{2,1,0:T(8,128)(2,1)S(1)} %pad_maximum_fusion), channel_id=1, source_target_pairs={{0,192},{64,0},{128,64},{192,128},{1,193},{65,1},{129,65},{193,129... | collective-permute-start | bytes 9437192 | tf_op jit(solution)/shard_map/ppermute | solution.py:20
  7.4 8.8 %collective-permute-start.2 = (bf16[2,384,1024]{2,1,0:T(8,128)(2,1)S(1)}, bf16[2,384,1024]{2,1,0:T(8,128)(2,1)}, u32[]{:S(2)}, u32[]{:S(2)}) collective-permute-start(bf16[2,384,1024]{2,1,0:T(8,128)(2,1)S(1)} %pad_maximum_fusion.4), channel_id=1, source_target_pairs={{0,63},{1,0},{2,1},{3,2},{4,3},{5,4},{6,5},{7,6},{8,7},{9,8},{10,9... | collective-permute-start | bytes 4718600 | tf_op jit(solution)/shard_map/ppermute | solution.py:20
  16.1 34.1 %collective-permute-done.1.kp_ref.vp_ref = bf16[2,384,1024]{2,1,0:T(8,128)(2,1)} collective-permute-done((bf16[2,384,1024]{2,1,0:T(8,128)(2,1)S(1)}, bf16[2,384,1024]{2,1,0:T(8,128)(2,1)}, u32[]{:S(2)}, u32[]{:S(2)}) %collective-permute-start.1) | collective-permute-done | bytes 1572896 | tf_op jit(solution)/shard_map/ppermute | solution.py:20
  50.2 25.1 %collective-permute-done = bf16[4,384,1024]{2,1,0:T(8,128)(2,1)S(1)} collective-permute-done((bf16[4,384,1024]{2,1,0:T(8,128)(2,1)S(1)}, bf16[4,384,1024]{2,1,0:T(8,128)(2,1)S(1)}, u32[]{:S(2)}, u32[]{:S(2)}) %collective-permute-start) | collective-permute-done | bytes 3145760 | tf_op jit(solution)/shard_map/ppermute | solution.py:20
  75.3 4.1 %copy.33 = bf16[4,6,64,1024]{3,0,1,2:T(4,128)(2,1)} copy(bf16[4,6,64,1024]{3,2,1,0:T(8,128)(2,1)S(1)} %bitcast.45) | data formatting | bytes 6291456 | tf_op jit(solution)/shard_map/reshape | solution.py:165
  79.4 12.7 %all-to-all-start = ((bf16[4,6,64,1024]{3,0,1,2:T(4,128)(2,1)}), bf16[4,6,64,1024]{3,0,1,2:T(4,128)(2,1)S(1)}, u32[]{:S(2)}, u32[]{:S(2)}) async-start(bf16[4,6,64,1024]{3,0,1,2:T(4,128)(2,1)} %copy.33), calls=%async_computation | async-start | bytes 6291456 | tf_op jit(solution)/shard_map/all_to_all | solution.py:164
  92.5 0.6 copy.45
  93.1 24.3 %shard_map.85 = (bf16[384,1024]{1,0:T(8,128)(2,1)}, bf16[2,384,1024]{2,1,0:T(8,128)(2,1)}, f32[2,384,1024]{2,1,0:T(8,128)}, bf16[2,384,1024]{2,1,0:T(8,128)(2,1)}) custom-call(bf16[384,2048]{1,0:T(8,128)(2,1)} %bitcast.44, bf16[384,2048]{1,0:T(8,128)(2,1)} %bitcast.42, bf16[2,384,1024]{2,1,0:T(8,128)(2,1)} %collective-permute-done.1.kp_ref.vp_ref, ...), custom_call_target="tpu_custom_call" | custom-call | tf_op jit(solution)/shard_map/pallas_call | solution.py:97
  117.4 46.4 %all-to-all-done = bf16[4,6,64,1024]{3,0,1,2:T(4,128)(2,1)S(1)} async-done(((bf16[4,6,64,1024]{3,0,1,2:T(4,128)(2,1)}), bf16[4,6,64,1024]{3,0,1,2:T(4,128)(2,1)S(1)}, u32[]{:S(2)}, u32[]{:S(2)}) %all-to-all-start) | async-done | bytes 3145760 | tf_op jit(solution)/shard_map/all_to_all | solution.py:164
  163.8 5.3 %collective-permute-start.3 = (bf16[2,384,1024]{2,1,0:T(8,128)(2,1)}, bf16[2,384,1024]{2,1,0:T(8,128)(2,1)}, u32[]{:S(2)}, u32[]{:S(2)}) collective-permute-start(bf16[2,384,1024]{2,1,0:T(8,128)(2,1)} %get-tuple-element.34), channel_id=1, source_target_pairs={{0,63},{1,0},{2,1},{3,2},{4,3},{5,4},{6,5},{7,6},{8,7},{9,8},{10,9... | collective-permute-start | bytes 4718600 | tf_op jit(solution)/shard_map/ppermute | solution.py:20
  169.3 1.3 gather_fusion
  170.7 1.9 gather_fusion.1
  172.6 0.3 copy.36
  172.9 0.9 convert_bitcast_fusion.keep_ref
  173.8 2.7 copy.37.q_ref.k_ref.v_ref.do_ref
  176.4 10.3 %shard_map.86 = (bf16[1,384,1024]{2,1,0:T(8,128)(2,1)}, bf16[1,384,1024]{2,1,0:T(8,128)(2,1)}, bf16[1,384,1024]{2,1,0:T(8,128)(2,1)}) custom-call(bf16[4,384,1024]{2,1,0:T(8,128)(2,1)} %copy.37.q_ref.k_ref.v_ref.do_ref, bf16[4,384,1024]{2,1,0:T(8,128)(2,1)} %copy.37.q_ref.k_ref.v_ref.do_ref, bf16[4,384,1024]{2,1,0:T(8,128)(2,1)} %copy.37.q_ref.k_ref.v_ref.do_ref, ...), custom_call_target="tpu_custom_call" | custom-call | tf_op jit(solution)/shard_map/pallas_call | solution.py:132
  186.8 3.3 %pad_maximum_fusion.1 = bf16[3,384,1024]{2,1,0:T(8,128)(2,1)} fusion(bf16[1,384,1024]{2,1,0:T(8,128)(2,1)} %get-tuple-element.33, bf16[1,384,1024]{2,1,0:T(8,128)(2,1)} %get-tuple-element.32, bf16[1,384,1024]{2,1,0:T(8,128)(2,1)} %get-tuple-element.31), kind=kLoop, calls=%fused_computation.8 | loop fusion | flops 2359296 | bytes 4718592 | tf_op jit(solution)/shard_map/concatenate | solution.py:192
  190.1 12.4 %collective-permute-done.3 = bf16[2,384,1024]{2,1,0:T(8,128)(2,1)} collective-permute-done((bf16[2,384,1024]{2,1,0:T(8,128)(2,1)}, bf16[2,384,1024]{2,1,0:T(8,128)(2,1)}, u32[]{:S(2)}, u32[]{:S(2)}) %collective-permute-start.3) | collective-permute-done | bytes 1572896 | tf_op jit(solution)/shard_map/ppermute | solution.py:20
  202.5 7.6 %collective-permute-done.4 = bf16[2,384,1024]{2,1,0:T(8,128)(2,1)} collective-permute-done((bf16[2,384,1024]{2,1,0:T(8,128)(2,1)}, bf16[2,384,1024]{2,1,0:T(8,128)(2,1)}, u32[]{:S(2)}, u32[]{:S(2)}) %collective-permute-start.4) | collective-permute-done | bytes 1572896 | tf_op jit(solution)/shard_map/ppermute | solution.py:20
  210.1 3.6 %reshape.178 = bf16[3,64,6,1,1024]{4,2,1,0,3:T(8,128)(2,1)S(1)} reshape(bf16[3,384,1024]{2,1,0:T(8,128)(2,1)} %pad_maximum_fusion.1) | data formatting | bytes 4718592 | tf_op jit(solution)/shard_map/reshape | solution.py:201
  213.7 2.0 copy.41
  215.7 5.4 %all-to-all-start.1 = ((bf16[3,64,6,1,1024]{4,2,0,3,1:T(8,128)(2,1)}), bf16[3,64,6,1,1024]{4,2,0,3,1:T(8,128)(2,1)S(1)}, u32[]{:S(2)}, u32[]{:S(2)}) async-start(bf16[3,64,6,1,1024]{4,2,0,3,1:T(8,128)(2,1)} %copy.41), calls=%async_computation.1 | async-start | bytes 6291456 | tf_op jit(solution)/shard_map/all_to_all | solution.py:200
  221.1 3.7 %add_convert_fusion = bf16[2,384,1024]{2,1,0:T(8,128)(2,1)S(1)} fusion(bf16[2,384,1024]{2,1,0:T(8,128)(2,1)} %collective-permute-done.3, f32[2,384,1024]{2,1,0:T(8,128)} %get-tuple-element.29, bf16[2,384,1024]{2,1,0:T(8,128)(2,1)} %collective-permute-done.4), kind=kLoop, calls=%fused_computation.7 | loop fusion | flops 3932160 | bytes 7864320 | tf_op jit(solution)/shard_map/convert_element_type | solution.py:195
  224.9 1.6 pad_maximum_fusion.2
  226.5 2.0 collective-permute-start.5
  228.5 63.0 %all-to-all-done.1 = bf16[3,64,6,1,1024]{4,2,0,3,1:T(8,128)(2,1)S(1)} async-done(((bf16[3,64,6,1,1024]{4,2,0,3,1:T(8,128)(2,1)}), bf16[3,64,6,1,1024]{4,2,0,3,1:T(8,128)(2,1)S(1)}, u32[]{:S(2)}, u32[]{:S(2)}) %all-to-all-start.1) | async-done | bytes 2359328 | tf_op jit(solution)/shard_map/all_to_all | solution.py:200
  291.5 1.3 copy.42
  292.8 3.5 %pad_maximum_fusion.3 = (bf16[1,384,2048]{2,1,0:T(8,128)(2,1)}, bf16[1,384,2048]{2,1,0:T(8,128)(2,1)}, bf16[1,384,2048]{2,1,0:T(8,128)(2,1)}) fusion(bf16[3,384,1024]{2,1,0:T(8,128)(2,1)S(1)} %bitcast.36, bf16[3,384,1024]{2,1,0:T(8,128)(2,1)} %collective-permute-done.5), kind=kLoop, calls=%fused_computation.12 | loop fusion | flops 9437184 | bytes 9437184 | tf_op jit(solution)/shard_map/concatenate | solution.py:204
  (26 shorter events, 1.0 us)
Async XLA Ops:
  0.6 1.9 copy-start
  0.6 2.3 copy-start.1
  3.9 71.4 %collective-permute-start = (bf16[4,384,1024]{2,1,0:T(8,128)(2,1)S(1)}, bf16[4,384,1024]{2,1,0:T(8,128)(2,1)S(1)}, u32[]{:S(2)}, u32[]{:S(2)}) collective-permute-start(bf16[4,384,1024]{2,1,0:T(8,128)(2,1)S(1)} %pad_maximum_fusion), channel_id=1, source_target_pairs={{0,192},{64,0},{128,64},{192,128},{1,193},{65,1},{129,65},{193,129... | collective-permute-start | bytes 9437192 | tf_op jit(solution)/shard_map/ppermute | solution.py:20
  7.3 42.9 %collective-permute-start.1 = (bf16[2,384,1024]{2,1,0:T(8,128)(2,1)S(1)}, bf16[2,384,1024]{2,1,0:T(8,128)(2,1)}, u32[]{:S(2)}, u32[]{:S(2)}) collective-permute-start(bf16[2,384,1024]{2,1,0:T(8,128)(2,1)S(1)} %pad_maximum_fusion.4), channel_id=1, source_target_pairs={{0,1},{1,2},{2,3},{3,4},{4,5},{5,6},{6,7},{7,8},{8,9},{9,10},{10,1... | collective-permute-start | bytes 4718600 | tf_op jit(solution)/shard_map/ppermute | solution.py:20
  7.4 42.8 %collective-permute-start.2 = (bf16[2,384,1024]{2,1,0:T(8,128)(2,1)S(1)}, bf16[2,384,1024]{2,1,0:T(8,128)(2,1)}, u32[]{:S(2)}, u32[]{:S(2)}) collective-permute-start(bf16[2,384,1024]{2,1,0:T(8,128)(2,1)S(1)} %pad_maximum_fusion.4), channel_id=1, source_target_pairs={{0,63},{1,0},{2,1},{3,2},{4,3},{5,4},{6,5},{7,6},{8,7},{9,8},{10,9... | collective-permute-start | bytes 4718600 | tf_op jit(solution)/shard_map/ppermute | solution.py:20
  79.4 12.7 %copy-start.3 = (s32[3,5]{1,0:T(4,128)S(1)}, s32[3,5]{1,0:T(4,128)}, u32[]{:S(2)}) copy-start(s32[3,5]{1,0:T(4,128)} %param.10) | copy-start | bytes 184
  79.4 84.5 %all-to-all-start = ((bf16[4,6,64,1024]{3,0,1,2:T(4,128)(2,1)}), bf16[4,6,64,1024]{3,0,1,2:T(4,128)(2,1)S(1)}, u32[]{:S(2)}, u32[]{:S(2)}) async-start(bf16[4,6,64,1024]{3,0,1,2:T(4,128)(2,1)} %copy.33), calls=%async_computation | async-start | bytes 6291456 | tf_op jit(solution)/shard_map/all_to_all | solution.py:164
  93.1 76.1 %copy-start.4 = (s32[3,2]{0,1:T(2,128)S(1)}, s32[3,2]{0,1:T(2,128)}, u32[]{:S(2)}) copy-start(s32[3,2]{0,1:T(2,128)} %param.11) | copy-start | bytes 76
  163.8 38.6 %collective-permute-start.3 = (bf16[2,384,1024]{2,1,0:T(8,128)(2,1)}, bf16[2,384,1024]{2,1,0:T(8,128)(2,1)}, u32[]{:S(2)}, u32[]{:S(2)}) collective-permute-start(bf16[2,384,1024]{2,1,0:T(8,128)(2,1)} %get-tuple-element.34), channel_id=1, source_target_pairs={{0,63},{1,0},{2,1},{3,2},{4,3},{5,4},{6,5},{7,6},{8,7},{9,8},{10,9... | collective-permute-start | bytes 4718600 | tf_op jit(solution)/shard_map/ppermute | solution.py:20
  169.2 41.0 %collective-permute-start.4 = (bf16[2,384,1024]{2,1,0:T(8,128)(2,1)}, bf16[2,384,1024]{2,1,0:T(8,128)(2,1)}, u32[]{:S(2)}, u32[]{:S(2)}) collective-permute-start(bf16[2,384,1024]{2,1,0:T(8,128)(2,1)} %get-tuple-element.35), channel_id=1, source_target_pairs={{0,1},{1,2},{2,3},{3,4},{4,5},{5,6},{6,7},{7,8},{8,9},{9,10},{10,1... | collective-permute-start | bytes 4718600 | tf_op jit(solution)/shard_map/ppermute | solution.py:20
  215.7 75.8 %all-to-all-start.1 = ((bf16[3,64,6,1,1024]{4,2,0,3,1:T(8,128)(2,1)}), bf16[3,64,6,1,1024]{4,2,0,3,1:T(8,128)(2,1)S(1)}, u32[]{:S(2)}, u32[]{:S(2)}) async-start(bf16[3,64,6,1,1024]{4,2,0,3,1:T(8,128)(2,1)} %copy.41), calls=%async_computation.1 | async-start | bytes 6291456 | tf_op jit(solution)/shard_map/all_to_all | solution.py:200
  221.1 3.8 %copy-start.2 = (bf16[384,1024]{1,0:T(8,128)(2,1)S(1)}, bf16[384,1024]{1,0:T(8,128)(2,1)}, u32[]{:S(2)}) copy-start(bf16[384,1024]{1,0:T(8,128)(2,1)} %get-tuple-element.28) | copy-start | bytes 2359300
  226.5 66.4 %collective-permute-start.5 = (bf16[3,384,1024]{2,1,0:T(8,128)(2,1)}, bf16[3,384,1024]{2,1,0:T(8,128)(2,1)}, u32[]{:S(2)}, u32[]{:S(2)}) collective-permute-start(bf16[3,384,1024]{2,1,0:T(8,128)(2,1)} %pad_maximum_fusion.2), channel_id=1, source_target_pairs={{0,192},{64,0},{128,64},{192,128},{1,193},{65,1},{129,65},{193,129... | collective-permute-start | bytes 7077896 | tf_op jit(solution)/shard_map/ppermute | solution.py:20

commit v5 on v1

--- a/solution.py
+++ b/solution.py
@@ -172,11 +172,10 @@
     dq_row, d_prev, d_own, d_next = row_side(
         query_now, key_now, value_now, grad_now, near_before, near_after, row_keep
     )
-    from_after = shifted(d_prev, "seq", -1).astype(jnp.float32)
-    from_before = shifted(d_next, "seq", 1).astype(jnp.float32)
-    d_total = (d_own + from_before + from_after).astype(jnp.bfloat16)
-    row_grads = jnp.concatenate([dq_row[None], d_total], axis=0)
-    row_handed = shifted(row_grads, "pipe", -1)
+    from_after = shifted(d_prev, "seq", -1)
+    from_before = shifted(d_next, "seq", 1)
+
+    received, from_after, from_before = lax.optimization_barrier((received, from_after, from_before))
 
     grid_rows = tokens * devices // COLS
     arrival = jnp.arange(tokens, dtype=jnp.int32)
@@ -187,6 +186,12 @@
     )
     col_keep = col_allowed[col_block][:, col_block].astype(jnp.float32)
     col_grads = jnp.concatenate(col_side(received, col_keep), axis=0)
+
+    d_total = (d_own + from_before.astype(jnp.float32) + from_after.astype(jnp.float32)).astype(
+        jnp.bfloat16
+    )
+    row_grads = jnp.concatenate([dq_row[None], d_total], axis=0)
+    row_handed = shifted(row_grads, "pipe", -1)
     returned = lax.all_to_all(
         col_grads.reshape(3, devices, share, 1, COLS), "seq", split_axis=1, concat_axis=3, tiled=True
     ).reshape(3, tokens, COLS)

time: 371 us -> 340 us (0.916)
  waiting for transfers between devices: 246 us -> 220 us
  starting transfers between devices: 42.3 us -> 35.5 us
    all_to_all x1, waiting for transfers between devices: 65.5 us -> 0.01 us  [body(): lax.all_to_all(sent.reshape(4, share, devices, COLS), 'seq', split_axis=2...]
    all_to_all x1, waiting for transfers between devices: 0.01 us -> 62.5 us  [body(): lax.all_to_all(col_grads.reshape(3, devices, share, 1, COLS), 'seq', spli...]
    ppermute x6, waiting for transfers between devices: 180 us -> 157 us  [shifted(): return lax.ppermute(value, axis, pairs)]
    all_to_all x1, starting transfers between devices: 10.3 us -> 5.63 us  [body(): lax.all_to_all(col_grads.reshape(3, devices, share, 1, COLS), 'seq', spli...]
  transfers between devices with their start and end apart: 8 -> 8, of which waited for: 6 -> 5; matrix products, arithmetic and copies ran while one was open for 4% -> 5% of each run, Pallas kernels for 7% -> 7%
where the time goes in v5:
time: 340 us; the launch traced here: 338 us
  waiting for transfers between devices  220 us (65%)
  starting transfers between devices  35.5 us (10%)
  Pallas kernels  34.6 us (10%)
  local copies, waits for them, and re-layouts  26.1 us (8%)
  other arithmetic  21 us (6%)
    ppermute x6, waiting for transfers between devices, shifted(): return lax.ppermute(value, axis, pairs)  157 us
    all_to_all x1, waiting for transfers between devices, body(): lax.all_to_all(col_grads.reshape(3, devices, share, 1, COLS), 'seq', spli...  62.5 us
    pallas_call x1, Pallas kernels, row_side(): pl.pallas_call(row_kernel, grid=(HEADS_ROW,), in_specs=[plain, plain, sta...  24.3 us
    all_to_all x1, starting transfers between devices, body(): lax.all_to_all(sent.reshape(4, share, devices, COLS), 'seq', split_axis=2...  15.1 us
    ppermute x6, starting transfers between devices, shifted(): return lax.ppermute(value, axis, pairs)  14.8 us
    pallas_call x1, Pallas kernels, col_side(): pl.pallas_call(col_kernel, grid=(HEADS_COL,), in_specs=[part_block(0), pa...  10.3 us
    another operation x1, other arithmetic, body(): jnp.stack([item[:, row_width:] for item in (query_now, key_now, value_now...  8.38 us
  transfers between devices with their start and end apart: 8, of which 5 were waited for; matrix products, arithmetic and copies ran while one was open for 5% of the time, Pallas kernels for 7%

profile of v5, /device:TPU:1, one launch (start us, length us, event | category | flops | bytes accessed | tf_op | source)
XLA Modules:
  0.0 337.8 jit_solution(5035570148504730780)
XLA Ops:
  0.7 1.3 slice.45
  2.0 1.2 copy.46
  3.2 1.5 slice_bitcast_fusion
  4.8 1.2 copy.45
  6.0 1.2 copy.44
  7.3 1.2 copy.43
  8.5 8.4 %pad_maximum_fusion = bf16[4,6,64,1024]{3,0,1,2:T(4,128)(2,1)} fusion(bf16[1,6,64,1024]{3,0,1,2:T(2,128)(2,1)S(1)} %copy.46, bf16[1,6,64,1024]{3,0,1,2:T(2,128)(2,1)S(1)} %copy.45, bf16[1,6,64,1024]{3,0,1,2:T(2,128)(2,1)S(1)} %copy.44, bf16[1,6,64,1024]{3,0,1,2:T(2,128)(2,1)S(1)} %copy.43), kind=kLoop, calls=%fused_computation.2 | loop fusion | flops 12582912 | bytes 6291456 | tf_op jit(solution)/shard_map/stack | solution.py:157
  16.9 15.1 %all-to-all-start = ((bf16[4,6,64,1024]{3,0,1,2:T(4,128)(2,1)}), bf16[4,6,64,1024]{3,0,1,2:T(4,128)(2,1)S(1)}, u32[]{:S(2)}, u32[]{:S(2)}) async-start(bf16[4,6,64,1024]{3,0,1,2:T(4,128)(2,1)} %pad_maximum_fusion), calls=%async_computation | async-start | bytes 6291456 | tf_op jit(solution)/shard_map/all_to_all | solution.py:158
  32.0 2.7 pad_maximum_fusion.3
  34.7 1.0 collective-permute-start
  35.7 6.2 %collective-permute-start.1 = (bf16[2,384,1024]{2,1,0:T(8,128)(2,1)}, bf16[2,384,1024]{2,1,0:T(8,128)(2,1)}, u32[]{:S(2)}, u32[]{:S(2)}) collective-permute-start(bf16[2,384,1024]{2,1,0:T(8,128)(2,1)} %pad_maximum_fusion.3), channel_id=1, source_target_pairs={{0,63},{1,0},{2,1},{3,2},{4,3},{5,4},{6,5},{7,6},{8,7},{9,8},{10,9... | collective-permute-start | bytes 4718600 | tf_op jit(solution)/shard_map/ppermute | solution.py:20
  42.8 97.6 %collective-permute-done.kp_ref.vp_ref = bf16[2,384,1024]{2,1,0:T(8,128)(2,1)} collective-permute-done((bf16[2,384,1024]{2,1,0:T(8,128)(2,1)}, bf16[2,384,1024]{2,1,0:T(8,128)(2,1)}, u32[]{:S(2)}, u32[]{:S(2)}) %collective-permute-start) | collective-permute-done | bytes 1572896 | tf_op jit(solution)/shard_map/ppermute | solution.py:20
  140.4 24.3 %shard_map.85 = (bf16[384,1024]{1,0:T(8,128)(2,1)}, bf16[2,384,1024]{2,1,0:T(8,128)(2,1)}, f32[2,384,1024]{2,1,0:T(8,128)}, bf16[2,384,1024]{2,1,0:T(8,128)(2,1)}) custom-call(bf16[384,2048]{1,0:T(8,128)(2,1)} %bitcast.35, bf16[384,2048]{1,0:T(8,128)(2,1)} %bitcast.38, bf16[2,384,1024]{2,1,0:T(8,128)(2,1)} %collective-permute-done.kp_ref.vp_ref, ...), custom_call_target="tpu_custom_call" | custom-call | tf_op jit(solution)/shard_map/pallas_call | solution.py:97
  166.4 1.3 gather_fusion
  167.8 1.9 gather_fusion.1
  170.9 28.8 %collective-permute-done.2 = bf16[2,384,1024]{2,1,0:T(8,128)(2,1)} collective-permute-done((bf16[2,384,1024]{2,1,0:T(8,128)(2,1)}, bf16[2,384,1024]{2,1,0:T(8,128)(2,1)}, u32[]{:S(2)}, u32[]{:S(2)}) %collective-permute-start.2) | collective-permute-done | bytes 1572896 | tf_op jit(solution)/shard_map/ppermute | solution.py:20
  199.7 6.0 %collective-permute-done.3 = bf16[2,384,1024]{2,1,0:T(8,128)(2,1)} collective-permute-done((bf16[2,384,1024]{2,1,0:T(8,128)(2,1)}, bf16[2,384,1024]{2,1,0:T(8,128)(2,1)}, u32[]{:S(2)}, u32[]{:S(2)}) %collective-permute-start.3) | collective-permute-done | bytes 1572896 | tf_op jit(solution)/shard_map/ppermute | solution.py:20
  205.7 2.7 copy.49.q_ref.k_ref.v_ref.do_ref
  208.3 10.3 %shard_map.86 = (bf16[1,384,1024]{2,1,0:T(8,128)(2,1)}, bf16[1,384,1024]{2,1,0:T(8,128)(2,1)}, bf16[1,384,1024]{2,1,0:T(8,128)(2,1)}) custom-call(bf16[4,384,1024]{2,1,0:T(8,128)(2,1)} %copy.49.q_ref.k_ref.v_ref.do_ref, bf16[4,384,1024]{2,1,0:T(8,128)(2,1)} %copy.49.q_ref.k_ref.v_ref.do_ref, bf16[4,384,1024]{2,1,0:T(8,128)(2,1)} %copy.49.q_ref.k_ref.v_ref.do_ref, ...), custom_call_target="tpu_custom_call" | custom-call | tf_op jit(solution)/shard_map/pallas_call | solution.py:132
  218.6 3.3 pad_maximum_fusion.2
  222.0 3.6 %reshape.183 = bf16[3,64,6,1,1024]{4,2,1,0,3:T(8,128)(2,1)S(1)} reshape(bf16[3,384,1024]{2,1,0:T(8,128)(2,1)} %pad_maximum_fusion.2) | data formatting | bytes 4718592 | tf_op jit(solution)/shard_map/reshape | solution.py:196
  225.6 2.0 copy.53
  227.5 5.6 %all-to-all-start.1 = ((bf16[3,64,6,1,1024]{4,2,0,3,1:T(8,128)(2,1)}), bf16[3,64,6,1,1024]{4,2,0,3,1:T(8,128)(2,1)S(1)}, u32[]{:S(2)}, u32[]{:S(2)}) async-start(bf16[3,64,6,1,1024]{4,2,0,3,1:T(8,128)(2,1)} %copy.53), calls=%async_computation.1 | async-start | bytes 6291456 | tf_op jit(solution)/shard_map/all_to_all | solution.py:195
  233.2 3.7 %add_convert_fusion = bf16[2,384,1024]{2,1,0:T(8,128)(2,1)S(1)} fusion(bf16[2,384,1024]{2,1,0:T(8,128)(2,1)} %collective-permute-done.2, f32[2,384,1024]{2,1,0:T(8,128)} %get-tuple-element.14, bf16[2,384,1024]{2,1,0:T(8,128)(2,1)} %collective-permute-done.3), kind=kLoop, calls=%fused_computation.3 | loop fusion | flops 3932160 | bytes 7864320 | tf_op jit(solution)/shard_map/convert_element_type | solution.py:190
  237.0 1.6 pad_maximum_fusion.1
  238.6 2.3 collective-permute-start.4
  240.9 62.5 %all-to-all-done.1 = bf16[3,64,6,1,1024]{4,2,0,3,1:T(8,128)(2,1)S(1)} async-done(((bf16[3,64,6,1,1024]{4,2,0,3,1:T(8,128)(2,1)}), bf16[3,64,6,1,1024]{4,2,0,3,1:T(8,128)(2,1)S(1)}, u32[]{:S(2)}, u32[]{:S(2)}) %all-to-all-start.1) | async-done | bytes 2359328 | tf_op jit(solution)/shard_map/all_to_all | solution.py:195
  303.4 1.3 copy.54
  304.6 3.7 %collective-permute-start.5 = (bf16[3,384,1024]{2,1,0:T(8,128)(2,1)S(1)}, bf16[3,384,1024]{2,1,0:T(8,128)(2,1)S(1)}, u32[]{:S(2)}, u32[]{:S(2)}) collective-permute-start(bf16[3,384,1024]{2,1,0:T(8,128)(2,1)S(1)} %bitcast.43), channel_id=1, source_target_pairs={{0,192},{64,0},{128,64},{192,128},{1,193},{65,1},{129,65},{193,129... | collective-permute-start | bytes 7077896 | tf_op jit(solution)/shard_map/ppermute | solution.py:20
  308.4 1.9 constant_dynamic-update-slice_fusion.1
  310.3 24.9 %collective-permute-done.5 = bf16[3,384,1024]{2,1,0:T(8,128)(2,1)S(1)} collective-permute-done((bf16[3,384,1024]{2,1,0:T(8,128)(2,1)S(1)}, bf16[3,384,1024]{2,1,0:T(8,128)(2,1)S(1)}, u32[]{:S(2)}, u32[]{:S(2)}) %collective-permute-start.5) | collective-permute-done | bytes 2359328 | tf_op jit(solution)/shard_map/ppermute | solution.py:20
  335.4 2.4 fusion.7
  (34 shorter events, 4.2 us)
Async XLA Ops:
  0.6 2.6 copy-start
  0.6 2.6 copy-start.1
  4.8 2.4 copy-start.2
  16.9 188.8 %all-to-all-start = ((bf16[4,6,64,1024]{3,0,1,2:T(4,128)(2,1)}), bf16[4,6,64,1024]{3,0,1,2:T(4,128)(2,1)S(1)}, u32[]{:S(2)}, u32[]{:S(2)}) async-start(bf16[4,6,64,1024]{3,0,1,2:T(4,128)(2,1)} %pad_maximum_fusion), calls=%async_computation | async-start | bytes 6291456 | tf_op jit(solution)/shard_map/all_to_all | solution.py:158
  32.0 9.9 %copy-start.4 = (s32[3,5]{1,0:T(4,128)S(1)}, s32[3,5]{1,0:T(4,128)}, u32[]{:S(2)}) copy-start(s32[3,5]{1,0:T(4,128)} %param.10) | copy-start | bytes 184
  34.7 105.7 %collective-permute-start = (bf16[2,384,1024]{2,1,0:T(8,128)(2,1)}, bf16[2,384,1024]{2,1,0:T(8,128)(2,1)}, u32[]{:S(2)}, u32[]{:S(2)}) collective-permute-start(bf16[2,384,1024]{2,1,0:T(8,128)(2,1)} %pad_maximum_fusion.3), channel_id=1, source_target_pairs={{0,1},{1,2},{2,3},{3,4},{4,5},{5,6},{6,7},{7,8},{8,9},{9,10},{10,1... | collective-permute-start | bytes 4718600 | tf_op jit(solution)/shard_map/ppermute | solution.py:20
  35.7 104.7 %collective-permute-start.1 = (bf16[2,384,1024]{2,1,0:T(8,128)(2,1)}, bf16[2,384,1024]{2,1,0:T(8,128)(2,1)}, u32[]{:S(2)}, u32[]{:S(2)}) collective-permute-start(bf16[2,384,1024]{2,1,0:T(8,128)(2,1)} %pad_maximum_fusion.3), channel_id=1, source_target_pairs={{0,63},{1,0},{2,1},{3,2},{4,3},{5,4},{6,5},{7,6},{8,7},{9,8},{10,9... | collective-permute-start | bytes 4718600 | tf_op jit(solution)/shard_map/ppermute | solution.py:20
  140.4 25.9 %copy-start.5 = (s32[3,2]{0,1:T(2,128)S(1)}, s32[3,2]{0,1:T(2,128)}, u32[]{:S(2)}) copy-start(s32[3,2]{0,1:T(2,128)} %param.11) | copy-start | bytes 76
  164.7 35.0 %collective-permute-start.2 = (bf16[2,384,1024]{2,1,0:T(8,128)(2,1)}, bf16[2,384,1024]{2,1,0:T(8,128)(2,1)}, u32[]{:S(2)}, u32[]{:S(2)}) collective-permute-start(bf16[2,384,1024]{2,1,0:T(8,128)(2,1)} %get-tuple-element.15), channel_id=1, source_target_pairs={{0,63},{1,0},{2,1},{3,2},{4,3},{5,4},{6,5},{7,6},{8,7},{9,8},{10,9... | collective-permute-start | bytes 4718600 | tf_op jit(solution)/shard_map/ppermute | solution.py:20
  165.3 40.3 %collective-permute-start.3 = (bf16[2,384,1024]{2,1,0:T(8,128)(2,1)}, bf16[2,384,1024]{2,1,0:T(8,128)(2,1)}, u32[]{:S(2)}, u32[]{:S(2)}) collective-permute-start(bf16[2,384,1024]{2,1,0:T(8,128)(2,1)} %get-tuple-element.16), channel_id=1, source_target_pairs={{0,1},{1,2},{2,3},{3,4},{4,5},{5,6},{6,7},{7,8},{8,9},{9,10},{10,1... | collective-permute-start | bytes 4718600 | tf_op jit(solution)/shard_map/ppermute | solution.py:20
  227.5 75.8 %all-to-all-start.1 = ((bf16[3,64,6,1,1024]{4,2,0,3,1:T(8,128)(2,1)}), bf16[3,64,6,1,1024]{4,2,0,3,1:T(8,128)(2,1)S(1)}, u32[]{:S(2)}, u32[]{:S(2)}) async-start(bf16[3,64,6,1,1024]{4,2,0,3,1:T(8,128)(2,1)} %copy.53), calls=%async_computation.1 | async-start | bytes 6291456 | tf_op jit(solution)/shard_map/all_to_all | solution.py:195
  233.2 3.8 %copy-start.3 = (bf16[384,1024]{1,0:T(8,128)(2,1)S(1)}, bf16[384,1024]{1,0:T(8,128)(2,1)}, u32[]{:S(2)}) copy-start(bf16[384,1024]{1,0:T(8,128)(2,1)} %get-tuple-element.13) | copy-start | bytes 2359300
  238.6 69.8 %collective-permute-start.4 = (bf16[3,384,1024]{2,1,0:T(8,128)(2,1)}, bf16[3,384,1024]{2,1,0:T(8,128)(2,1)}, u32[]{:S(2)}, u32[]{:S(2)}) collective-permute-start(bf16[3,384,1024]{2,1,0:T(8,128)(2,1)} %pad_maximum_fusion.1), channel_id=1, source_target_pairs={{0,192},{64,0},{128,64},{192,128},{1,193},{65,1},{129,65},{193,129... | collective-permute-start | bytes 7077896 | tf_op jit(solution)/shard_map/ppermute | solution.py:20
  304.6 30.6 %collective-permute-start.5 = (bf16[3,384,1024]{2,1,0:T(8,128)(2,1)S(1)}, bf16[3,384,1024]{2,1,0:T(8,128)(2,1)S(1)}, u32[]{:S(2)}, u32[]{:S(2)}) collective-permute-start(bf16[3,384,1024]{2,1,0:T(8,128)(2,1)S(1)} %bitcast.43), channel_id=1, source_target_pairs={{0,192},{64,0},{128,64},{192,128},{1,193},{65,1},{129,65},{193,129... | collective-permute-start | bytes 7077896 | tf_op jit(solution)/shard_map/ppermute | solution.py:20

commit v6 on v4

--- a/solution.py
+++ b/solution.py
@@ -76,15 +76,15 @@
     dnext_ref[1] = dvwin[2 * tokens:3 * tokens, :].astype(dnext_ref.dtype)
 
 
-def col_kernel(q_ref, k_ref, v_ref, do_ref, keep_ref, dq_ref, dk_ref, dv_ref):
+def col_kernel(q_ref, k_ref, v_ref, do_ref, keep_ref, out_ref):
     scale = HEAD_DIM ** (-0.5)
     keep = keep_ref[...] > 0.5
     grad_q, grad_k, grad_v = chunk_grads(
         q_ref[0], do_ref[0], k_ref[0], v_ref[0], keep, scale
     )
-    dq_ref[0] = grad_q.astype(dq_ref.dtype)
-    dk_ref[0] = grad_k.astype(dk_ref.dtype)
-    dv_ref[0] = grad_v.astype(dv_ref.dtype)
+    out_ref[0] = grad_q.astype(out_ref.dtype)
+    out_ref[1] = grad_k.astype(out_ref.dtype)
+    out_ref[2] = grad_v.astype(out_ref.dtype)
 
 
 def row_side(query_now, key_now, value_now, grad_now, near_before, near_after, keep):
@@ -127,8 +127,6 @@
 def col_side(received, keep):
     tokens = received.shape[1]
     part_block = lambda part: pl.BlockSpec((1, tokens, HEAD_DIM), lambda h: (part, 0, h))
-    out_block = pl.BlockSpec((1, tokens, HEAD_DIM), lambda h: (0, 0, h))
-    out_struct = jax.ShapeDtypeStruct((1, tokens, HEADS_COL * HEAD_DIM), jnp.bfloat16)
     return pl.pallas_call(
         col_kernel,
         grid=(HEADS_COL,),
@@ -136,8 +134,8 @@
             part_block(0), part_block(1), part_block(2), part_block(3),
             pl.BlockSpec(keep.shape, lambda h: (0, 0)),
         ],
-        out_specs=[out_block, out_block, out_block],
-        out_shape=[out_struct, out_struct, out_struct],
+        out_specs=pl.BlockSpec((3, tokens, HEAD_DIM), lambda h: (0, 0, h)),
+        out_shape=jax.ShapeDtypeStruct((3, tokens, HEADS_COL * HEAD_DIM), jnp.bfloat16),
     )(received, received, received, received, keep)
 
 
@@ -185,11 +183,12 @@
     arrival = jnp.arange(tokens, dtype=jnp.int32)
     col_block = ((arrival % GROUP_COLS) * grid_rows + arrival // GROUP_COLS) // BLOCK
     local_strided = strided_lists - position * block_count
-    col_allowed = jnp.any(
-        local_strided[:, None, :] == jnp.arange(block_count, dtype=jnp.int32)[None, :, None], axis=2
-    )
-    col_keep = col_allowed[col_block][:, col_block].astype(jnp.float32)
-    col_grads = jnp.concatenate(col_side(received, col_keep), axis=0)
+    listed = sum(
+        (col_block == number)[:, None] * local_strided[number][None, :]
+        for number in range(block_count)
+    )
+    col_keep = jnp.any(listed[:, :, None] == col_block[None, None, :], axis=1).astype(jnp.float32)
+    col_grads = col_side(received, col_keep)
 
     col_grads, from_after, from_before = lax.optimization_barrier((col_grads, from_after, from_before))
     d_total = (d_own + from_before.astype(jnp.float32) + from_after.astype(jnp.float32)).astype(

time: 301 us -> 301 us (level)
  waiting for transfers between devices: 189 us -> 195 us
  local copies, waits for them, and re-layouts: 20.7 us -> 17.4 us
  other arithmetic: 14 us -> 10.8 us
    ppermute x6, waiting for transfers between devices: 79.1 us -> 85.3 us  [shifted(): return lax.ppermute(value, axis, pairs)]
    gather x4 -> x0, local copies, waits for them, and re-layouts: 3.56 us -> none  [body(): col_keep = col_allowed[col_block][:, col_block].astype(jnp.float32)]
    concatenate x1 -> x0, other arithmetic: 3.34 us -> none  [body(): col_grads = jnp.concatenate(col_side(received, col_keep), axis=0)]
  transfers between devices with their start and end apart: 8 -> 8, of which waited for: 6 -> 6; matrix products, arithmetic and copies ran while one was open for 6% -> 4% of each run, Pallas kernels for 12% -> 12%
where the time goes in v6:
time: 301 us; the launch traced here: 296 us
  waiting for transfers between devices  195 us (65%)
  starting transfers between devices  37.6 us (12%)
  Pallas kernels  35 us (12%)
  local copies, waits for them, and re-layouts  17.4 us (6%)
  other arithmetic  10.8 us (4%)
    ppermute x6, waiting for transfers between devices, shifted(): return lax.ppermute(value, axis, pairs)  85.3 us
    all_to_all x1, waiting for transfers between devices, body(): lax.all_to_all(col_grads.reshape(3, devices, share, 1, COLS), 'seq', spli...  63 us
    all_to_all x1, waiting for transfers between devices, body(): lax.all_to_all(sent.reshape(4, share, devices, COLS), 'seq', split_axis=2...  46.5 us
    pallas_call x1, Pallas kernels, row_side(): pl.pallas_call(row_kernel, grid=(HEADS_ROW,), in_specs=[plain, plain, sta...  24.3 us
    ppermute x6, starting transfers between devices, shifted(): return lax.ppermute(value, axis, pairs)  19.5 us
    all_to_all x1, starting transfers between devices, body(): lax.all_to_all(sent.reshape(4, share, devices, COLS), 'seq', split_axis=2...  12.7 us
    pallas_call x1, Pallas kernels, col_side(): pl.pallas_call(col_kernel, grid=(HEADS_COL,), in_specs=[part_block(0), pa...  10.7 us
  transfers between devices with their start and end apart: 8, of which 6 were waited for; matrix products, arithmetic and copies ran while one was open for 4% of the time, Pallas kernels for 12%

profile of v6, /device:TPU:1, one launch (start us, length us, event | category | flops | bytes accessed | tf_op | source)
XLA Modules:
  0.0 296.3 jit_solution(723980020205702033)
XLA Ops:
  0.7 1.6 slice_bitcast_fusion.2
  2.3 0.2 copy-done
  2.5 0.5 copy-done.1
  3.0 0.4 slice_bitcast_fusion
  3.4 0.4 pad_maximum_fusion
  3.9 3.3 %collective-permute-start = (bf16[4,384,1024]{2,1,0:T(8,128)(2,1)S(1)}, bf16[4,384,1024]{2,1,0:T(8,128)(2,1)S(1)}, u32[]{:S(2)}, u32[]{:S(2)}) collective-permute-start(bf16[4,384,1024]{2,1,0:T(8,128)(2,1)S(1)} %pad_maximum_fusion), channel_id=1, source_target_pairs={{0,192},{64,0},{128,64},{192,128},{1,193},{65,1},{129,65},{193,129... | collective-permute-start | bytes 9437192 | tf_op jit(solution)/shard_map/ppermute | solution.py:20
  7.1 0.1 pad_maximum_fusion.3
  7.4 8.8 %collective-permute-start.2 = (bf16[2,384,1024]{2,1,0:T(8,128)(2,1)S(1)}, bf16[2,384,1024]{2,1,0:T(8,128)(2,1)}, u32[]{:S(2)}, u32[]{:S(2)}) collective-permute-start(bf16[2,384,1024]{2,1,0:T(8,128)(2,1)S(1)} %pad_maximum_fusion.3), channel_id=1, source_target_pairs={{0,63},{1,0},{2,1},{3,2},{4,3},{5,4},{6,5},{7,6},{8,7},{9,8},{10,9... | collective-permute-start | bytes 4718600 | tf_op jit(solution)/shard_map/ppermute | solution.py:20
  16.1 34.1 %collective-permute-done.1.kp_ref.vp_ref = bf16[2,384,1024]{2,1,0:T(8,128)(2,1)} collective-permute-done((bf16[2,384,1024]{2,1,0:T(8,128)(2,1)S(1)}, bf16[2,384,1024]{2,1,0:T(8,128)(2,1)}, u32[]{:S(2)}, u32[]{:S(2)}) %collective-permute-start.1) | collective-permute-done | bytes 1572896 | tf_op jit(solution)/shard_map/ppermute | solution.py:20
  50.2 25.1 %collective-permute-done = bf16[4,384,1024]{2,1,0:T(8,128)(2,1)S(1)} collective-permute-done((bf16[4,384,1024]{2,1,0:T(8,128)(2,1)S(1)}, bf16[4,384,1024]{2,1,0:T(8,128)(2,1)S(1)}, u32[]{:S(2)}, u32[]{:S(2)}) %collective-permute-start) | collective-permute-done | bytes 3145760 | tf_op jit(solution)/shard_map/ppermute | solution.py:20
  75.3 4.1 %copy.24 = bf16[4,6,64,1024]{3,0,1,2:T(4,128)(2,1)} copy(bf16[4,6,64,1024]{3,2,1,0:T(8,128)(2,1)S(1)} %bitcast.43) | data formatting | bytes 6291456 | tf_op jit(solution)/shard_map/reshape | solution.py:163
  79.4 12.7 %all-to-all-start = ((bf16[4,6,64,1024]{3,0,1,2:T(4,128)(2,1)}), bf16[4,6,64,1024]{3,0,1,2:T(4,128)(2,1)S(1)}, u32[]{:S(2)}, u32[]{:S(2)}) async-start(bf16[4,6,64,1024]{3,0,1,2:T(4,128)(2,1)} %copy.24), calls=%async_computation | async-start | bytes 6291456 | tf_op jit(solution)/shard_map/all_to_all | solution.py:162
  92.5 0.6 copy.34
  93.1 24.3 %shard_map.85 = (bf16[384,1024]{1,0:T(8,128)(2,1)}, bf16[2,384,1024]{2,1,0:T(8,128)(2,1)}, f32[2,384,1024]{2,1,0:T(8,128)}, bf16[2,384,1024]{2,1,0:T(8,128)(2,1)}) custom-call(bf16[384,2048]{1,0:T(8,128)(2,1)} %bitcast.42, bf16[384,2048]{1,0:T(8,128)(2,1)} %bitcast.40, bf16[2,384,1024]{2,1,0:T(8,128)(2,1)} %collective-permute-done.1.kp_ref.vp_ref, ...), custom_call_target="tpu_custom_call" | custom-call | tf_op jit(solution)/shard_map/pallas_call | solution.py:97
  117.4 46.5 %all-to-all-done = bf16[4,6,64,1024]{3,0,1,2:T(4,128)(2,1)S(1)} async-done(((bf16[4,6,64,1024]{3,0,1,2:T(4,128)(2,1)}), bf16[4,6,64,1024]{3,0,1,2:T(4,128)(2,1)S(1)}, u32[]{:S(2)}, u32[]{:S(2)}) %all-to-all-start) | async-done | bytes 3145760 | tf_op jit(solution)/shard_map/all_to_all | solution.py:162
  163.9 5.3 %collective-permute-start.3 = (bf16[2,384,1024]{2,1,0:T(8,128)(2,1)}, bf16[2,384,1024]{2,1,0:T(8,128)(2,1)}, u32[]{:S(2)}, u32[]{:S(2)}) collective-permute-start(bf16[2,384,1024]{2,1,0:T(8,128)(2,1)} %get-tuple-element.28), channel_id=1, source_target_pairs={{0,63},{1,0},{2,1},{3,2},{4,3},{5,4},{6,5},{7,6},{8,7},{9,8},{10,9... | collective-permute-start | bytes 4718600 | tf_op jit(solution)/shard_map/ppermute | solution.py:20
  169.2 0.2 slice_reduce_fusion.2
  169.5 0.2 compare_reduce_fusion
  169.7 0.9 convert_element_type.43.keep_ref
  170.5 2.7 copy.26.q_ref.k_ref.v_ref.do_ref
  173.2 10.7 %shard_map.86 = bf16[3,384,1024]{2,1,0:T(8,128)(2,1)} custom-call(bf16[4,384,1024]{2,1,0:T(8,128)(2,1)} %copy.26.q_ref.k_ref.v_ref.do_ref, bf16[4,384,1024]{2,1,0:T(8,128)(2,1)} %copy.26.q_ref.k_ref.v_ref.do_ref, bf16[4,384,1024]{2,1,0:T(8,128)(2,1)} %copy.26.q_ref.k_ref.v_ref.do_ref, bf16[4,384,1024]{2,1,0:T(8,128)(2,1)} %copy.26.q_ref.k_ref.v_ref.do_ref, ...), custom_call_target="tpu_custom_call" | custom-call | tf_op jit(solution)/shard_map/pallas_call | solution.py:130
  183.9 18.6 %collective-permute-done.3 = bf16[2,384,1024]{2,1,0:T(8,128)(2,1)} collective-permute-done((bf16[2,384,1024]{2,1,0:T(8,128)(2,1)}, bf16[2,384,1024]{2,1,0:T(8,128)(2,1)}, u32[]{:S(2)}, u32[]{:S(2)}) %collective-permute-start.3) | collective-permute-done | bytes 1572896 | tf_op jit(solution)/shard_map/ppermute | solution.py:20
  202.5 7.6 %collective-permute-done.4 = bf16[2,384,1024]{2,1,0:T(8,128)(2,1)} collective-permute-done((bf16[2,384,1024]{2,1,0:T(8,128)(2,1)}, bf16[2,384,1024]{2,1,0:T(8,128)(2,1)}, u32[]{:S(2)}, u32[]{:S(2)}) %collective-permute-start.4) | collective-permute-done | bytes 1572896 | tf_op jit(solution)/shard_map/ppermute | solution.py:20
  210.1 3.6 %reshape.241 = bf16[3,64,6,1,1024]{4,2,1,0,3:T(8,128)(2,1)S(1)} reshape(bf16[3,384,1024]{2,1,0:T(8,128)(2,1)} %shard_map.86) | data formatting | bytes 4718592 | tf_op jit(solution)/shard_map/reshape | solution.py:200
  213.7 2.0 copy.30
  215.7 5.4 %all-to-all-start.1 = ((bf16[3,64,6,1,1024]{4,2,0,3,1:T(8,128)(2,1)}), bf16[3,64,6,1,1024]{4,2,0,3,1:T(8,128)(2,1)S(1)}, u32[]{:S(2)}, u32[]{:S(2)}) async-start(bf16[3,64,6,1,1024]{4,2,0,3,1:T(8,128)(2,1)} %copy.30), calls=%async_computation.1 | async-start | bytes 6291456 | tf_op jit(solution)/shard_map/all_to_all | solution.py:199
  221.1 3.7 %add_convert_fusion = bf16[2,384,1024]{2,1,0:T(8,128)(2,1)S(1)} fusion(bf16[2,384,1024]{2,1,0:T(8,128)(2,1)} %collective-permute-done.3, f32[2,384,1024]{2,1,0:T(8,128)} %get-tuple-element.26, bf16[2,384,1024]{2,1,0:T(8,128)(2,1)} %collective-permute-done.4), kind=kLoop, calls=%fused_computation.5 | loop fusion | flops 3932160 | bytes 7864320 | tf_op jit(solution)/shard_map/convert_element_type | solution.py:194
  224.9 1.6 pad_maximum_fusion.1
  226.5 2.0 collective-permute-start.5
  228.5 63.0 %all-to-all-done.1 = bf16[3,64,6,1,1024]{4,2,0,3,1:T(8,128)(2,1)S(1)} async-done(((bf16[3,64,6,1,1024]{4,2,0,3,1:T(8,128)(2,1)}), bf16[3,64,6,1,1024]{4,2,0,3,1:T(8,128)(2,1)S(1)}, u32[]{:S(2)}, u32[]{:S(2)}) %all-to-all-start.1) | async-done | bytes 2359328 | tf_op jit(solution)/shard_map/all_to_all | solution.py:199
  291.5 1.3 copy.31
  292.9 3.5 %pad_maximum_fusion.2 = (bf16[1,384,2048]{2,1,0:T(8,128)(2,1)}, bf16[1,384,2048]{2,1,0:T(8,128)(2,1)}, bf16[1,384,2048]{2,1,0:T(8,128)(2,1)}) fusion(bf16[3,384,1024]{2,1,0:T(8,128)(2,1)S(1)} %bitcast.34, bf16[3,384,1024]{2,1,0:T(8,128)(2,1)} %collective-permute-done.5), kind=kLoop, calls=%fused_computation.9 | loop fusion | flops 9437184 | bytes 9437184 | tf_op jit(solution)/shard_map/concatenate | solution.py:203
  (24 shorter events, 0.6 us)
Async XLA Ops:
  0.6 1.9 copy-start
  0.6 2.3 copy-start.1
  3.9 71.4 %collective-permute-start = (bf16[4,384,1024]{2,1,0:T(8,128)(2,1)S(1)}, bf16[4,384,1024]{2,1,0:T(8,128)(2,1)S(1)}, u32[]{:S(2)}, u32[]{:S(2)}) collective-permute-start(bf16[4,384,1024]{2,1,0:T(8,128)(2,1)S(1)} %pad_maximum_fusion), channel_id=1, source_target_pairs={{0,192},{64,0},{128,64},{192,128},{1,193},{65,1},{129,65},{193,129... | collective-permute-start | bytes 9437192 | tf_op jit(solution)/shard_map/ppermute | solution.py:20
  7.3 42.9 %collective-permute-start.1 = (bf16[2,384,1024]{2,1,0:T(8,128)(2,1)S(1)}, bf16[2,384,1024]{2,1,0:T(8,128)(2,1)}, u32[]{:S(2)}, u32[]{:S(2)}) collective-permute-start(bf16[2,384,1024]{2,1,0:T(8,128)(2,1)S(1)} %pad_maximum_fusion.3), channel_id=1, source_target_pairs={{0,1},{1,2},{2,3},{3,4},{4,5},{5,6},{6,7},{7,8},{8,9},{9,10},{10,1... | collective-permute-start | bytes 4718600 | tf_op jit(solution)/shard_map/ppermute | solution.py:20
  7.4 42.8 %collective-permute-start.2 = (bf16[2,384,1024]{2,1,0:T(8,128)(2,1)S(1)}, bf16[2,384,1024]{2,1,0:T(8,128)(2,1)}, u32[]{:S(2)}, u32[]{:S(2)}) collective-permute-start(bf16[2,384,1024]{2,1,0:T(8,128)(2,1)S(1)} %pad_maximum_fusion.3), channel_id=1, source_target_pairs={{0,63},{1,0},{2,1},{3,2},{4,3},{5,4},{6,5},{7,6},{8,7},{9,8},{10,9... | collective-permute-start | bytes 4718600 | tf_op jit(solution)/shard_map/ppermute | solution.py:20
  79.4 12.7 %copy-start.3 = (s32[3,5]{1,0:T(4,128)S(1)}, s32[3,5]{1,0:T(4,128)}, u32[]{:S(2)}) copy-start(s32[3,5]{1,0:T(4,128)} %param.10) | copy-start | bytes 184
  79.4 84.5 %all-to-all-start = ((bf16[4,6,64,1024]{3,0,1,2:T(4,128)(2,1)}), bf16[4,6,64,1024]{3,0,1,2:T(4,128)(2,1)S(1)}, u32[]{:S(2)}, u32[]{:S(2)}) async-start(bf16[4,6,64,1024]{3,0,1,2:T(4,128)(2,1)} %copy.24), calls=%async_computation | async-start | bytes 6291456 | tf_op jit(solution)/shard_map/all_to_all | solution.py:162
  93.1 76.1 %copy-start.4 = (s32[3,2]{0,1:T(2,128)S(1)}, s32[3,2]{0,1:T(2,128)}, u32[]{:S(2)}) copy-start(s32[3,2]{0,1:T(2,128)} %param.11) | copy-start | bytes 76
  163.9 38.6 %collective-permute-start.3 = (bf16[2,384,1024]{2,1,0:T(8,128)(2,1)}, bf16[2,384,1024]{2,1,0:T(8,128)(2,1)}, u32[]{:S(2)}, u32[]{:S(2)}) collective-permute-start(bf16[2,384,1024]{2,1,0:T(8,128)(2,1)} %get-tuple-element.28), channel_id=1, source_target_pairs={{0,63},{1,0},{2,1},{3,2},{4,3},{5,4},{6,5},{7,6},{8,7},{9,8},{10,9... | collective-permute-start | bytes 4718600 | tf_op jit(solution)/shard_map/ppermute | solution.py:20
  169.2 41.0 %collective-permute-start.4 = (bf16[2,384,1024]{2,1,0:T(8,128)(2,1)}, bf16[2,384,1024]{2,1,0:T(8,128)(2,1)}, u32[]{:S(2)}, u32[]{:S(2)}) collective-permute-start(bf16[2,384,1024]{2,1,0:T(8,128)(2,1)} %get-tuple-element.29), channel_id=1, source_target_pairs={{0,1},{1,2},{2,3},{3,4},{4,5},{5,6},{6,7},{7,8},{8,9},{9,10},{10,1... | collective-permute-start | bytes 4718600 | tf_op jit(solution)/shard_map/ppermute | solution.py:20
  215.7 75.8 %all-to-all-start.1 = ((bf16[3,64,6,1,1024]{4,2,0,3,1:T(8,128)(2,1)}), bf16[3,64,6,1,1024]{4,2,0,3,1:T(8,128)(2,1)S(1)}, u32[]{:S(2)}, u32[]{:S(2)}) async-start(bf16[3,64,6,1,1024]{4,2,0,3,1:T(8,128)(2,1)} %copy.30), calls=%async_computation.1 | async-start | bytes 6291456 | tf_op jit(solution)/shard_map/all_to_all | solution.py:199
  221.1 3.8 %copy-start.2 = (bf16[384,1024]{1,0:T(8,128)(2,1)S(1)}, bf16[384,1024]{1,0:T(8,128)(2,1)}, u32[]{:S(2)}) copy-start(bf16[384,1024]{1,0:T(8,128)(2,1)} %get-tuple-element.25) | copy-start | bytes 2359300
  226.5 66.4 %collective-permute-start.5 = (bf16[3,384,1024]{2,1,0:T(8,128)(2,1)}, bf16[3,384,1024]{2,1,0:T(8,128)(2,1)}, u32[]{:S(2)}, u32[]{:S(2)}) collective-permute-start(bf16[3,384,1024]{2,1,0:T(8,128)(2,1)} %pad_maximum_fusion.1), channel_id=1, source_target_pairs={{0,192},{64,0},{128,64},{192,128},{1,193},{65,1},{129,65},{193,129... | collective-permute-start | bytes 7077896 | tf_op jit(solution)/shard_map/ppermute | solution.py:20

commit v7 on v6

--- a/solution.py
+++ b/solution.py
@@ -156,7 +156,6 @@
     near_before = shifted(near, "seq", 1)
     near_after = shifted(near, "seq", -1)
     sent = jnp.stack([item[:, row_width:] for item in (query_now, key_now, value_now, grad_now)])
-    sent = shifted(sent, "pipe", -1)
 
     sent, near_before, near_after = lax.optimization_barrier((sent, near_before, near_after))
     received = lax.all_to_all(
@@ -196,9 +195,10 @@
     )
     row_grads = jnp.concatenate([dq_row[None], d_total], axis=0)
     row_handed = shifted(row_grads, "pipe", -1)
-    col_handed = lax.all_to_all(
+    returned = lax.all_to_all(
         col_grads.reshape(3, devices, share, 1, COLS), "seq", split_axis=1, concat_axis=3, tiled=True
     ).reshape(3, tokens, COLS)
+    col_handed = shifted(returned, "pipe", -1)
 
     handed = jnp.concatenate([row_handed, col_handed], axis=2)
     return (handed[0][None], handed[1][None], handed[2][None])

time: 301 us -> 295 us (0.980)
  waiting for transfers between devices: 195 us -> 187 us
  local copies, waits for them, and re-layouts: 17.4 us -> 21.4 us
  starting transfers between devices: 37.6 us -> 41.2 us
  other arithmetic: 10.8 us -> 7.29 us
    ppermute x6, starting transfers between devices: 19.5 us -> 26.4 us  [shifted(): return lax.ppermute(value, axis, pairs)]
    all_to_all x1, waiting for transfers between devices: 63 us -> 59.3 us  [body(): lax.all_to_all(col_grads.reshape(3, devices, share, 1, COLS), 'seq', spli...]
    concatenate x1 -> x0, other arithmetic: 3.48 us -> none  [body(): handed = jnp.concatenate([row_handed, col_handed], axis=2)]
    all_to_all x1, starting transfers between devices: 12.7 us -> 9.41 us  [body(): lax.all_to_all(sent.reshape(4, share, devices, COLS), 'seq', split_axis=2...]
  transfers between devices with their start and end apart: 8 -> 8, of which waited for: 6 -> 6; matrix products, arithmetic and copies ran while one was open for 4% -> 5% of each run, Pallas kernels for 12% -> 12%
where the time goes in v7:
time: 295 us; the launch traced here: 293 us
  waiting for transfers between devices  187 us (63%)
  starting transfers between devices  41.2 us (14%)
  Pallas kernels  35 us (12%)
  local copies, waits for them, and re-layouts  21.4 us (7%)
  other arithmetic  7.29 us (2%)
    ppermute x6, waiting for transfers between devices, shifted(): return lax.ppermute(value, axis, pairs)  82.7 us
    all_to_all x1, waiting for transfers between devices, body(): lax.all_to_all(col_grads.reshape(3, devices, share, 1, COLS), 'seq', spli...  59.3 us
    all_to_all x1, waiting for transfers between devices, body(): lax.all_to_all(sent.reshape(4, share, devices, COLS), 'seq', split_axis=2...  45.3 us
    ppermute x6, starting transfers between devices, shifted(): return lax.ppermute(value, axis, pairs)  26.4 us
    pallas_call x1, Pallas kernels, row_side(): pl.pallas_call(row_kernel, grid=(HEADS_ROW,), in_specs=[plain, plain, sta...  24.3 us
    pallas_call x1, Pallas kernels, col_side(): pl.pallas_call(col_kernel, grid=(HEADS_COL,), in_specs=[part_block(0), pa...  10.7 us
    all_to_all x1, starting transfers between devices, body(): lax.all_to_all(sent.reshape(4, share, devices, COLS), 'seq', split_axis=2...  9.41 us
  transfers between devices with their start and end apart: 8, of which 6 were waited for; matrix products, arithmetic and copies ran while one was open for 5% of the time, Pallas kernels for 12%

profile of v7, /device:TPU:1, one launch (start us, length us, event | category | flops | bytes accessed | tf_op | source)
XLA Modules:
  0.0 292.9 jit_solution(6972397356234184545)
XLA Ops:
  0.6 2.2 slice_bitcast_fusion
  2.8 0.1 pad_maximum_fusion.2
  3.0 2.1 collective-permute-start
  5.1 9.3 %collective-permute-start.1 = (bf16[2,384,1024]{2,1,0:T(8,128)(2,1)S(1)}, bf16[2,384,1024]{2,1,0:T(8,128)(2,1)}, u32[]{:S(2)}, u32[]{:S(2)}) collective-permute-start(bf16[2,384,1024]{2,1,0:T(8,128)(2,1)S(1)} %pad_maximum_fusion.2), channel_id=1, source_target_pairs={{0,63},{1,0},{2,1},{3,2},{4,3},{5,4},{6,5},{7,6},{8,7},{9,8},{10,9... | collective-permute-start | bytes 4718600 | tf_op jit(solution)/shard_map/ppermute | solution.py:20
  14.5 0.4 pad_maximum_fusion
  14.9 33.5 %collective-permute-done.kp_ref.vp_ref = bf16[2,384,1024]{2,1,0:T(8,128)(2,1)} collective-permute-done((bf16[2,384,1024]{2,1,0:T(8,128)(2,1)S(1)}, bf16[2,384,1024]{2,1,0:T(8,128)(2,1)}, u32[]{:S(2)}, u32[]{:S(2)}) %collective-permute-start) | collective-permute-done | bytes 1572896 | tf_op jit(solution)/shard_map/ppermute | solution.py:20
  48.5 4.1 %copy.24 = bf16[4,6,64,1024]{3,0,1,2:T(4,128)(2,1)} copy(bf16[4,6,64,1024]{3,2,1,0:T(8,128)(2,1)S(1)} %bitcast.33) | data formatting | bytes 6291456 | tf_op jit(solution)/shard_map/reshape | solution.py:162
  52.6 9.4 %all-to-all-start = ((bf16[4,6,64,1024]{3,0,1,2:T(4,128)(2,1)}), bf16[4,6,64,1024]{3,0,1,2:T(4,128)(2,1)S(1)}, u32[]{:S(2)}, u32[]{:S(2)}) async-start(bf16[4,6,64,1024]{3,0,1,2:T(4,128)(2,1)} %copy.24), calls=%async_computation | async-start | bytes 6291456 | tf_op jit(solution)/shard_map/all_to_all | solution.py:161
  62.4 0.6 copy.34
  63.0 24.3 %shard_map.85 = (bf16[384,1024]{1,0:T(8,128)(2,1)}, bf16[2,384,1024]{2,1,0:T(8,128)(2,1)}, f32[2,384,1024]{2,1,0:T(8,128)}, bf16[2,384,1024]{2,1,0:T(8,128)(2,1)}) custom-call(bf16[384,2048]{1,0:T(8,128)(2,1)} %bitcast.39, bf16[384,2048]{1,0:T(8,128)(2,1)} %bitcast.41, bf16[2,384,1024]{2,1,0:T(8,128)(2,1)} %collective-permute-done.kp_ref.vp_ref, ...), custom_call_target="tpu_custom_call" | custom-call | tf_op jit(solution)/shard_map/pallas_call | solution.py:97
  87.3 45.3 %all-to-all-done = bf16[4,6,64,1024]{3,0,1,2:T(4,128)(2,1)S(1)} async-done(((bf16[4,6,64,1024]{3,0,1,2:T(4,128)(2,1)}), bf16[4,6,64,1024]{3,0,1,2:T(4,128)(2,1)S(1)}, u32[]{:S(2)}, u32[]{:S(2)}) %all-to-all-start) | async-done | bytes 3145760 | tf_op jit(solution)/shard_map/all_to_all | solution.py:161
  132.6 5.4 %collective-permute-start.2 = (bf16[2,384,1024]{2,1,0:T(8,128)(2,1)}, bf16[2,384,1024]{2,1,0:T(8,128)(2,1)}, u32[]{:S(2)}, u32[]{:S(2)}) collective-permute-start(bf16[2,384,1024]{2,1,0:T(8,128)(2,1)} %get-tuple-element.28), channel_id=1, source_target_pairs={{0,63},{1,0},{2,1},{3,2},{4,3},{5,4},{6,5},{7,6},{8,7},{9,8},{10,9... | collective-permute-start | bytes 4718600 | tf_op jit(solution)/shard_map/ppermute | solution.py:20
  138.0 0.2 slice_reduce_fusion.2
  138.3 0.2 compare_reduce_fusion
  138.4 0.9 convert_element_type.43.keep_ref
  139.3 2.7 copy.26.q_ref.k_ref.v_ref.do_ref
  142.0 10.7 %shard_map.86 = bf16[3,384,1024]{2,1,0:T(8,128)(2,1)} custom-call(bf16[4,384,1024]{2,1,0:T(8,128)(2,1)} %copy.26.q_ref.k_ref.v_ref.do_ref, bf16[4,384,1024]{2,1,0:T(8,128)(2,1)} %copy.26.q_ref.k_ref.v_ref.do_ref, bf16[4,384,1024]{2,1,0:T(8,128)(2,1)} %copy.26.q_ref.k_ref.v_ref.do_ref, bf16[4,384,1024]{2,1,0:T(8,128)(2,1)} %copy.26.q_ref.k_ref.v_ref.do_ref, ...), custom_call_target="tpu_custom_call" | custom-call | tf_op jit(solution)/shard_map/pallas_call | solution.py:130
  152.7 16.6 %collective-permute-done.2 = bf16[2,384,1024]{2,1,0:T(8,128)(2,1)} collective-permute-done((bf16[2,384,1024]{2,1,0:T(8,128)(2,1)}, bf16[2,384,1024]{2,1,0:T(8,128)(2,1)}, u32[]{:S(2)}, u32[]{:S(2)}) %collective-permute-start.2) | collective-permute-done | bytes 1572896 | tf_op jit(solution)/shard_map/ppermute | solution.py:20
  169.3 7.6 %collective-permute-done.3 = bf16[2,384,1024]{2,1,0:T(8,128)(2,1)} collective-permute-done((bf16[2,384,1024]{2,1,0:T(8,128)(2,1)}, bf16[2,384,1024]{2,1,0:T(8,128)(2,1)}, u32[]{:S(2)}, u32[]{:S(2)}) %collective-permute-start.3) | collective-permute-done | bytes 1572896 | tf_op jit(solution)/shard_map/ppermute | solution.py:20
  176.9 3.6 %reshape.241 = bf16[3,64,6,1,1024]{4,2,1,0,3:T(8,128)(2,1)S(1)} reshape(bf16[3,384,1024]{2,1,0:T(8,128)(2,1)} %shard_map.86) | data formatting | bytes 4718592 | tf_op jit(solution)/shard_map/reshape | solution.py:199
  180.5 2.0 copy.30
  182.5 5.4 %all-to-all-start.1 = ((bf16[3,64,6,1,1024]{4,2,0,3,1:T(8,128)(2,1)}), bf16[3,64,6,1,1024]{4,2,0,3,1:T(8,128)(2,1)S(1)}, u32[]{:S(2)}, u32[]{:S(2)}) async-start(bf16[3,64,6,1,1024]{4,2,0,3,1:T(8,128)(2,1)} %copy.30), calls=%async_computation.1 | async-start | bytes 6291456 | tf_op jit(solution)/shard_map/all_to_all | solution.py:198
  187.9 3.7 %add_convert_fusion = bf16[2,384,1024]{2,1,0:T(8,128)(2,1)S(1)} fusion(bf16[2,384,1024]{2,1,0:T(8,128)(2,1)} %collective-permute-done.2, f32[2,384,1024]{2,1,0:T(8,128)} %get-tuple-element.26, bf16[2,384,1024]{2,1,0:T(8,128)(2,1)} %collective-permute-done.3), kind=kLoop, calls=%fused_computation.1 | loop fusion | flops 3932160 | bytes 7864320 | tf_op jit(solution)/shard_map/convert_element_type | solution.py:193
  191.6 1.6 pad_maximum_fusion.1
  193.2 3.8 %collective-permute-start.4 = (bf16[3,384,1024]{2,1,0:T(8,128)(2,1)}, bf16[3,384,1024]{2,1,0:T(8,128)(2,1)}, u32[]{:S(2)}, u32[]{:S(2)}) collective-permute-start(bf16[3,384,1024]{2,1,0:T(8,128)(2,1)} %pad_maximum_fusion.1), channel_id=1, source_target_pairs={{0,192},{64,0},{128,64},{192,128},{1,193},{65,1},{129,65},{193,129... | collective-permute-start | bytes 7077896 | tf_op jit(solution)/shard_map/ppermute | solution.py:20
  197.0 59.3 %all-to-all-done.1 = bf16[3,64,6,1,1024]{4,2,0,3,1:T(8,128)(2,1)S(1)} async-done(((bf16[3,64,6,1,1024]{4,2,0,3,1:T(8,128)(2,1)}), bf16[3,64,6,1,1024]{4,2,0,3,1:T(8,128)(2,1)S(1)}, u32[]{:S(2)}, u32[]{:S(2)}) %all-to-all-start.1) | async-done | bytes 2359328 | tf_op jit(solution)/shard_map/all_to_all | solution.py:198
  256.3 1.3 copy.31
  257.6 5.9 %collective-permute-start.5 = (bf16[3,384,1024]{2,1,0:T(8,128)(2,1)S(1)}, bf16[3,384,1024]{2,1,0:T(8,128)(2,1)S(1)}, u32[]{:S(2)}, u32[]{:S(2)}) collective-permute-start(bf16[3,384,1024]{2,1,0:T(8,128)(2,1)S(1)} %bitcast.43), channel_id=1, source_target_pairs={{0,192},{64,0},{128,64},{192,128},{1,193},{65,1},{129,65},{193,129... | collective-permute-start | bytes 7077896 | tf_op jit(solution)/shard_map/ppermute | solution.py:20
  263.6 1.9 constant_dynamic-update-slice_fusion.1
  265.5 24.9 %collective-permute-done.5 = bf16[3,384,1024]{2,1,0:T(8,128)(2,1)S(1)} collective-permute-done((bf16[3,384,1024]{2,1,0:T(8,128)(2,1)S(1)}, bf16[3,384,1024]{2,1,0:T(8,128)(2,1)S(1)}, u32[]{:S(2)}, u32[]{:S(2)}) %collective-permute-start.5) | collective-permute-done | bytes 2359328 | tf_op jit(solution)/shard_map/ppermute | solution.py:20
  290.4 0.2 constant_dynamic-update-slice_fusion
  290.6 2.4 fusion.14
  (26 shorter events, 0.6 us)
Async XLA Ops:
  2.8 11.6 %copy-start = (bf16[1,384,2048]{2,1,0:T(8,128)(2,1)S(1)}, bf16[1,384,2048]{2,1,0:T(8,128)(2,1)}, u32[]{:S(2)}) copy-start(bf16[1,384,2048]{2,1,0:T(8,128)(2,1)} %param.6) | copy-start | bytes 4718596
  2.8 11.6 %copy-start.1 = (bf16[1,384,2048]{2,1,0:T(8,128)(2,1)S(1)}, bf16[1,384,2048]{2,1,0:T(8,128)(2,1)}, u32[]{:S(2)}) copy-start(bf16[1,384,2048]{2,1,0:T(8,128)(2,1)} %param.9) | copy-start | bytes 4718596
  3.0 45.5 %collective-permute-start = (bf16[2,384,1024]{2,1,0:T(8,128)(2,1)S(1)}, bf16[2,384,1024]{2,1,0:T(8,128)(2,1)}, u32[]{:S(2)}, u32[]{:S(2)}) collective-permute-start(bf16[2,384,1024]{2,1,0:T(8,128)(2,1)S(1)} %pad_maximum_fusion.2), channel_id=1, source_target_pairs={{0,1},{1,2},{2,3},{3,4},{4,5},{5,6},{6,7},{7,8},{8,9},{9,10},{10,1... | collective-permute-start | bytes 4718600 | tf_op jit(solution)/shard_map/ppermute | solution.py:20
  5.1 43.4 %collective-permute-start.1 = (bf16[2,384,1024]{2,1,0:T(8,128)(2,1)S(1)}, bf16[2,384,1024]{2,1,0:T(8,128)(2,1)}, u32[]{:S(2)}, u32[]{:S(2)}) collective-permute-start(bf16[2,384,1024]{2,1,0:T(8,128)(2,1)S(1)} %pad_maximum_fusion.2), channel_id=1, source_target_pairs={{0,63},{1,0},{2,1},{3,2},{4,3},{5,4},{6,5},{7,6},{8,7},{9,8},{10,9... | collective-permute-start | bytes 4718600 | tf_op jit(solution)/shard_map/ppermute | solution.py:20
  52.6 9.4 %copy-start.3 = (s32[3,5]{1,0:T(4,128)S(1)}, s32[3,5]{1,0:T(4,128)}, u32[]{:S(2)}) copy-start(s32[3,5]{1,0:T(4,128)} %param.10) | copy-start | bytes 184
  52.6 80.0 %all-to-all-start = ((bf16[4,6,64,1024]{3,0,1,2:T(4,128)(2,1)}), bf16[4,6,64,1024]{3,0,1,2:T(4,128)(2,1)S(1)}, u32[]{:S(2)}, u32[]{:S(2)}) async-start(bf16[4,6,64,1024]{3,0,1,2:T(4,128)(2,1)} %copy.24), calls=%async_computation | async-start | bytes 6291456 | tf_op jit(solution)/shard_map/all_to_all | solution.py:161
  63.0 75.0 %copy-start.4 = (s32[3,2]{0,1:T(2,128)S(1)}, s32[3,2]{0,1:T(2,128)}, u32[]{:S(2)}) copy-start(s32[3,2]{0,1:T(2,128)} %param.11) | copy-start | bytes 76
  132.6 36.7 %collective-permute-start.2 = (bf16[2,384,1024]{2,1,0:T(8,128)(2,1)}, bf16[2,384,1024]{2,1,0:T(8,128)(2,1)}, u32[]{:S(2)}, u32[]{:S(2)}) collective-permute-start(bf16[2,384,1024]{2,1,0:T(8,128)(2,1)} %get-tuple-element.28), channel_id=1, source_target_pairs={{0,63},{1,0},{2,1},{3,2},{4,3},{5,4},{6,5},{7,6},{8,7},{9,8},{10,9... | collective-permute-start | bytes 4718600 | tf_op jit(solution)/shard_map/ppermute | solution.py:20
  137.9 39.0 %collective-permute-start.3 = (bf16[2,384,1024]{2,1,0:T(8,128)(2,1)}, bf16[2,384,1024]{2,1,0:T(8,128)(2,1)}, u32[]{:S(2)}, u32[]{:S(2)}) collective-permute-start(bf16[2,384,1024]{2,1,0:T(8,128)(2,1)} %get-tuple-element.29), channel_id=1, source_target_pairs={{0,1},{1,2},{2,3},{3,4},{4,5},{5,6},{6,7},{7,8},{8,9},{9,10},{10,1... | collective-permute-start | bytes 4718600 | tf_op jit(solution)/shard_map/ppermute | solution.py:20
  182.5 73.8 %all-to-all-start.1 = ((bf16[3,64,6,1,1024]{4,2,0,3,1:T(8,128)(2,1)}), bf16[3,64,6,1,1024]{4,2,0,3,1:T(8,128)(2,1)S(1)}, u32[]{:S(2)}, u32[]{:S(2)}) async-start(bf16[3,64,6,1,1024]{4,2,0,3,1:T(8,128)(2,1)} %copy.30), calls=%async_computation.1 | async-start | bytes 6291456 | tf_op jit(solution)/shard_map/all_to_all | solution.py:198
  187.9 3.8 %copy-start.2 = (bf16[384,1024]{1,0:T(8,128)(2,1)S(1)}, bf16[384,1024]{1,0:T(8,128)(2,1)}, u32[]{:S(2)}) copy-start(bf16[384,1024]{1,0:T(8,128)(2,1)} %get-tuple-element.25) | copy-start | bytes 2359300
  193.2 70.3 %collective-permute-start.4 = (bf16[3,384,1024]{2,1,0:T(8,128)(2,1)}, bf16[3,384,1024]{2,1,0:T(8,128)(2,1)}, u32[]{:S(2)}, u32[]{:S(2)}) collective-permute-start(bf16[3,384,1024]{2,1,0:T(8,128)(2,1)} %pad_maximum_fusion.1), channel_id=1, source_target_pairs={{0,192},{64,0},{128,64},{192,128},{1,193},{65,1},{129,65},{193,129... | collective-permute-start | bytes 7077896 | tf_op jit(solution)/shard_map/ppermute | solution.py:20
  257.6 32.7 %collective-permute-start.5 = (bf16[3,384,1024]{2,1,0:T(8,128)(2,1)S(1)}, bf16[3,384,1024]{2,1,0:T(8,128)(2,1)S(1)}, u32[]{:S(2)}, u32[]{:S(2)}) collective-permute-start(bf16[3,384,1024]{2,1,0:T(8,128)(2,1)S(1)} %bitcast.43), channel_id=1, source_target_pairs={{0,192},{64,0},{128,64},{192,128},{1,193},{65,1},{129,65},{193,129... | collective-permute-start | bytes 7077896 | tf_op jit(solution)/shard_map/ppermute | solution.py:20

commit v8 on v6

--- a/solution.py
+++ b/solution.py
@@ -156,7 +156,6 @@
     near_before = shifted(near, "seq", 1)
     near_after = shifted(near, "seq", -1)
     sent = jnp.stack([item[:, row_width:] for item in (query_now, key_now, value_now, grad_now)])
-    sent = shifted(sent, "pipe", -1)
 
     sent, near_before, near_after = lax.optimization_barrier((sent, near_before, near_after))
     received = lax.all_to_all(
@@ -188,7 +187,7 @@
         for number in range(block_count)
     )
     col_keep = jnp.any(listed[:, :, None] == col_block[None, None, :], axis=1).astype(jnp.float32)
-    col_grads = col_side(received, col_keep)
+    col_grads = shifted(col_side(received, col_keep), "pipe", -1)
 
     col_grads, from_after, from_before = lax.optimization_barrier((col_grads, from_after, from_before))
     d_total = (d_own + from_before.astype(jnp.float32) + from_after.astype(jnp.float32)).astype(

time: 301 us -> 303 us (level); the launches traced: 296 us -> 302 us
  waiting for transfers between devices: 195 us -> 202 us
    all_to_all x1, waiting for transfers between devices: 63 us -> 68.3 us  [body(): lax.all_to_all(col_grads.reshape(3, devices, share, 1, COLS), 'seq', spli...]
    ppermute x6, waiting for transfers between devices: 85.3 us -> 89.6 us  [shifted(): return lax.ppermute(value, axis, pairs)]
    all_to_all x1, starting transfers between devices: 12.7 us -> 9.41 us  [body(): lax.all_to_all(sent.reshape(4, share, devices, COLS), 'seq', split_axis=2...]
  transfers between devices with their start and end apart: 8 -> 8, of which waited for: 6 -> 6; matrix products, arithmetic and copies ran while one was open for 4% -> 3% of each run, Pallas kernels for 12% -> 8%
where the time goes in v8:
time: 303 us; the launch traced here: 302 us
  waiting for transfers between devices  202 us (67%)
  starting transfers between devices  35.4 us (12%)
  Pallas kernels  35.2 us (12%)
  local copies, waits for them, and re-layouts  18.1 us (6%)
  other arithmetic  10.8 us (4%)
    ppermute x6, waiting for transfers between devices, shifted(): return lax.ppermute(value, axis, pairs)  89.6 us
    all_to_all x1, waiting for transfers between devices, body(): lax.all_to_all(col_grads.reshape(3, devices, share, 1, COLS), 'seq', spli...  68.3 us
    all_to_all x1, waiting for transfers between devices, body(): lax.all_to_all(sent.reshape(4, share, devices, COLS), 'seq', split_axis=2...  43.9 us
    pallas_call x1, Pallas kernels, row_side(): pl.pallas_call(row_kernel, grid=(HEADS_ROW,), in_specs=[plain, plain, sta...  24.3 us
    ppermute x6, starting transfers between devices, shifted(): return lax.ppermute(value, axis, pairs)  19.5 us
    pallas_call x1, Pallas kernels, col_side(): pl.pallas_call(col_kernel, grid=(HEADS_COL,), in_specs=[part_block(0), pa...  10.9 us
    all_to_all x1, starting transfers between devices, body(): lax.all_to_all(sent.reshape(4, share, devices, COLS), 'seq', split_axis=2...  9.41 us
    all_to_all x1, starting transfers between devices, body(): lax.all_to_all(col_grads.reshape(3, devices, share, 1, COLS), 'seq', spli...  6.53 us
  transfers between devices with their start and end apart: 8, of which 6 were waited for; matrix products, arithmetic and copies ran while one was open for 3% of the time, Pallas kernels for 8%

profile of v8, /device:TPU:1, one launch (start us, length us, event | category | flops | bytes accessed | tf_op | source)
XLA Modules:
  0.0 301.9 jit_solution(14305108645373504670)
XLA Ops:
  0.6 2.2 slice_bitcast_fusion
  2.8 0.1 pad_maximum_fusion.3
  3.0 2.1 collective-permute-start
  5.1 9.3 %collective-permute-start.1 = (bf16[2,384,1024]{2,1,0:T(8,128)(2,1)S(1)}, bf16[2,384,1024]{2,1,0:T(8,128)(2,1)}, u32[]{:S(2)}, u32[]{:S(2)}) collective-permute-start(bf16[2,384,1024]{2,1,0:T(8,128)(2,1)S(1)} %pad_maximum_fusion.3), channel_id=1, source_target_pairs={{0,63},{1,0},{2,1},{3,2},{4,3},{5,4},{6,5},{7,6},{8,7},{9,8},{10,9... | collective-permute-start | bytes 4718600 | tf_op jit(solution)/shard_map/ppermute | solution.py:20
  14.4 0.1 slice_bitcast_fusion.2
  14.5 0.4 pad_maximum_fusion
  14.9 33.5 %collective-permute-done.kp_ref.vp_ref = bf16[2,384,1024]{2,1,0:T(8,128)(2,1)} collective-permute-done((bf16[2,384,1024]{2,1,0:T(8,128)(2,1)S(1)}, bf16[2,384,1024]{2,1,0:T(8,128)(2,1)}, u32[]{:S(2)}, u32[]{:S(2)}) %collective-permute-start) | collective-permute-done | bytes 1572896 | tf_op jit(solution)/shard_map/ppermute | solution.py:20
  48.5 4.1 %copy.24 = bf16[4,6,64,1024]{3,0,1,2:T(4,128)(2,1)} copy(bf16[4,6,64,1024]{3,2,1,0:T(8,128)(2,1)S(1)} %bitcast.33) | data formatting | bytes 6291456 | tf_op jit(solution)/shard_map/reshape | solution.py:162
  52.6 9.4 %all-to-all-start = ((bf16[4,6,64,1024]{3,0,1,2:T(4,128)(2,1)}), bf16[4,6,64,1024]{3,0,1,2:T(4,128)(2,1)S(1)}, u32[]{:S(2)}, u32[]{:S(2)}) async-start(bf16[4,6,64,1024]{3,0,1,2:T(4,128)(2,1)} %copy.24), calls=%async_computation | async-start | bytes 6291456 | tf_op jit(solution)/shard_map/all_to_all | solution.py:161
  62.0 0.1 copy.25
  62.4 0.6 copy.34
  63.0 0.2 slice_reduce_fusion.2
  63.3 0.2 compare_reduce_fusion
  63.5 0.9 convert_element_type.43.keep_ref
  64.4 24.3 %shard_map.85 = (bf16[384,1024]{1,0:T(8,128)(2,1)}, bf16[2,384,1024]{2,1,0:T(8,128)(2,1)}, f32[2,384,1024]{2,1,0:T(8,128)}, bf16[2,384,1024]{2,1,0:T(8,128)(2,1)}) custom-call(bf16[384,2048]{1,0:T(8,128)(2,1)} %bitcast.42, bf16[384,2048]{1,0:T(8,128)(2,1)} %bitcast.40, bf16[2,384,1024]{2,1,0:T(8,128)(2,1)} %collective-permute-done.kp_ref.vp_ref, ...), custom_call_target="tpu_custom_call" | custom-call | tf_op jit(solution)/shard_map/pallas_call | solution.py:97
  88.6 43.9 %all-to-all-done = bf16[4,6,64,1024]{3,0,1,2:T(4,128)(2,1)S(1)} async-done(((bf16[4,6,64,1024]{3,0,1,2:T(4,128)(2,1)}), bf16[4,6,64,1024]{3,0,1,2:T(4,128)(2,1)S(1)}, u32[]{:S(2)}, u32[]{:S(2)}) %all-to-all-start) | async-done | bytes 3145760 | tf_op jit(solution)/shard_map/all_to_all | solution.py:161
  132.6 2.7 copy.26.q_ref.k_ref.v_ref.do_ref
  135.2 10.9 %shard_map.86 = bf16[3,384,1024]{2,1,0:T(8,128)(2,1)} custom-call(bf16[4,384,1024]{2,1,0:T(8,128)(2,1)} %copy.26.q_ref.k_ref.v_ref.do_ref, bf16[4,384,1024]{2,1,0:T(8,128)(2,1)} %copy.26.q_ref.k_ref.v_ref.do_ref, bf16[4,384,1024]{2,1,0:T(8,128)(2,1)} %copy.26.q_ref.k_ref.v_ref.do_ref, bf16[4,384,1024]{2,1,0:T(8,128)(2,1)} %copy.26.q_ref.k_ref.v_ref.do_ref, ...), custom_call_target="tpu_custom_call" | custom-call | tf_op jit(solution)/shard_map/pallas_call | solution.py:130
  146.1 4.4 %collective-permute-start.2 = (bf16[3,384,1024]{2,1,0:T(8,128)(2,1)}, bf16[3,384,1024]{2,1,0:T(8,128)(2,1)}, u32[]{:S(2)}, u32[]{:S(2)}) collective-permute-start(bf16[3,384,1024]{2,1,0:T(8,128)(2,1)} %shard_map.86), channel_id=1, source_target_pairs={{0,192},{64,0},{128,64},{192,128},{1,193},{65,1},{129,65},{193,129... | collective-permute-start | bytes 7077896 | tf_op jit(solution)/shard_map/ppermute | solution.py:20
  150.6 3.6 %collective-permute-start.3 = (bf16[2,384,1024]{2,1,0:T(8,128)(2,1)S(1)}, bf16[2,384,1024]{2,1,0:T(8,128)(2,1)S(1)}, u32[]{:S(2)}, u32[]{:S(2)}) collective-permute-start(bf16[2,384,1024]{2,1,0:T(8,128)(2,1)S(1)} %copy-done.8), channel_id=1, source_target_pairs={{0,63},{1,0},{2,1},{3,2},{4,3},{5,4},{6,5},{7,6},{8,7},{9,8},{10,9... | collective-permute-start | bytes 4718600 | tf_op jit(solution)/shard_map/ppermute | solution.py:20
  154.2 33.7 %collective-permute-done.3 = bf16[2,384,1024]{2,1,0:T(8,128)(2,1)S(1)} collective-permute-done((bf16[2,384,1024]{2,1,0:T(8,128)(2,1)S(1)}, bf16[2,384,1024]{2,1,0:T(8,128)(2,1)S(1)}, u32[]{:S(2)}, u32[]{:S(2)}) %collective-permute-start.3) | collective-permute-done | bytes 1572896 | tf_op jit(solution)/shard_map/ppermute | solution.py:20
  187.9 7.6 %collective-permute-done.4 = bf16[2,384,1024]{2,1,0:T(8,128)(2,1)S(1)} collective-permute-done((bf16[2,384,1024]{2,1,0:T(8,128)(2,1)S(1)}, bf16[2,384,1024]{2,1,0:T(8,128)(2,1)S(1)}, u32[]{:S(2)}, u32[]{:S(2)}) %collective-permute-start.4) | collective-permute-done | bytes 1572896 | tf_op jit(solution)/shard_map/ppermute | solution.py:20
  195.5 1.1 copy-done.3
  196.7 14.7 %collective-permute-done.2 = bf16[3,384,1024]{2,1,0:T(8,128)(2,1)} collective-permute-done((bf16[3,384,1024]{2,1,0:T(8,128)(2,1)}, bf16[3,384,1024]{2,1,0:T(8,128)(2,1)}, u32[]{:S(2)}, u32[]{:S(2)}) %collective-permute-start.2) | collective-permute-done | bytes 2359328 | tf_op jit(solution)/shard_map/ppermute | solution.py:20
  211.4 3.6 %reshape.241 = bf16[3,64,6,1,1024]{4,2,1,0,3:T(8,128)(2,1)S(1)} reshape(bf16[3,384,1024]{2,1,0:T(8,128)(2,1)} %collective-permute-done.2) | data formatting | bytes 4718592 | tf_op jit(solution)/shard_map/reshape | solution.py:199
  215.0 2.0 copy.30
  216.9 6.5 %all-to-all-start.1 = ((bf16[3,64,6,1,1024]{4,2,0,3,1:T(8,128)(2,1)}), bf16[3,64,6,1,1024]{4,2,0,3,1:T(8,128)(2,1)S(1)}, u32[]{:S(2)}, u32[]{:S(2)}) async-start(bf16[3,64,6,1,1024]{4,2,0,3,1:T(8,128)(2,1)} %copy.30), calls=%async_computation.1 | async-start | bytes 6291456 | tf_op jit(solution)/shard_map/all_to_all | solution.py:198
  223.5 3.7 %add_convert_fusion = bf16[2,384,1024]{2,1,0:T(8,128)(2,1)S(1)} fusion(bf16[2,384,1024]{2,1,0:T(8,128)(2,1)} %copy-done.2, f32[2,384,1024]{2,1,0:T(8,128)} %get-tuple-element.26, bf16[2,384,1024]{2,1,0:T(8,128)(2,1)} %copy-done.3), kind=kLoop, calls=%fused_computation.5 | loop fusion | flops 3932160 | bytes 7864320 | tf_op jit(solution)/shard_map/convert_element_type | solution.py:193
  227.3 1.6 pad_maximum_fusion.1
  228.9 68.3 %all-to-all-done.1 = bf16[3,64,6,1,1024]{4,2,0,3,1:T(8,128)(2,1)S(1)} async-done(((bf16[3,64,6,1,1024]{4,2,0,3,1:T(8,128)(2,1)}), bf16[3,64,6,1,1024]{4,2,0,3,1:T(8,128)(2,1)S(1)}, u32[]{:S(2)}, u32[]{:S(2)}) %all-to-all-start.1) | async-done | bytes 2359328 | tf_op jit(solution)/shard_map/all_to_all | solution.py:198
  297.2 1.3 copy.31
  298.5 3.5 %pad_maximum_fusion.2 = (bf16[1,384,2048]{2,1,0:T(8,128)(2,1)}, bf16[1,384,2048]{2,1,0:T(8,128)(2,1)}, bf16[1,384,2048]{2,1,0:T(8,128)(2,1)}) fusion(bf16[3,384,1024]{2,1,0:T(8,128)(2,1)S(1)} %bitcast.35, bf16[3,384,1024]{2,1,0:T(8,128)(2,1)} %collective-permute-done.5), kind=kLoop, calls=%fused_computation.9 | loop fusion | flops 9437184 | bytes 9437184 | tf_op jit(solution)/shard_map/concatenate | solution.py:202
  (32 shorter events, 0.4 us)
Async XLA Ops:
  2.8 11.6 %copy-start = (bf16[1,384,2048]{2,1,0:T(8,128)(2,1)S(1)}, bf16[1,384,2048]{2,1,0:T(8,128)(2,1)}, u32[]{:S(2)}) copy-start(bf16[1,384,2048]{2,1,0:T(8,128)(2,1)} %param.9) | copy-start | bytes 4718596
  2.8 11.6 %copy-start.1 = (bf16[1,384,2048]{2,1,0:T(8,128)(2,1)S(1)}, bf16[1,384,2048]{2,1,0:T(8,128)(2,1)}, u32[]{:S(2)}) copy-start(bf16[1,384,2048]{2,1,0:T(8,128)(2,1)} %param.6) | copy-start | bytes 4718596
  3.0 45.5 %collective-permute-start = (bf16[2,384,1024]{2,1,0:T(8,128)(2,1)S(1)}, bf16[2,384,1024]{2,1,0:T(8,128)(2,1)}, u32[]{:S(2)}, u32[]{:S(2)}) collective-permute-start(bf16[2,384,1024]{2,1,0:T(8,128)(2,1)S(1)} %pad_maximum_fusion.3), channel_id=1, source_target_pairs={{0,1},{1,2},{2,3},{3,4},{4,5},{5,6},{6,7},{7,8},{8,9},{9,10},{10,1... | collective-permute-start | bytes 4718600 | tf_op jit(solution)/shard_map/ppermute | solution.py:20
  5.1 43.4 %collective-permute-start.1 = (bf16[2,384,1024]{2,1,0:T(8,128)(2,1)S(1)}, bf16[2,384,1024]{2,1,0:T(8,128)(2,1)}, u32[]{:S(2)}, u32[]{:S(2)}) collective-permute-start(bf16[2,384,1024]{2,1,0:T(8,128)(2,1)S(1)} %pad_maximum_fusion.3), channel_id=1, source_target_pairs={{0,63},{1,0},{2,1},{3,2},{4,3},{5,4},{6,5},{7,6},{8,7},{9,8},{10,9... | collective-permute-start | bytes 4718600 | tf_op jit(solution)/shard_map/ppermute | solution.py:20
  52.6 9.4 %copy-start.5 = (s32[3,5]{1,0:T(4,128)S(1)}, s32[3,5]{1,0:T(4,128)}, u32[]{:S(2)}) copy-start(s32[3,5]{1,0:T(4,128)} %param.10) | copy-start | bytes 184
  52.6 10.4 %copy-start.6 = (s32[3,2]{0,1:T(2,128)S(1)}, s32[3,2]{0,1:T(2,128)}, u32[]{:S(2)}) copy-start(s32[3,2]{0,1:T(2,128)} %param.11) | copy-start | bytes 76
  52.6 80.0 %all-to-all-start = ((bf16[4,6,64,1024]{3,0,1,2:T(4,128)(2,1)}), bf16[4,6,64,1024]{3,0,1,2:T(4,128)(2,1)S(1)}, u32[]{:S(2)}, u32[]{:S(2)}) async-start(bf16[4,6,64,1024]{3,0,1,2:T(4,128)(2,1)} %copy.24), calls=%async_computation | async-start | bytes 6291456 | tf_op jit(solution)/shard_map/all_to_all | solution.py:161
  135.2 15.3 %copy-start.8 = (bf16[2,384,1024]{2,1,0:T(8,128)(2,1)S(1)}, bf16[2,384,1024]{2,1,0:T(8,128)(2,1)}, u32[]{:S(2)}) copy-start(bf16[2,384,1024]{2,1,0:T(8,128)(2,1)} %get-tuple-element.28) | copy-start | bytes 4718596
  135.2 19.0 %copy-start.7 = (bf16[2,384,1024]{2,1,0:T(8,128)(2,1)S(1)}, bf16[2,384,1024]{2,1,0:T(8,128)(2,1)}, u32[]{:S(2)}) copy-start(bf16[2,384,1024]{2,1,0:T(8,128)(2,1)} %get-tuple-element.29) | copy-start | bytes 4718596
  146.1 65.3 %collective-permute-start.2 = (bf16[3,384,1024]{2,1,0:T(8,128)(2,1)}, bf16[3,384,1024]{2,1,0:T(8,128)(2,1)}, u32[]{:S(2)}, u32[]{:S(2)}) collective-permute-start(bf16[3,384,1024]{2,1,0:T(8,128)(2,1)} %shard_map.86), channel_id=1, source_target_pairs={{0,192},{64,0},{128,64},{192,128},{1,193},{65,1},{129,65},{193,129... | collective-permute-start | bytes 7077896 | tf_op jit(solution)/shard_map/ppermute | solution.py:20
  150.6 37.3 %collective-permute-start.3 = (bf16[2,384,1024]{2,1,0:T(8,128)(2,1)S(1)}, bf16[2,384,1024]{2,1,0:T(8,128)(2,1)S(1)}, u32[]{:S(2)}, u32[]{:S(2)}) collective-permute-start(bf16[2,384,1024]{2,1,0:T(8,128)(2,1)S(1)} %copy-done.8), channel_id=1, source_target_pairs={{0,63},{1,0},{2,1},{3,2},{4,3},{5,4},{6,5},{7,6},{8,7},{9,8},{10,9... | collective-permute-start | bytes 4718600 | tf_op jit(solution)/shard_map/ppermute | solution.py:20
  154.2 41.3 %collective-permute-start.4 = (bf16[2,384,1024]{2,1,0:T(8,128)(2,1)S(1)}, bf16[2,384,1024]{2,1,0:T(8,128)(2,1)S(1)}, u32[]{:S(2)}, u32[]{:S(2)}) collective-permute-start(bf16[2,384,1024]{2,1,0:T(8,128)(2,1)S(1)} %copy-done.7), channel_id=1, source_target_pairs={{0,1},{1,2},{2,3},{3,4},{4,5},{5,6},{6,7},{7,8},{8,9},{9,10},{10,1... | collective-permute-start | bytes 4718600 | tf_op jit(solution)/shard_map/ppermute | solution.py:20
  187.9 7.6 %copy-start.2 = (bf16[2,384,1024]{2,1,0:T(8,128)(2,1)}, bf16[2,384,1024]{2,1,0:T(8,128)(2,1)S(1)}, u32[]{:S(2)}) copy-start(bf16[2,384,1024]{2,1,0:T(8,128)(2,1)S(1)} %collective-permute-done.3) | copy-start | bytes 4718596
  195.5 1.1 copy-start.3
  216.9 80.2 %all-to-all-start.1 = ((bf16[3,64,6,1,1024]{4,2,0,3,1:T(8,128)(2,1)}), bf16[3,64,6,1,1024]{4,2,0,3,1:T(8,128)(2,1)S(1)}, u32[]{:S(2)}, u32[]{:S(2)}) async-start(bf16[3,64,6,1,1024]{4,2,0,3,1:T(8,128)(2,1)} %copy.30), calls=%async_computation.1 | async-start | bytes 6291456 | tf_op jit(solution)/shard_map/all_to_all | solution.py:198
  223.5 3.8 %copy-start.4 = (bf16[384,1024]{1,0:T(8,128)(2,1)S(1)}, bf16[384,1024]{1,0:T(8,128)(2,1)}, u32[]{:S(2)}) copy-start(bf16[384,1024]{1,0:T(8,128)(2,1)} %get-tuple-element.25) | copy-start | bytes 2359300
  228.9 69.6 %collective-permute-start.5 = (bf16[3,384,1024]{2,1,0:T(8,128)(2,1)}, bf16[3,384,1024]{2,1,0:T(8,128)(2,1)}, u32[]{:S(2)}, u32[]{:S(2)}) collective-permute-start(bf16[3,384,1024]{2,1,0:T(8,128)(2,1)} %pad_maximum_fusion.1), channel_id=1, source_target_pairs={{0,192},{64,0},{128,64},{192,128},{1,193},{65,1},{129,65},{193,129... | collective-permute-start | bytes 7077896 | tf_op jit(solution)/shard_map/ppermute | solution.py:20

commit v9 on v7

--- a/solution.py
+++ b/solution.py
@@ -157,9 +157,10 @@
     near_after = shifted(near, "seq", -1)
     sent = jnp.stack([item[:, row_width:] for item in (query_now, key_now, value_now, grad_now)])
 
+    sent = sent.reshape(4, share, devices, COLS)
     sent, near_before, near_after = lax.optimization_barrier((sent, near_before, near_after))
     received = lax.all_to_all(
-        sent.reshape(4, share, devices, COLS), "seq", split_axis=2, concat_axis=1, tiled=True
+        sent, "seq", split_axis=2, concat_axis=1, tiled=True
     ).reshape(4, tokens, COLS)
 
     own_blocks = position * block_count + jnp.arange(block_count, dtype=jnp.int32)
@@ -187,7 +188,7 @@
         for number in range(block_count)
     )
     col_keep = jnp.any(listed[:, :, None] == col_block[None, None, :], axis=1).astype(jnp.float32)
-    col_grads = col_side(received, col_keep)
+    col_grads = col_side(received, col_keep).reshape(3, devices, share, 1, COLS)
 
     col_grads, from_after, from_before = lax.optimization_barrier((col_grads, from_after, from_before))
     d_total = (d_own + from_before.astype(jnp.float32) + from_after.astype(jnp.float32)).astype(
@@ -196,7 +197,7 @@
     row_grads = jnp.concatenate([dq_row[None], d_total], axis=0)
     row_handed = shifted(row_grads, "pipe", -1)
     returned = lax.all_to_all(
-        col_grads.reshape(3, devices, share, 1, COLS), "seq", split_axis=1, concat_axis=3, tiled=True
+        col_grads, "seq", split_axis=1, concat_axis=3, tiled=True
     ).reshape(3, tokens, COLS)
     col_handed = shifted(returned, "pipe", -1)
 

time: 295 us -> 287 us (0.973)
  waiting for transfers between devices: 187 us -> 171 us
  other arithmetic: 7.29 us -> 15.2 us
    ppermute x6, waiting for transfers between devices: 82.7 us -> 66.2 us  [shifted(): return lax.ppermute(value, axis, pairs)]
    another operation x1, other arithmetic: 0.44 us -> 8.39 us  [body(): jnp.stack([item[:, row_width:] for item in (query_now, key_now, value_now...]
    reshape x3 -> x1, local copies, waits for them, and re-layouts: 9.67 us -> 3.57 us  [body(): col_grads = col_side(received, col_keep).reshape(3, devices, share, 1, COLS)]
    another operation x1 -> x4, local copies, waits for them, and re-layouts: 0.12 us -> 4.86 us  [body(): jnp.stack([item[:, row_width:] for item in (query_now, key_now, value_now...]
  transfers between devices with their start and end apart: 8 -> 8, of which waited for: 6 -> 6; matrix products, arithmetic and copies ran while one was open for 5% -> 11% of each run, Pallas kernels for 12% -> 12%
where the time goes in v9:
time: 287 us; the launch traced here: 285 us
  waiting for transfers between devices  171 us (60%)
  starting transfers between devices  41.3 us (14%)
  Pallas kernels  35.1 us (12%)
  local copies, waits for them, and re-layouts  22.1 us (8%)
  other arithmetic  15.2 us (5%)
    ppermute x6, waiting for transfers between devices, shifted(): return lax.ppermute(value, axis, pairs)  66.2 us
    all_to_all x1, waiting for transfers between devices, body(): lax.all_to_all(col_grads, 'seq', split_axis=1, concat_axis=3, tiled=True)  59.3 us
    all_to_all x1, waiting for transfers between devices, body(): lax.all_to_all(sent, 'seq', split_axis=2, concat_axis=1, tiled=True)  45.1 us
    ppermute x6, starting transfers between devices, shifted(): return lax.ppermute(value, axis, pairs)  26.4 us
    pallas_call x1, Pallas kernels, row_side(): pl.pallas_call(row_kernel, grid=(HEADS_ROW,), in_specs=[plain, plain, sta...  24.3 us
    pallas_call x1, Pallas kernels, col_side(): pl.pallas_call(col_kernel, grid=(HEADS_COL,), in_specs=[part_block(0), pa...  10.7 us
    all_to_all x1, starting transfers between devices, body(): lax.all_to_all(sent, 'seq', split_axis=2, concat_axis=1, tiled=True)  9.46 us
    another operation x1, other arithmetic, body(): jnp.stack([item[:, row_width:] for item in (query_now, key_now, value_now...  8.39 us
  transfers between devices with their start and end apart: 8, of which 6 were waited for; matrix products, arithmetic and copies ran while one was open for 11% of the time, Pallas kernels for 12%

profile of v9, /device:TPU:1, one launch (start us, length us, event | category | flops | bytes accessed | tf_op | source)
XLA Modules:
  0.0 285.1 jit_solution(924780924136335249)
XLA Ops:
  0.6 2.2 slice_bitcast_fusion
  3.0 2.1 collective-permute-start
  5.1 9.3 %collective-permute-start.1 = (bf16[2,384,1024]{2,1,0:T(8,128)(2,1)S(1)}, bf16[2,384,1024]{2,1,0:T(8,128)(2,1)}, u32[]{:S(2)}, u32[]{:S(2)}) collective-permute-start(bf16[2,384,1024]{2,1,0:T(8,128)(2,1)S(1)} %pad_maximum_fusion.2), channel_id=1, source_target_pairs={{0,63},{1,0},{2,1},{3,2},{4,3},{5,4},{6,5},{7,6},{8,7},{9,8},{10,9... | collective-permute-start | bytes 4718600 | tf_op jit(solution)/shard_map/ppermute | solution.py:20
  14.4 1.2 copy.36
  15.7 1.2 copy.35
  16.9 1.2 copy.34
  18.2 1.2 copy.33
  19.4 8.4 %pad_maximum_fusion = bf16[4,6,64,1024]{3,0,1,2:T(4,128)(2,1)} fusion(bf16[1,6,64,1024]{3,0,1,2:T(2,128)(2,1)S(1)} %copy.36, bf16[1,6,64,1024]{3,0,1,2:T(2,128)(2,1)S(1)} %copy.35, bf16[1,6,64,1024]{3,0,1,2:T(2,128)(2,1)S(1)} %copy.34, bf16[1,6,64,1024]{3,0,1,2:T(2,128)(2,1)S(1)} %copy.33), kind=kLoop, calls=%fused_computation | loop fusion | flops 12582912 | bytes 6291456 | tf_op jit(solution)/shard_map/stack | solution.py:158
  27.8 20.7 %collective-permute-done.kp_ref.vp_ref = bf16[2,384,1024]{2,1,0:T(8,128)(2,1)} collective-permute-done((bf16[2,384,1024]{2,1,0:T(8,128)(2,1)S(1)}, bf16[2,384,1024]{2,1,0:T(8,128)(2,1)}, u32[]{:S(2)}, u32[]{:S(2)}) %collective-permute-start) | collective-permute-done | bytes 1572896 | tf_op jit(solution)/shard_map/ppermute | solution.py:20
  48.5 9.5 %all-to-all-start = ((bf16[4,6,64,1024]{3,0,1,2:T(4,128)(2,1)}), bf16[4,6,64,1024]{3,0,1,2:T(4,128)(2,1)S(1)}, u32[]{:S(2)}, u32[]{:S(2)}) async-start(bf16[4,6,64,1024]{3,0,1,2:T(4,128)(2,1)} %pad_maximum_fusion), calls=%async_computation | async-start | bytes 6291456 | tf_op jit(solution)/shard_map/all_to_all | solution.py:162
  58.3 0.6 copy.46
  58.9 24.3 %shard_map.85 = (bf16[384,1024]{1,0:T(8,128)(2,1)}, bf16[2,384,1024]{2,1,0:T(8,128)(2,1)}, f32[2,384,1024]{2,1,0:T(8,128)}, bf16[2,384,1024]{2,1,0:T(8,128)(2,1)}) custom-call(bf16[384,2048]{1,0:T(8,128)(2,1)} %bitcast.33, bf16[384,2048]{1,0:T(8,128)(2,1)} %bitcast.35, bf16[2,384,1024]{2,1,0:T(8,128)(2,1)} %collective-permute-done.kp_ref.vp_ref, ...), custom_call_target="tpu_custom_call" | custom-call | tf_op jit(solution)/shard_map/pallas_call | solution.py:97
  83.3 45.1 %all-to-all-done = bf16[4,6,64,1024]{3,0,1,2:T(4,128)(2,1)S(1)} async-done(((bf16[4,6,64,1024]{3,0,1,2:T(4,128)(2,1)}), bf16[4,6,64,1024]{3,0,1,2:T(4,128)(2,1)S(1)}, u32[]{:S(2)}, u32[]{:S(2)}) %all-to-all-start) | async-done | bytes 3145760 | tf_op jit(solution)/shard_map/all_to_all | solution.py:162
  128.3 5.4 %collective-permute-start.2 = (bf16[2,384,1024]{2,1,0:T(8,128)(2,1)}, bf16[2,384,1024]{2,1,0:T(8,128)(2,1)}, u32[]{:S(2)}, u32[]{:S(2)}) collective-permute-start(bf16[2,384,1024]{2,1,0:T(8,128)(2,1)} %get-tuple-element.28), channel_id=1, source_target_pairs={{0,63},{1,0},{2,1},{3,2},{4,3},{5,4},{6,5},{7,6},{8,7},{9,8},{10,9... | collective-permute-start | bytes 4718600 | tf_op jit(solution)/shard_map/ppermute | solution.py:20
  134.2 0.9 convert_element_type.43.keep_ref
  135.1 2.7 copy.38.q_ref.k_ref.v_ref.do_ref
  137.7 10.7 %shard_map.86 = bf16[3,384,1024]{2,1,0:T(8,128)(2,1)} custom-call(bf16[4,384,1024]{2,1,0:T(8,128)(2,1)} %copy.38.q_ref.k_ref.v_ref.do_ref, bf16[4,384,1024]{2,1,0:T(8,128)(2,1)} %copy.38.q_ref.k_ref.v_ref.do_ref, bf16[4,384,1024]{2,1,0:T(8,128)(2,1)} %copy.38.q_ref.k_ref.v_ref.do_ref, bf16[4,384,1024]{2,1,0:T(8,128)(2,1)} %copy.38.q_ref.k_ref.v_ref.do_ref, ...), custom_call_target="tpu_custom_call" | custom-call | tf_op jit(solution)/shard_map/pallas_call | solution.py:130
  148.5 3.6 %reshape.246 = bf16[3,64,6,1,1024]{4,2,1,0,3:T(8,128)(2,1)S(1)} reshape(bf16[3,384,1024]{2,1,0:T(8,128)(2,1)} %shard_map.86) | data formatting | bytes 4718592 | tf_op jit(solution)/shard_map/reshape | solution.py:191
  152.0 13.0 %collective-permute-done.2 = bf16[2,384,1024]{2,1,0:T(8,128)(2,1)} collective-permute-done((bf16[2,384,1024]{2,1,0:T(8,128)(2,1)}, bf16[2,384,1024]{2,1,0:T(8,128)(2,1)}, u32[]{:S(2)}, u32[]{:S(2)}) %collective-permute-start.2) | collective-permute-done | bytes 1572896 | tf_op jit(solution)/shard_map/ppermute | solution.py:20
  165.0 7.6 %collective-permute-done.3 = bf16[2,384,1024]{2,1,0:T(8,128)(2,1)} collective-permute-done((bf16[2,384,1024]{2,1,0:T(8,128)(2,1)}, bf16[2,384,1024]{2,1,0:T(8,128)(2,1)}, u32[]{:S(2)}, u32[]{:S(2)}) %collective-permute-start.3) | collective-permute-done | bytes 1572896 | tf_op jit(solution)/shard_map/ppermute | solution.py:20
  172.7 2.0 copy.42
  174.7 5.4 %all-to-all-start.1 = ((bf16[3,64,6,1,1024]{4,2,0,3,1:T(8,128)(2,1)}), bf16[3,64,6,1,1024]{4,2,0,3,1:T(8,128)(2,1)S(1)}, u32[]{:S(2)}, u32[]{:S(2)}) async-start(bf16[3,64,6,1,1024]{4,2,0,3,1:T(8,128)(2,1)} %copy.42), calls=%async_computation.1 | async-start | bytes 6291456 | tf_op jit(solution)/shard_map/all_to_all | solution.py:199
  180.0 3.7 %add_convert_fusion = bf16[2,384,1024]{2,1,0:T(8,128)(2,1)S(1)} fusion(bf16[2,384,1024]{2,1,0:T(8,128)(2,1)} %collective-permute-done.2, f32[2,384,1024]{2,1,0:T(8,128)} %get-tuple-element.26, bf16[2,384,1024]{2,1,0:T(8,128)(2,1)} %collective-permute-done.3), kind=kLoop, calls=%fused_computation.1 | loop fusion | flops 3932160 | bytes 7864320 | tf_op jit(solution)/shard_map/convert_element_type | solution.py:194
  183.8 1.6 pad_maximum_fusion.1
  185.4 3.8 %collective-permute-start.4 = (bf16[3,384,1024]{2,1,0:T(8,128)(2,1)}, bf16[3,384,1024]{2,1,0:T(8,128)(2,1)}, u32[]{:S(2)}, u32[]{:S(2)}) collective-permute-start(bf16[3,384,1024]{2,1,0:T(8,128)(2,1)} %pad_maximum_fusion.1), channel_id=1, source_target_pairs={{0,192},{64,0},{128,64},{192,128},{1,193},{65,1},{129,65},{193,129... | collective-permute-start | bytes 7077896 | tf_op jit(solution)/shard_map/ppermute | solution.py:20
  189.2 59.3 %all-to-all-done.1 = bf16[3,64,6,1,1024]{4,2,0,3,1:T(8,128)(2,1)S(1)} async-done(((bf16[3,64,6,1,1024]{4,2,0,3,1:T(8,128)(2,1)}), bf16[3,64,6,1,1024]{4,2,0,3,1:T(8,128)(2,1)S(1)}, u32[]{:S(2)}, u32[]{:S(2)}) %all-to-all-start.1) | async-done | bytes 2359328 | tf_op jit(solution)/shard_map/all_to_all | solution.py:199
  248.5 1.3 copy.43
  249.8 5.9 %collective-permute-start.5 = (bf16[3,384,1024]{2,1,0:T(8,128)(2,1)S(1)}, bf16[3,384,1024]{2,1,0:T(8,128)(2,1)S(1)}, u32[]{:S(2)}, u32[]{:S(2)}) collective-permute-start(bf16[3,384,1024]{2,1,0:T(8,128)(2,1)S(1)} %bitcast.41), channel_id=1, source_target_pairs={{0,192},{64,0},{128,64},{192,128},{1,193},{65,1},{129,65},{193,129... | collective-permute-start | bytes 7077896 | tf_op jit(solution)/shard_map/ppermute | solution.py:20
  255.7 1.9 constant_dynamic-update-slice_fusion.1
  257.7 24.9 %collective-permute-done.5 = bf16[3,384,1024]{2,1,0:T(8,128)(2,1)S(1)} collective-permute-done((bf16[3,384,1024]{2,1,0:T(8,128)(2,1)S(1)}, bf16[3,384,1024]{2,1,0:T(8,128)(2,1)S(1)}, u32[]{:S(2)}, u32[]{:S(2)}) %collective-permute-start.5) | collective-permute-done | bytes 2359328 | tf_op jit(solution)/shard_map/ppermute | solution.py:20
  282.5 0.2 constant_dynamic-update-slice_fusion
  282.8 2.4 fusion.14
  (30 shorter events, 1.1 us)
Async XLA Ops:
  2.8 11.6 %copy-start.1 = (bf16[1,384,2048]{2,1,0:T(8,128)(2,1)S(1)}, bf16[1,384,2048]{2,1,0:T(8,128)(2,1)}, u32[]{:S(2)}) copy-start(bf16[1,384,2048]{2,1,0:T(8,128)(2,1)} %param.9) | copy-start | bytes 4718596
  3.0 45.5 %collective-permute-start = (bf16[2,384,1024]{2,1,0:T(8,128)(2,1)S(1)}, bf16[2,384,1024]{2,1,0:T(8,128)(2,1)}, u32[]{:S(2)}, u32[]{:S(2)}) collective-permute-start(bf16[2,384,1024]{2,1,0:T(8,128)(2,1)S(1)} %pad_maximum_fusion.2), channel_id=1, source_target_pairs={{0,1},{1,2},{2,3},{3,4},{4,5},{5,6},{6,7},{7,8},{8,9},{9,10},{10,1... | collective-permute-start | bytes 4718600 | tf_op jit(solution)/shard_map/ppermute | solution.py:20
  5.1 43.4 %collective-permute-start.1 = (bf16[2,384,1024]{2,1,0:T(8,128)(2,1)S(1)}, bf16[2,384,1024]{2,1,0:T(8,128)(2,1)}, u32[]{:S(2)}, u32[]{:S(2)}) collective-permute-start(bf16[2,384,1024]{2,1,0:T(8,128)(2,1)S(1)} %pad_maximum_fusion.2), channel_id=1, source_target_pairs={{0,63},{1,0},{2,1},{3,2},{4,3},{5,4},{6,5},{7,6},{8,7},{9,8},{10,9... | collective-permute-start | bytes 4718600 | tf_op jit(solution)/shard_map/ppermute | solution.py:20
  15.7 2.5 copy-start
  27.8 30.1 %copy-start.3 = (s32[3,5]{1,0:T(4,128)S(1)}, s32[3,5]{1,0:T(4,128)}, u32[]{:S(2)}) copy-start(s32[3,5]{1,0:T(4,128)} %param.10) | copy-start | bytes 184
  48.5 79.8 %all-to-all-start = ((bf16[4,6,64,1024]{3,0,1,2:T(4,128)(2,1)}), bf16[4,6,64,1024]{3,0,1,2:T(4,128)(2,1)S(1)}, u32[]{:S(2)}, u32[]{:S(2)}) async-start(bf16[4,6,64,1024]{3,0,1,2:T(4,128)(2,1)} %pad_maximum_fusion), calls=%async_computation | async-start | bytes 6291456 | tf_op jit(solution)/shard_map/all_to_all | solution.py:162
  58.9 74.8 %copy-start.4 = (s32[3,2]{0,1:T(2,128)S(1)}, s32[3,2]{0,1:T(2,128)}, u32[]{:S(2)}) copy-start(s32[3,2]{0,1:T(2,128)} %param.11) | copy-start | bytes 76
  128.3 36.7 %collective-permute-start.2 = (bf16[2,384,1024]{2,1,0:T(8,128)(2,1)}, bf16[2,384,1024]{2,1,0:T(8,128)(2,1)}, u32[]{:S(2)}, u32[]{:S(2)}) collective-permute-start(bf16[2,384,1024]{2,1,0:T(8,128)(2,1)} %get-tuple-element.28), channel_id=1, source_target_pairs={{0,63},{1,0},{2,1},{3,2},{4,3},{5,4},{6,5},{7,6},{8,7},{9,8},{10,9... | collective-permute-start | bytes 4718600 | tf_op jit(solution)/shard_map/ppermute | solution.py:20
  133.7 39.0 %collective-permute-start.3 = (bf16[2,384,1024]{2,1,0:T(8,128)(2,1)}, bf16[2,384,1024]{2,1,0:T(8,128)(2,1)}, u32[]{:S(2)}, u32[]{:S(2)}) collective-permute-start(bf16[2,384,1024]{2,1,0:T(8,128)(2,1)} %get-tuple-element.29), channel_id=1, source_target_pairs={{0,1},{1,2},{2,3},{3,4},{4,5},{5,6},{6,7},{7,8},{8,9},{9,10},{10,1... | collective-permute-start | bytes 4718600 | tf_op jit(solution)/shard_map/ppermute | solution.py:20
  174.7 73.8 %all-to-all-start.1 = ((bf16[3,64,6,1,1024]{4,2,0,3,1:T(8,128)(2,1)}), bf16[3,64,6,1,1024]{4,2,0,3,1:T(8,128)(2,1)S(1)}, u32[]{:S(2)}, u32[]{:S(2)}) async-start(bf16[3,64,6,1,1024]{4,2,0,3,1:T(8,128)(2,1)} %copy.42), calls=%async_computation.1 | async-start | bytes 6291456 | tf_op jit(solution)/shard_map/all_to_all | solution.py:199
  180.0 3.8 %copy-start.2 = (bf16[384,1024]{1,0:T(8,128)(2,1)S(1)}, bf16[384,1024]{1,0:T(8,128)(2,1)}, u32[]{:S(2)}) copy-start(bf16[384,1024]{1,0:T(8,128)(2,1)} %get-tuple-element.25) | copy-start | bytes 2359300
  185.4 70.3 %collective-permute-start.4 = (bf16[3,384,1024]{2,1,0:T(8,128)(2,1)}, bf16[3,384,1024]{2,1,0:T(8,128)(2,1)}, u32[]{:S(2)}, u32[]{:S(2)}) collective-permute-start(bf16[3,384,1024]{2,1,0:T(8,128)(2,1)} %pad_maximum_fusion.1), channel_id=1, source_target_pairs={{0,192},{64,0},{128,64},{192,128},{1,193},{65,1},{129,65},{193,129... | collective-permute-start | bytes 7077896 | tf_op jit(solution)/shard_map/ppermute | solution.py:20
  249.8 32.7 %collective-permute-start.5 = (bf16[3,384,1024]{2,1,0:T(8,128)(2,1)S(1)}, bf16[3,384,1024]{2,1,0:T(8,128)(2,1)S(1)}, u32[]{:S(2)}, u32[]{:S(2)}) collective-permute-start(bf16[3,384,1024]{2,1,0:T(8,128)(2,1)S(1)} %bitcast.41), channel_id=1, source_target_pairs={{0,192},{64,0},{128,64},{192,128},{1,193},{65,1},{129,65},{193,129... | collective-permute-start | bytes 7077896 | tf_op jit(solution)/shard_map/ppermute | solution.py:20

commit v10 on v9

--- a/solution.py
+++ b/solution.py
@@ -196,10 +196,8 @@
     )
     row_grads = jnp.concatenate([dq_row[None], d_total], axis=0)
     row_handed = shifted(row_grads, "pipe", -1)
-    returned = lax.all_to_all(
-        col_grads, "seq", split_axis=1, concat_axis=3, tiled=True
-    ).reshape(3, tokens, COLS)
-    col_handed = shifted(returned, "pipe", -1)
+    returned = lax.all_to_all(col_grads, "seq", split_axis=1, concat_axis=3, tiled=True)
+    col_handed = shifted(returned, "pipe", -1).reshape(3, tokens, COLS)
 
     handed = jnp.concatenate([row_handed, col_handed], axis=2)
     return (handed[0][None], handed[1][None], handed[2][None])

time: 287 us -> 288 us (level)
  local copies, waits for them, and re-layouts: 22.1 us -> 17.7 us
  other arithmetic: 15.2 us -> 18.7 us
    concatenate x0 -> x1, other arithmetic: none -> 3.48 us  [body(): handed = jnp.concatenate([row_handed, col_handed], axis=2)]
  transfers between devices with their start and end apart: 8 -> 8, of which waited for: 6 -> 6; matrix products, arithmetic and copies ran while one was open for 11% -> 10% of each run, Pallas kernels for 12% -> 12%
where the time goes in v10:
time: 288 us; the launch traced here: 286 us
  waiting for transfers between devices  173 us (60%)
  starting transfers between devices  41.3 us (14%)
  Pallas kernels  35 us (12%)
  other arithmetic  18.7 us (6%)
  local copies, waits for them, and re-layouts  17.7 us (6%)
    ppermute x6, waiting for transfers between devices, shifted(): return lax.ppermute(value, axis, pairs)  68.1 us
    all_to_all x1, waiting for transfers between devices, body(): lax.all_to_all(col_grads, 'seq', split_axis=1, concat_axis=3, tiled=True)  59.3 us
    all_to_all x1, waiting for transfers between devices, body(): lax.all_to_all(sent, 'seq', split_axis=2, concat_axis=1, tiled=True)  45.1 us
    ppermute x6, starting transfers between devices, shifted(): return lax.ppermute(value, axis, pairs)  26.4 us
    pallas_call x1, Pallas kernels, row_side(): pl.pallas_call(row_kernel, grid=(HEADS_ROW,), in_specs=[plain, plain, sta...  24.3 us
    pallas_call x1, Pallas kernels, col_side(): pl.pallas_call(col_kernel, grid=(HEADS_COL,), in_specs=[part_block(0), pa...  10.7 us
    all_to_all x1, starting transfers between devices, body(): lax.all_to_all(sent, 'seq', split_axis=2, concat_axis=1, tiled=True)  9.46 us
    another operation x1, other arithmetic, body(): jnp.stack([item[:, row_width:] for item in (query_now, key_now, value_now...  8.39 us
  transfers between devices with their start and end apart: 8, of which 6 were waited for; matrix products, arithmetic and copies ran while one was open for 10% of the time, Pallas kernels for 12%

profile of v10, /device:TPU:1, one launch (start us, length us, event | category | flops | bytes accessed | tf_op | source)
XLA Modules:
  0.0 286.1 jit_solution(6833611017250141914)
XLA Ops:
  0.6 2.2 slice_bitcast_fusion
  3.0 2.1 collective-permute-start
  5.1 9.3 %collective-permute-start.1 = (bf16[2,384,1024]{2,1,0:T(8,128)(2,1)S(1)}, bf16[2,384,1024]{2,1,0:T(8,128)(2,1)}, u32[]{:S(2)}, u32[]{:S(2)}) collective-permute-start(bf16[2,384,1024]{2,1,0:T(8,128)(2,1)S(1)} %pad_maximum_fusion.3), channel_id=1, source_target_pairs={{0,63},{1,0},{2,1},{3,2},{4,3},{5,4},{6,5},{7,6},{8,7},{9,8},{10,9... | collective-permute-start | bytes 4718600 | tf_op jit(solution)/shard_map/ppermute | solution.py:20
  14.5 1.2 copy.36
  15.7 1.2 copy.35
  16.9 1.2 copy.34
  18.2 1.2 copy.33
  19.4 8.4 %pad_maximum_fusion = bf16[4,6,64,1024]{3,0,1,2:T(4,128)(2,1)} fusion(bf16[1,6,64,1024]{3,0,1,2:T(2,128)(2,1)S(1)} %copy.36, bf16[1,6,64,1024]{3,0,1,2:T(2,128)(2,1)S(1)} %copy.35, bf16[1,6,64,1024]{3,0,1,2:T(2,128)(2,1)S(1)} %copy.34, bf16[1,6,64,1024]{3,0,1,2:T(2,128)(2,1)S(1)} %copy.33), kind=kLoop, calls=%fused_computation.4 | loop fusion | flops 12582912 | bytes 6291456 | tf_op jit(solution)/shard_map/stack | solution.py:158
  27.8 20.7 %collective-permute-done.kp_ref.vp_ref = bf16[2,384,1024]{2,1,0:T(8,128)(2,1)} collective-permute-done((bf16[2,384,1024]{2,1,0:T(8,128)(2,1)S(1)}, bf16[2,384,1024]{2,1,0:T(8,128)(2,1)}, u32[]{:S(2)}, u32[]{:S(2)}) %collective-permute-start) | collective-permute-done | bytes 1572896 | tf_op jit(solution)/shard_map/ppermute | solution.py:20
  48.5 9.5 %all-to-all-start = ((bf16[4,6,64,1024]{3,0,1,2:T(4,128)(2,1)}), bf16[4,6,64,1024]{3,0,1,2:T(4,128)(2,1)S(1)}, u32[]{:S(2)}, u32[]{:S(2)}) async-start(bf16[4,6,64,1024]{3,0,1,2:T(4,128)(2,1)} %pad_maximum_fusion), calls=%async_computation | async-start | bytes 6291456 | tf_op jit(solution)/shard_map/all_to_all | solution.py:162
  58.3 0.6 copy.46
  58.9 24.3 %shard_map.85 = (bf16[384,1024]{1,0:T(8,128)(2,1)}, bf16[2,384,1024]{2,1,0:T(8,128)(2,1)}, f32[2,384,1024]{2,1,0:T(8,128)}, bf16[2,384,1024]{2,1,0:T(8,128)(2,1)}) custom-call(bf16[384,2048]{1,0:T(8,128)(2,1)} %bitcast.37, bf16[384,2048]{1,0:T(8,128)(2,1)} %bitcast.35, bf16[2,384,1024]{2,1,0:T(8,128)(2,1)} %collective-permute-done.kp_ref.vp_ref, ...), custom_call_target="tpu_custom_call" | custom-call | tf_op jit(solution)/shard_map/pallas_call | solution.py:97
  83.2 45.1 %all-to-all-done = bf16[4,6,64,1024]{3,0,1,2:T(4,128)(2,1)S(1)} async-done(((bf16[4,6,64,1024]{3,0,1,2:T(4,128)(2,1)}), bf16[4,6,64,1024]{3,0,1,2:T(4,128)(2,1)S(1)}, u32[]{:S(2)}, u32[]{:S(2)}) %all-to-all-start) | async-done | bytes 3145760 | tf_op jit(solution)/shard_map/all_to_all | solution.py:162
  128.3 5.4 %collective-permute-start.2 = (bf16[2,384,1024]{2,1,0:T(8,128)(2,1)}, bf16[2,384,1024]{2,1,0:T(8,128)(2,1)}, u32[]{:S(2)}, u32[]{:S(2)}) collective-permute-start(bf16[2,384,1024]{2,1,0:T(8,128)(2,1)} %get-tuple-element.28), channel_id=1, source_target_pairs={{0,63},{1,0},{2,1},{3,2},{4,3},{5,4},{6,5},{7,6},{8,7},{9,8},{10,9... | collective-permute-start | bytes 4718600 | tf_op jit(solution)/shard_map/ppermute | solution.py:20
  133.8 0.2 slice_reduce_fusion.2
  134.0 0.2 compare_reduce_fusion
  134.2 0.9 convert_element_type.43.keep_ref
  135.1 2.7 copy.38.q_ref.k_ref.v_ref.do_ref
  137.8 10.7 %shard_map.86 = bf16[3,384,1024]{2,1,0:T(8,128)(2,1)} custom-call(bf16[4,384,1024]{2,1,0:T(8,128)(2,1)} %copy.38.q_ref.k_ref.v_ref.do_ref, bf16[4,384,1024]{2,1,0:T(8,128)(2,1)} %copy.38.q_ref.k_ref.v_ref.do_ref, bf16[4,384,1024]{2,1,0:T(8,128)(2,1)} %copy.38.q_ref.k_ref.v_ref.do_ref, bf16[4,384,1024]{2,1,0:T(8,128)(2,1)} %copy.38.q_ref.k_ref.v_ref.do_ref, ...), custom_call_target="tpu_custom_call" | custom-call | tf_op jit(solution)/shard_map/pallas_call | solution.py:130
  148.5 3.6 %reshape.245 = bf16[3,64,6,1,1024]{4,2,1,0,3:T(8,128)(2,1)S(1)} reshape(bf16[3,384,1024]{2,1,0:T(8,128)(2,1)} %shard_map.86) | data formatting | bytes 4718592 | tf_op jit(solution)/shard_map/reshape | solution.py:191
  152.1 13.0 %collective-permute-done.2 = bf16[2,384,1024]{2,1,0:T(8,128)(2,1)} collective-permute-done((bf16[2,384,1024]{2,1,0:T(8,128)(2,1)}, bf16[2,384,1024]{2,1,0:T(8,128)(2,1)}, u32[]{:S(2)}, u32[]{:S(2)}) %collective-permute-start.2) | collective-permute-done | bytes 1572896 | tf_op jit(solution)/shard_map/ppermute | solution.py:20
  165.1 7.6 %collective-permute-done.3 = bf16[2,384,1024]{2,1,0:T(8,128)(2,1)} collective-permute-done((bf16[2,384,1024]{2,1,0:T(8,128)(2,1)}, bf16[2,384,1024]{2,1,0:T(8,128)(2,1)}, u32[]{:S(2)}, u32[]{:S(2)}) %collective-permute-start.3) | collective-permute-done | bytes 1572896 | tf_op jit(solution)/shard_map/ppermute | solution.py:20
  172.7 2.0 copy.42
  174.7 5.4 %all-to-all-start.1 = ((bf16[3,64,6,1,1024]{4,2,0,3,1:T(8,128)(2,1)}), bf16[3,64,6,1,1024]{4,2,0,3,1:T(8,128)(2,1)S(1)}, u32[]{:S(2)}, u32[]{:S(2)}) async-start(bf16[3,64,6,1,1024]{4,2,0,3,1:T(8,128)(2,1)} %copy.42), calls=%async_computation.1 | async-start | bytes 6291456 | tf_op jit(solution)/shard_map/all_to_all | solution.py:199
  180.1 3.7 %add_convert_fusion = bf16[2,384,1024]{2,1,0:T(8,128)(2,1)S(1)} fusion(bf16[2,384,1024]{2,1,0:T(8,128)(2,1)} %collective-permute-done.2, f32[2,384,1024]{2,1,0:T(8,128)} %get-tuple-element.26, bf16[2,384,1024]{2,1,0:T(8,128)(2,1)} %collective-permute-done.3), kind=kLoop, calls=%fused_computation.5 | loop fusion | flops 3932160 | bytes 7864320 | tf_op jit(solution)/shard_map/convert_element_type | solution.py:194
  183.8 1.6 pad_maximum_fusion.1
  185.5 3.8 %collective-permute-start.4 = (bf16[3,384,1024]{2,1,0:T(8,128)(2,1)}, bf16[3,384,1024]{2,1,0:T(8,128)(2,1)}, u32[]{:S(2)}, u32[]{:S(2)}) collective-permute-start(bf16[3,384,1024]{2,1,0:T(8,128)(2,1)} %pad_maximum_fusion.1), channel_id=1, source_target_pairs={{0,192},{64,0},{128,64},{192,128},{1,193},{65,1},{129,65},{193,129... | collective-permute-start | bytes 7077896 | tf_op jit(solution)/shard_map/ppermute | solution.py:20
  189.2 59.3 %all-to-all-done.1 = bf16[3,64,6,1,1024]{4,2,0,3,1:T(8,128)(2,1)S(1)} async-done(((bf16[3,64,6,1,1024]{4,2,0,3,1:T(8,128)(2,1)}), bf16[3,64,6,1,1024]{4,2,0,3,1:T(8,128)(2,1)S(1)}, u32[]{:S(2)}, u32[]{:S(2)}) %all-to-all-start.1) | async-done | bytes 2359328 | tf_op jit(solution)/shard_map/all_to_all | solution.py:199
  248.5 1.3 copy.43
  249.8 5.9 %collective-permute-start.5 = (bf16[3,1,6,64,1024]{4,3,2,1,0:T(8,128)(2,1)S(1)}, bf16[3,1,6,64,1024]{4,3,2,1,0:T(8,128)(2,1)S(1)}, u32[]{:S(2)}, u32[]{:S(2)}) collective-permute-start(bf16[3,1,6,64,1024]{4,3,2,1,0:T(8,128)(2,1)S(1)} %copy.43), channel_id=1, source_target_pairs={{0,192},{64,0},{128,64},{192,128},{1,193},{65,1},{129,65},{193,129... | collective-permute-start | bytes 7077896 | tf_op jit(solution)/shard_map/ppermute | solution.py:20
  255.8 26.8 %collective-permute-done.5 = bf16[3,1,6,64,1024]{4,3,2,1,0:T(8,128)(2,1)S(1)} collective-permute-done((bf16[3,1,6,64,1024]{4,3,2,1,0:T(8,128)(2,1)S(1)}, bf16[3,1,6,64,1024]{4,3,2,1,0:T(8,128)(2,1)S(1)}, u32[]{:S(2)}, u32[]{:S(2)}) %collective-permute-start.5) | collective-permute-done | bytes 2359328 | tf_op jit(solution)/shard_map/ppermute | solution.py:20
  282.6 3.5 %pad_maximum_fusion.2 = (bf16[1,384,2048]{2,1,0:T(8,128)(2,1)}, bf16[1,384,2048]{2,1,0:T(8,128)(2,1)}, bf16[1,384,2048]{2,1,0:T(8,128)(2,1)}) fusion(bf16[3,384,1024]{2,1,0:T(8,128)(2,1)S(1)} %bitcast.43, bf16[3,384,1024]{2,1,0:T(8,128)(2,1)} %collective-permute-done.4), kind=kLoop, calls=%fused_computation.9 | loop fusion | flops 9437184 | bytes 9437184 | tf_op jit(solution)/shard_map/concatenate | solution.py:202
  (28 shorter events, 0.8 us)
Async XLA Ops:
  2.8 11.6 %copy-start = (bf16[1,384,2048]{2,1,0:T(8,128)(2,1)S(1)}, bf16[1,384,2048]{2,1,0:T(8,128)(2,1)}, u32[]{:S(2)}) copy-start(bf16[1,384,2048]{2,1,0:T(8,128)(2,1)} %param.9) | copy-start | bytes 4718596
  3.0 45.5 %collective-permute-start = (bf16[2,384,1024]{2,1,0:T(8,128)(2,1)S(1)}, bf16[2,384,1024]{2,1,0:T(8,128)(2,1)}, u32[]{:S(2)}, u32[]{:S(2)}) collective-permute-start(bf16[2,384,1024]{2,1,0:T(8,128)(2,1)S(1)} %pad_maximum_fusion.3), channel_id=1, source_target_pairs={{0,1},{1,2},{2,3},{3,4},{4,5},{5,6},{6,7},{7,8},{8,9},{9,10},{10,1... | collective-permute-start | bytes 4718600 | tf_op jit(solution)/shard_map/ppermute | solution.py:20
  5.1 43.4 %collective-permute-start.1 = (bf16[2,384,1024]{2,1,0:T(8,128)(2,1)S(1)}, bf16[2,384,1024]{2,1,0:T(8,128)(2,1)}, u32[]{:S(2)}, u32[]{:S(2)}) collective-permute-start(bf16[2,384,1024]{2,1,0:T(8,128)(2,1)S(1)} %pad_maximum_fusion.3), channel_id=1, source_target_pairs={{0,63},{1,0},{2,1},{3,2},{4,3},{5,4},{6,5},{7,6},{8,7},{9,8},{10,9... | collective-permute-start | bytes 4718600 | tf_op jit(solution)/shard_map/ppermute | solution.py:20
  15.7 2.5 copy-start.1
  27.8 30.1 %copy-start.3 = (s32[3,5]{1,0:T(4,128)S(1)}, s32[3,5]{1,0:T(4,128)}, u32[]{:S(2)}) copy-start(s32[3,5]{1,0:T(4,128)} %param.10) | copy-start | bytes 184
  48.5 79.8 %all-to-all-start = ((bf16[4,6,64,1024]{3,0,1,2:T(4,128)(2,1)}), bf16[4,6,64,1024]{3,0,1,2:T(4,128)(2,1)S(1)}, u32[]{:S(2)}, u32[]{:S(2)}) async-start(bf16[4,6,64,1024]{3,0,1,2:T(4,128)(2,1)} %pad_maximum_fusion), calls=%async_computation | async-start | bytes 6291456 | tf_op jit(solution)/shard_map/all_to_all | solution.py:162
  58.9 74.8 %copy-start.4 = (s32[3,2]{0,1:T(2,128)S(1)}, s32[3,2]{0,1:T(2,128)}, u32[]{:S(2)}) copy-start(s32[3,2]{0,1:T(2,128)} %param.11) | copy-start | bytes 76
  128.3 36.7 %collective-permute-start.2 = (bf16[2,384,1024]{2,1,0:T(8,128)(2,1)}, bf16[2,384,1024]{2,1,0:T(8,128)(2,1)}, u32[]{:S(2)}, u32[]{:S(2)}) collective-permute-start(bf16[2,384,1024]{2,1,0:T(8,128)(2,1)} %get-tuple-element.28), channel_id=1, source_target_pairs={{0,63},{1,0},{2,1},{3,2},{4,3},{5,4},{6,5},{7,6},{8,7},{9,8},{10,9... | collective-permute-start | bytes 4718600 | tf_op jit(solution)/shard_map/ppermute | solution.py:20
  133.7 39.0 %collective-permute-start.3 = (bf16[2,384,1024]{2,1,0:T(8,128)(2,1)}, bf16[2,384,1024]{2,1,0:T(8,128)(2,1)}, u32[]{:S(2)}, u32[]{:S(2)}) collective-permute-start(bf16[2,384,1024]{2,1,0:T(8,128)(2,1)} %get-tuple-element.29), channel_id=1, source_target_pairs={{0,1},{1,2},{2,3},{3,4},{4,5},{5,6},{6,7},{7,8},{8,9},{9,10},{10,1... | collective-permute-start | bytes 4718600 | tf_op jit(solution)/shard_map/ppermute | solution.py:20
  174.7 73.8 %all-to-all-start.1 = ((bf16[3,64,6,1,1024]{4,2,0,3,1:T(8,128)(2,1)}), bf16[3,64,6,1,1024]{4,2,0,3,1:T(8,128)(2,1)S(1)}, u32[]{:S(2)}, u32[]{:S(2)}) async-start(bf16[3,64,6,1,1024]{4,2,0,3,1:T(8,128)(2,1)} %copy.42), calls=%async_computation.1 | async-start | bytes 6291456 | tf_op jit(solution)/shard_map/all_to_all | solution.py:199
  180.1 3.8 %copy-start.2 = (bf16[384,1024]{1,0:T(8,128)(2,1)S(1)}, bf16[384,1024]{1,0:T(8,128)(2,1)}, u32[]{:S(2)}) copy-start(bf16[384,1024]{1,0:T(8,128)(2,1)} %get-tuple-element.25) | copy-start | bytes 2359300
  185.5 70.3 %collective-permute-start.4 = (bf16[3,384,1024]{2,1,0:T(8,128)(2,1)}, bf16[3,384,1024]{2,1,0:T(8,128)(2,1)}, u32[]{:S(2)}, u32[]{:S(2)}) collective-permute-start(bf16[3,384,1024]{2,1,0:T(8,128)(2,1)} %pad_maximum_fusion.1), channel_id=1, source_target_pairs={{0,192},{64,0},{128,64},{192,128},{1,193},{65,1},{129,65},{193,129... | collective-permute-start | bytes 7077896 | tf_op jit(solution)/shard_map/ppermute | solution.py:20
  249.8 32.7 %collective-permute-start.5 = (bf16[3,1,6,64,1024]{4,3,2,1,0:T(8,128)(2,1)S(1)}, bf16[3,1,6,64,1024]{4,3,2,1,0:T(8,128)(2,1)S(1)}, u32[]{:S(2)}, u32[]{:S(2)}) collective-permute-start(bf16[3,1,6,64,1024]{4,3,2,1,0:T(8,128)(2,1)S(1)} %copy.43), channel_id=1, source_target_pairs={{0,192},{64,0},{128,64},{192,128},{1,193},{65,1},{129,65},{193,129... | collective-permute-start | bytes 7077896 | tf_op jit(solution)/shard_map/ppermute | solution.py:20

commit v11 on v10

--- a/solution.py
+++ b/solution.py
@@ -189,15 +189,26 @@
     )
     col_keep = jnp.any(listed[:, :, None] == col_block[None, None, :], axis=1).astype(jnp.float32)
     col_grads = col_side(received, col_keep).reshape(3, devices, share, 1, COLS)
-
-    col_grads, from_after, from_before = lax.optimization_barrier((col_grads, from_after, from_before))
+    half = COLS // 2
+    early, late = col_grads[..., :half], col_grads[..., half:]
+
+    early, late, from_after, from_before = lax.optimization_barrier(
+        (early, late, from_after, from_before)
+    )
     d_total = (d_own + from_before.astype(jnp.float32) + from_after.astype(jnp.float32)).astype(
         jnp.bfloat16
     )
     row_grads = jnp.concatenate([dq_row[None], d_total], axis=0)
     row_handed = shifted(row_grads, "pipe", -1)
-    returned = lax.all_to_all(col_grads, "seq", split_axis=1, concat_axis=3, tiled=True)
-    col_handed = shifted(returned, "pipe", -1).reshape(3, tokens, COLS)
+    early = shifted(early, "pipe", -1)
+    late = lax.all_to_all(late, "seq", split_axis=1, concat_axis=3, tiled=True)
+
+    early, late = lax.optimization_barrier((early, late))
+    early = lax.all_to_all(early, "seq", split_axis=1, concat_axis=3, tiled=True)
+    late = shifted(late, "pipe", -1)
+    col_handed = jnp.concatenate(
+        [early.reshape(3, tokens, half), late.reshape(3, tokens, half)], axis=2
+    )
 
     handed = jnp.concatenate([row_handed, col_handed], axis=2)
     return (handed[0][None], handed[1][None], handed[2][None])

time: 288 us -> 272 us (0.944)
  waiting for transfers between devices: 173 us -> 148 us
  starting transfers between devices: 41.3 us -> 47.4 us
  local copies, waits for them, and re-layouts: 17.7 us -> 23.4 us
    all_to_all x1 -> x2, waiting for transfers between devices: 59.3 us -> 37 us  [the longest x1 30.3 us: body(): lax.all_to_all(early, 'seq', split_axis=1, concat_axis=3, tiled=True)]
    all_to_all x1 -> x2, starting transfers between devices: 5.36 us -> 13.2 us  [the longest x1 7.68 us: body(): lax.all_to_all(early, 'seq', split_axis=1, concat_axis=3, tiled=True)]
    slice x0 -> x2, local copies, waits for them, and re-layouts: none -> 3.7 us  [the longest x1 2.36 us: body(): return (handed[0][None], handed[1][None], handed[2][None])]
    ppermute x6 -> x7, waiting for transfers between devices: 68.1 us -> 65.5 us  [shifted(): return lax.ppermute(value, axis, pairs)]
    ppermute x6 -> x7, starting transfers between devices: 26.4 us -> 24.8 us  [shifted(): return lax.ppermute(value, axis, pairs)]
  transfers between devices with their start and end apart: 8 -> 10, of which waited for: 6 -> 8; matrix products, arithmetic and copies ran while one was open for 10% -> 12% of each run, Pallas kernels for 12% -> 13%
where the time goes in v11:
time: 272 us
  waiting for transfers between devices  148 us (54%)
  starting transfers between devices  47.4 us (17%)
  Pallas kernels  35 us (13%)
  local copies, waits for them, and re-layouts  23.4 us (9%)
  other arithmetic  17.2 us (6%)
    ppermute x7, waiting for transfers between devices, shifted(): return lax.ppermute(value, axis, pairs)  65.5 us
    all_to_all x1, waiting for transfers between devices, body(): lax.all_to_all(sent, 'seq', split_axis=2, concat_axis=1, tiled=True)  45.1 us
    all_to_all x1, waiting for transfers between devices, body(): lax.all_to_all(early, 'seq', split_axis=1, concat_axis=3, tiled=True)  30.3 us
    ppermute x7, starting transfers between devices, shifted(): return lax.ppermute(value, axis, pairs)  24.8 us
    pallas_call x1, Pallas kernels, row_side(): pl.pallas_call(row_kernel, grid=(HEADS_ROW,), in_specs=[plain, plain, sta...  24.3 us
    pallas_call x1, Pallas kernels, col_side(): pl.pallas_call(col_kernel, grid=(HEADS_COL,), in_specs=[part_block(0), pa...  10.7 us
    all_to_all x1, starting transfers between devices, body(): lax.all_to_all(sent, 'seq', split_axis=2, concat_axis=1, tiled=True)  9.46 us
    another operation x1, other arithmetic, body(): jnp.stack([item[:, row_width:] for item in (query_now, key_now, value_now...  8.48 us
  transfers between devices with their start and end apart: 10, of which 8 were waited for; matrix products, arithmetic and copies ran while one was open for 12% of the time, Pallas kernels for 13%

profile of v11, /device:TPU:1, one launch (start us, length us, event | category | flops | bytes accessed | tf_op | source)
XLA Modules:
  0.0 271.6 jit_solution(11794322198396309953)
XLA Ops:
  0.6 2.2 slice_bitcast_fusion
  3.0 2.1 collective-permute-start
  5.1 9.3 %collective-permute-start.1 = (bf16[2,384,1024]{2,1,0:T(8,128)(2,1)S(1)}, bf16[2,384,1024]{2,1,0:T(8,128)(2,1)}, u32[]{:S(2)}, u32[]{:S(2)}) collective-permute-start(bf16[2,384,1024]{2,1,0:T(8,128)(2,1)S(1)} %pad_maximum_fusion.3), channel_id=1, source_target_pairs={{0,63},{1,0},{2,1},{3,2},{4,3},{5,4},{6,5},{7,6},{8,7},{9,8},{10,9... | collective-permute-start | bytes 4718600 | tf_op jit(solution)/shard_map/ppermute | solution.py:20
  15.7 1.2 copy.40
  18.4 1.2 copy.38
  19.6 8.5 %pad_maximum_fusion.1 = bf16[4,6,64,1024]{3,0,1,2:T(4,128)(2,1)} fusion(bf16[1,6,64,1024]{3,0,1,2:T(2,128)(2,1)S(1)} %copy.41, bf16[1,6,64,1024]{3,0,1,2:T(2,128)(2,1)S(1)} %copy.40, bf16[1,6,64,1024]{3,0,1,2:T(2,128)(2,1)S(1)} %copy.39, bf16[1,6,64,1024]{3,0,1,2:T(2,128)(2,1)S(1)} %copy.38), kind=kLoop, calls=%fused_computation.1 | loop fusion | flops 12582912 | bytes 6291456 | tf_op jit(solution)/shard_map/stack | solution.py:158
  28.1 20.4 %collective-permute-done.kp_ref.vp_ref = bf16[2,384,1024]{2,1,0:T(8,128)(2,1)} collective-permute-done((bf16[2,384,1024]{2,1,0:T(8,128)(2,1)S(1)}, bf16[2,384,1024]{2,1,0:T(8,128)(2,1)}, u32[]{:S(2)}, u32[]{:S(2)}) %collective-permute-start) | collective-permute-done | bytes 1572896 | tf_op jit(solution)/shard_map/ppermute | solution.py:20
  48.5 9.5 %all-to-all-start = ((bf16[4,6,64,1024]{3,0,1,2:T(4,128)(2,1)}), bf16[4,6,64,1024]{3,0,1,2:T(4,128)(2,1)S(1)}, u32[]{:S(2)}, u32[]{:S(2)}) async-start(bf16[4,6,64,1024]{3,0,1,2:T(4,128)(2,1)} %pad_maximum_fusion.1), calls=%async_computation | async-start | bytes 6291456 | tf_op jit(solution)/shard_map/all_to_all | solution.py:162
  58.9 24.3 %shard_map.85 = (bf16[384,1024]{1,0:T(8,128)(2,1)}, bf16[2,384,1024]{2,1,0:T(8,128)(2,1)}, f32[2,384,1024]{2,1,0:T(8,128)}, bf16[2,384,1024]{2,1,0:T(8,128)(2,1)}) custom-call(bf16[384,2048]{1,0:T(8,128)(2,1)} %bitcast.43, bf16[384,2048]{1,0:T(8,128)(2,1)} %bitcast.41, bf16[2,384,1024]{2,1,0:T(8,128)(2,1)} %collective-permute-done.kp_ref.vp_ref, ...), custom_call_target="tpu_custom_call" | custom-call | tf_op jit(solution)/shard_map/pallas_call | solution.py:97
  83.2 45.1 %all-to-all-done = bf16[4,6,64,1024]{3,0,1,2:T(4,128)(2,1)S(1)} async-done(((bf16[4,6,64,1024]{3,0,1,2:T(4,128)(2,1)}), bf16[4,6,64,1024]{3,0,1,2:T(4,128)(2,1)S(1)}, u32[]{:S(2)}, u32[]{:S(2)}) %all-to-all-start) | async-done | bytes 3145760 | tf_op jit(solution)/shard_map/all_to_all | solution.py:162
  128.3 5.4 %collective-permute-start.2 = (bf16[2,384,1024]{2,1,0:T(8,128)(2,1)}, bf16[2,384,1024]{2,1,0:T(8,128)(2,1)}, u32[]{:S(2)}, u32[]{:S(2)}) collective-permute-start(bf16[2,384,1024]{2,1,0:T(8,128)(2,1)} %get-tuple-element.31), channel_id=1, source_target_pairs={{0,63},{1,0},{2,1},{3,2},{4,3},{5,4},{6,5},{7,6},{8,7},{9,8},{10,9... | collective-permute-start | bytes 4718600 | tf_op jit(solution)/shard_map/ppermute | solution.py:20
  135.1 2.7 copy.43.q_ref.k_ref.v_ref.do_ref
  137.7 10.7 %shard_map.86 = bf16[3,384,1024]{2,1,0:T(8,128)(2,1)} custom-call(bf16[4,384,1024]{2,1,0:T(8,128)(2,1)} %copy.43.q_ref.k_ref.v_ref.do_ref, bf16[4,384,1024]{2,1,0:T(8,128)(2,1)} %copy.43.q_ref.k_ref.v_ref.do_ref, bf16[4,384,1024]{2,1,0:T(8,128)(2,1)} %copy.43.q_ref.k_ref.v_ref.do_ref, bf16[4,384,1024]{2,1,0:T(8,128)(2,1)} %copy.43.q_ref.k_ref.v_ref.do_ref, ...), custom_call_target="tpu_custom_call" | custom-call | tf_op jit(solution)/shard_map/pallas_call | solution.py:130
  148.5 3.6 %reshape.249 = bf16[3,64,6,1,1024]{4,2,1,0,3:T(8,128)(2,1)S(1)} reshape(bf16[3,384,1024]{2,1,0:T(8,128)(2,1)} %shard_map.86) | data formatting | bytes 4718592 | tf_op jit(solution)/shard_map/reshape | solution.py:191
  152.1 1.3 fusion.15
  153.4 11.6 %collective-permute-done.2 = bf16[2,384,1024]{2,1,0:T(8,128)(2,1)} collective-permute-done((bf16[2,384,1024]{2,1,0:T(8,128)(2,1)}, bf16[2,384,1024]{2,1,0:T(8,128)(2,1)}, u32[]{:S(2)}, u32[]{:S(2)}) %collective-permute-start.2) | collective-permute-done | bytes 1572896 | tf_op jit(solution)/shard_map/ppermute | solution.py:20
  165.0 7.6 %collective-permute-done.3 = bf16[2,384,1024]{2,1,0:T(8,128)(2,1)} collective-permute-done((bf16[2,384,1024]{2,1,0:T(8,128)(2,1)}, bf16[2,384,1024]{2,1,0:T(8,128)(2,1)}, u32[]{:S(2)}, u32[]{:S(2)}) %collective-permute-start.3) | collective-permute-done | bytes 1572896 | tf_op jit(solution)/shard_map/ppermute | solution.py:20
  172.7 1.2 copy.48
  173.9 5.5 %all-to-all-start.1 = ((bf16[3,64,6,1,512]{4,2,0,3,1:T(8,128)(2,1)}), bf16[3,64,6,1,512]{4,2,0,3,1:T(8,128)(2,1)S(1)}, u32[]{:S(2)}, u32[]{:S(2)}) async-start(bf16[3,64,6,1,512]{4,2,0,3,1:T(8,128)(2,1)} %copy.48), calls=%async_computation.1 | async-start | bytes 3145728 | tf_op jit(solution)/shard_map/all_to_all | solution.py:204
  179.8 3.9 %collective-permute-start.5 = (bf16[3,64,6,1,512]{4,1,3,2,0:T(8,128)(2,1)S(1)}, bf16[3,64,6,1,512]{4,1,3,2,0:T(8,128)(2,1)S(1)}, u32[]{:S(2)}, u32[]{:S(2)}) collective-permute-start(bf16[3,64,6,1,512]{4,1,3,2,0:T(8,128)(2,1)S(1)} %copy.47), channel_id=1, source_target_pairs={{0,192},{64,0},{128,64},{192,128},{1,193},{65,1},{129,65},{193,129... | collective-permute-start | bytes 3538952 | tf_op jit(solution)/shard_map/ppermute | solution.py:20
  183.7 3.7 %add_convert_fusion = bf16[2,384,1024]{2,1,0:T(8,128)(2,1)S(1)} fusion(bf16[2,384,1024]{2,1,0:T(8,128)(2,1)} %collective-permute-done.2, f32[2,384,1024]{2,1,0:T(8,128)} %get-tuple-element.29, bf16[2,384,1024]{2,1,0:T(8,128)(2,1)} %collective-permute-done.3), kind=kLoop, calls=%fused_computation.2 | loop fusion | flops 3932160 | bytes 7864320 | tf_op jit(solution)/shard_map/convert_element_type | solution.py:198
  187.4 1.6 pad_maximum_fusion.2
  189.1 20.3 %collective-permute-done.5 = bf16[3,64,6,1,512]{4,1,3,2,0:T(8,128)(2,1)S(1)} collective-permute-done((bf16[3,64,6,1,512]{4,1,3,2,0:T(8,128)(2,1)S(1)}, bf16[3,64,6,1,512]{4,1,3,2,0:T(8,128)(2,1)S(1)}, u32[]{:S(2)}, u32[]{:S(2)}) %collective-permute-start.5) | collective-permute-done | bytes 1179680 | tf_op jit(solution)/shard_map/ppermute | solution.py:20
  209.4 6.7 %all-to-all-done.1 = bf16[3,64,6,1,512]{4,2,0,3,1:T(8,128)(2,1)S(1)} async-done(((bf16[3,64,6,1,512]{4,2,0,3,1:T(8,128)(2,1)}), bf16[3,64,6,1,512]{4,2,0,3,1:T(8,128)(2,1)S(1)}, u32[]{:S(2)}, u32[]{:S(2)}) %all-to-all-start.1) | async-done | bytes 1179680 | tf_op jit(solution)/shard_map/all_to_all | solution.py:204
  216.1 1.8 copy.49
  217.9 7.7 %all-to-all-start.2 = ((bf16[3,64,6,1,512]{4,2,0,3,1:T(8,128)(2,1)}), bf16[3,64,6,1,512]{4,2,0,3,1:T(8,128)(2,1)S(1)}, u32[]{:S(2)}, u32[]{:S(2)}) async-start(bf16[3,64,6,1,512]{4,2,0,3,1:T(8,128)(2,1)} %copy.49), calls=%async_computation.2 | async-start | bytes 3145728 | tf_op jit(solution)/shard_map/all_to_all | solution.py:207
  225.6 1.4 copy.51
  227.0 4.1 %collective-permute-start.6 = (bf16[3,1,6,64,512]{4,3,2,1,0:T(8,128)(2,1)}, bf16[3,1,6,64,512]{4,3,2,1,0:T(8,128)(2,1)S(1)}, u32[]{:S(2)}, u32[]{:S(2)}) collective-permute-start(bf16[3,1,6,64,512]{4,3,2,1,0:T(8,128)(2,1)} %copy.51), channel_id=1, source_target_pairs={{0,192},{64,0},{128,64},{192,128},{1,193},{65,1},{129,65},{193,129... | collective-permute-start | bytes 3538952 | tf_op jit(solution)/shard_map/ppermute | solution.py:20
  231.1 30.3 %all-to-all-done.2 = bf16[3,64,6,1,512]{4,2,0,3,1:T(8,128)(2,1)S(1)} async-done(((bf16[3,64,6,1,512]{4,2,0,3,1:T(8,128)(2,1)}), bf16[3,64,6,1,512]{4,2,0,3,1:T(8,128)(2,1)S(1)}, u32[]{:S(2)}, u32[]{:S(2)}) %all-to-all-start.2) | async-done | bytes 1179680 | tf_op jit(solution)/shard_map/all_to_all | solution.py:207
  261.8 5.5 %collective-permute-done.6 = bf16[3,1,6,64,512]{4,3,2,1,0:T(8,128)(2,1)S(1)} collective-permute-done((bf16[3,1,6,64,512]{4,3,2,1,0:T(8,128)(2,1)}, bf16[3,1,6,64,512]{4,3,2,1,0:T(8,128)(2,1)S(1)}, u32[]{:S(2)}, u32[]{:S(2)}) %collective-permute-start.6) | collective-permute-done | bytes 1179680 | tf_op jit(solution)/shard_map/ppermute | solution.py:20
  267.3 1.9 pad_maximum_fusion
  269.2 2.4 fusion.14
  (39 shorter events, 6.0 us)
Async XLA Ops:
  2.8 11.6 %copy-start.1 = (bf16[1,384,2048]{2,1,0:T(8,128)(2,1)S(1)}, bf16[1,384,2048]{2,1,0:T(8,128)(2,1)}, u32[]{:S(2)}) copy-start(bf16[1,384,2048]{2,1,0:T(8,128)(2,1)} %param.9) | copy-start | bytes 4718596
  3.0 45.5 %collective-permute-start = (bf16[2,384,1024]{2,1,0:T(8,128)(2,1)S(1)}, bf16[2,384,1024]{2,1,0:T(8,128)(2,1)}, u32[]{:S(2)}, u32[]{:S(2)}) collective-permute-start(bf16[2,384,1024]{2,1,0:T(8,128)(2,1)S(1)} %pad_maximum_fusion.3), channel_id=1, source_target_pairs={{0,1},{1,2},{2,3},{3,4},{4,5},{5,6},{6,7},{7,8},{8,9},{9,10},{10,1... | collective-permute-start | bytes 4718600 | tf_op jit(solution)/shard_map/ppermute | solution.py:20
  5.1 43.4 %collective-permute-start.1 = (bf16[2,384,1024]{2,1,0:T(8,128)(2,1)S(1)}, bf16[2,384,1024]{2,1,0:T(8,128)(2,1)}, u32[]{:S(2)}, u32[]{:S(2)}) collective-permute-start(bf16[2,384,1024]{2,1,0:T(8,128)(2,1)S(1)} %pad_maximum_fusion.3), channel_id=1, source_target_pairs={{0,63},{1,0},{2,1},{3,2},{4,3},{5,4},{6,5},{7,6},{8,7},{9,8},{10,9... | collective-permute-start | bytes 4718600 | tf_op jit(solution)/shard_map/ppermute | solution.py:20
  16.9 1.4 copy-start.2
  28.1 29.9 %copy-start.4 = (s32[3,5]{1,0:T(4,128)S(1)}, s32[3,5]{1,0:T(4,128)}, u32[]{:S(2)}) copy-start(s32[3,5]{1,0:T(4,128)} %param.10) | copy-start | bytes 184
  48.5 79.8 %all-to-all-start = ((bf16[4,6,64,1024]{3,0,1,2:T(4,128)(2,1)}), bf16[4,6,64,1024]{3,0,1,2:T(4,128)(2,1)S(1)}, u32[]{:S(2)}, u32[]{:S(2)}) async-start(bf16[4,6,64,1024]{3,0,1,2:T(4,128)(2,1)} %pad_maximum_fusion.1), calls=%async_computation | async-start | bytes 6291456 | tf_op jit(solution)/shard_map/all_to_all | solution.py:162
  58.9 74.8 %copy-start.5 = (s32[3,2]{0,1:T(2,128)S(1)}, s32[3,2]{0,1:T(2,128)}, u32[]{:S(2)}) copy-start(s32[3,2]{0,1:T(2,128)} %param.11) | copy-start | bytes 76
  128.3 36.7 %collective-permute-start.2 = (bf16[2,384,1024]{2,1,0:T(8,128)(2,1)}, bf16[2,384,1024]{2,1,0:T(8,128)(2,1)}, u32[]{:S(2)}, u32[]{:S(2)}) collective-permute-start(bf16[2,384,1024]{2,1,0:T(8,128)(2,1)} %get-tuple-element.31), channel_id=1, source_target_pairs={{0,63},{1,0},{2,1},{3,2},{4,3},{5,4},{6,5},{7,6},{8,7},{9,8},{10,9... | collective-permute-start | bytes 4718600 | tf_op jit(solution)/shard_map/ppermute | solution.py:20
  133.7 39.0 %collective-permute-start.3 = (bf16[2,384,1024]{2,1,0:T(8,128)(2,1)}, bf16[2,384,1024]{2,1,0:T(8,128)(2,1)}, u32[]{:S(2)}, u32[]{:S(2)}) collective-permute-start(bf16[2,384,1024]{2,1,0:T(8,128)(2,1)} %get-tuple-element.32), channel_id=1, source_target_pairs={{0,1},{1,2},{2,3},{3,4},{4,5},{5,6},{6,7},{7,8},{8,9},{9,10},{10,1... | collective-permute-start | bytes 4718600 | tf_op jit(solution)/shard_map/ppermute | solution.py:20
  173.9 5.5 %copy-start = (bf16[3,64,6,1,512]{4,2,1,0,3:T(8,128)(2,1)S(1)}, bf16[3,64,6,1,512]{4,2,1,0,3:T(8,128)(2,1)}, u32[]{:S(2)}) copy-start(bf16[3,64,6,1,512]{4,2,1,0,3:T(8,128)(2,1)} %get-tuple-element.35) | copy-start | bytes 3538948
  173.9 42.1 %all-to-all-start.1 = ((bf16[3,64,6,1,512]{4,2,0,3,1:T(8,128)(2,1)}), bf16[3,64,6,1,512]{4,2,0,3,1:T(8,128)(2,1)S(1)}, u32[]{:S(2)}, u32[]{:S(2)}) async-start(bf16[3,64,6,1,512]{4,2,0,3,1:T(8,128)(2,1)} %copy.48), calls=%async_computation.1 | async-start | bytes 3145728 | tf_op jit(solution)/shard_map/all_to_all | solution.py:204
  179.8 7.5 %copy-start.3 = (bf16[384,1024]{1,0:T(8,128)(2,1)S(1)}, bf16[384,1024]{1,0:T(8,128)(2,1)}, u32[]{:S(2)}) copy-start(bf16[384,1024]{1,0:T(8,128)(2,1)} %get-tuple-element.28) | copy-start | bytes 2359300
  179.8 29.5 %collective-permute-start.5 = (bf16[3,64,6,1,512]{4,1,3,2,0:T(8,128)(2,1)S(1)}, bf16[3,64,6,1,512]{4,1,3,2,0:T(8,128)(2,1)S(1)}, u32[]{:S(2)}, u32[]{:S(2)}) collective-permute-start(bf16[3,64,6,1,512]{4,1,3,2,0:T(8,128)(2,1)S(1)} %copy.47), channel_id=1, source_target_pairs={{0,192},{64,0},{128,64},{192,128},{1,193},{65,1},{129,65},{193,129... | collective-permute-start | bytes 3538952 | tf_op jit(solution)/shard_map/ppermute | solution.py:20
  189.0 72.8 %collective-permute-start.4 = (bf16[3,384,1024]{2,1,0:T(8,128)(2,1)}, bf16[3,384,1024]{2,1,0:T(8,128)(2,1)}, u32[]{:S(2)}, u32[]{:S(2)}) collective-permute-start(bf16[3,384,1024]{2,1,0:T(8,128)(2,1)} %pad_maximum_fusion.2), channel_id=1, source_target_pairs={{0,192},{64,0},{128,64},{192,128},{1,193},{65,1},{129,65},{193,129... | collective-permute-start | bytes 7077896 | tf_op jit(solution)/shard_map/ppermute | solution.py:20
  217.9 43.5 %all-to-all-start.2 = ((bf16[3,64,6,1,512]{4,2,0,3,1:T(8,128)(2,1)}), bf16[3,64,6,1,512]{4,2,0,3,1:T(8,128)(2,1)S(1)}, u32[]{:S(2)}, u32[]{:S(2)}) async-start(bf16[3,64,6,1,512]{4,2,0,3,1:T(8,128)(2,1)} %copy.49), calls=%async_computation.2 | async-start | bytes 3145728 | tf_op jit(solution)/shard_map/all_to_all | solution.py:207
  227.0 40.4 %collective-permute-start.6 = (bf16[3,1,6,64,512]{4,3,2,1,0:T(8,128)(2,1)}, bf16[3,1,6,64,512]{4,3,2,1,0:T(8,128)(2,1)S(1)}, u32[]{:S(2)}, u32[]{:S(2)}) collective-permute-start(bf16[3,1,6,64,512]{4,3,2,1,0:T(8,128)(2,1)} %copy.51), channel_id=1, source_target_pairs={{0,192},{64,0},{128,64},{192,128},{1,193},{65,1},{129,65},{193,129... | collective-permute-start | bytes 3538952 | tf_op jit(solution)/shard_map/ppermute | solution.py:20

commit v12 on v11

--- a/solution.py
+++ b/solution.py
@@ -206,12 +206,12 @@
     early, late = lax.optimization_barrier((early, late))
     early = lax.all_to_all(early, "seq", split_axis=1, concat_axis=3, tiled=True)
     late = shifted(late, "pipe", -1)
-    col_handed = jnp.concatenate(
-        [early.reshape(3, tokens, half), late.reshape(3, tokens, half)], axis=2
-    )
-
-    handed = jnp.concatenate([row_handed, col_handed], axis=2)
-    return (handed[0][None], handed[1][None], handed[2][None])
+    early = early.reshape(3, tokens, half)
+    late = late.reshape(3, tokens, half)
+    return tuple(
+        jnp.concatenate([row_handed[kind], early[kind], late[kind]], axis=1)[None]
+        for kind in range(3)
+    )
 
 
 def solution(mesh):

time: 272 us -> 275 us (1.011)
    all_to_all x1, waiting for transfers between devices: 30.3 us -> 0.01 us  [body(): lax.all_to_all(early, 'seq', split_axis=1, concat_axis=3, tiled=True)]
    ppermute x7, waiting for transfers between devices: 65.5 us -> 94.5 us  [shifted(): return lax.ppermute(value, axis, pairs)]
    broadcast_in_dim x0 -> x3, other arithmetic: none -> 3.92 us  [body(): jnp.concatenate([row_handed[kind], early[kind], late[kind]], axis=1)[None]]
  transfers between devices with their start and end apart: 10 -> 10, of which waited for: 8 -> 8; matrix products, arithmetic and copies ran while one was open for 12% -> 13% of each run, Pallas kernels for 13% -> 13%
where the time goes in v12:
time: 275 us; the launch traced here: 274 us
  waiting for transfers between devices  146 us (53%)
  starting transfers between devices  47.5 us (17%)
  Pallas kernels  35 us (13%)
  local copies, waits for them, and re-layouts  24.7 us (9%)
  other arithmetic  19.1 us (7%)
    ppermute x7, waiting for transfers between devices, shifted(): return lax.ppermute(value, axis, pairs)  94.5 us
    all_to_all x1, waiting for transfers between devices, body(): lax.all_to_all(sent, 'seq', split_axis=2, concat_axis=1, tiled=True)  45.1 us
    ppermute x7, starting transfers between devices, shifted(): return lax.ppermute(value, axis, pairs)  24.9 us
    pallas_call x1, Pallas kernels, row_side(): pl.pallas_call(row_kernel, grid=(HEADS_ROW,), in_specs=[plain, plain, sta...  24.3 us
    pallas_call x1, Pallas kernels, col_side(): pl.pallas_call(col_kernel, grid=(HEADS_COL,), in_specs=[part_block(0), pa...  10.7 us
    all_to_all x1, starting transfers between devices, body(): lax.all_to_all(sent, 'seq', split_axis=2, concat_axis=1, tiled=True)  9.46 us
    another operation x1, other arithmetic, body(): jnp.stack([item[:, row_width:] for item in (query_now, key_now, value_now...  8.39 us
    all_to_all x1, starting transfers between devices, body(): lax.all_to_all(early, 'seq', split_axis=1, concat_axis=3, tiled=True)  7.68 us
  transfers between devices with their start and end apart: 10, of which 8 were waited for; matrix products, arithmetic and copies ran while one was open for 13% of the time, Pallas kernels for 13%

profile of v12, /device:TPU:1, one launch (start us, length us, event | category | flops | bytes accessed | tf_op | source)
XLA Modules:
  0.0 273.6 jit_solution(11867266528531066648)
XLA Ops:
  0.6 2.2 slice_bitcast_fusion.3
  3.0 2.1 collective-permute-start
  5.1 9.3 %collective-permute-start.1 = (bf16[2,384,1024]{2,1,0:T(8,128)(2,1)S(1)}, bf16[2,384,1024]{2,1,0:T(8,128)(2,1)}, u32[]{:S(2)}, u32[]{:S(2)}) collective-permute-start(bf16[2,384,1024]{2,1,0:T(8,128)(2,1)S(1)} %pad_maximum_fusion.2), channel_id=1, source_target_pairs={{0,63},{1,0},{2,1},{3,2},{4,3},{5,4},{6,5},{7,6},{8,7},{9,8},{10,9... | collective-permute-start | bytes 4718600 | tf_op jit(solution)/shard_map/ppermute | solution.py:20
  15.7 1.2 copy.50
  19.6 8.4 %pad_maximum_fusion = bf16[4,6,64,1024]{3,0,1,2:T(4,128)(2,1)} fusion(bf16[1,6,64,1024]{3,0,1,2:T(2,128)(2,1)S(1)} %copy.51, bf16[1,6,64,1024]{3,0,1,2:T(2,128)(2,1)S(1)} %copy.50, bf16[1,6,64,1024]{3,0,1,2:T(2,128)(2,1)S(1)} %copy.49, bf16[1,6,64,1024]{3,0,1,2:T(2,128)(2,1)S(1)} %copy.48), kind=kLoop, calls=%fused_computation | loop fusion | flops 12582912 | bytes 6291456 | tf_op jit(solution)/shard_map/stack | solution.py:158
  28.0 20.5 %collective-permute-done.kp_ref.vp_ref = bf16[2,384,1024]{2,1,0:T(8,128)(2,1)} collective-permute-done((bf16[2,384,1024]{2,1,0:T(8,128)(2,1)S(1)}, bf16[2,384,1024]{2,1,0:T(8,128)(2,1)}, u32[]{:S(2)}, u32[]{:S(2)}) %collective-permute-start) | collective-permute-done | bytes 1572896 | tf_op jit(solution)/shard_map/ppermute | solution.py:20
  48.5 9.5 %all-to-all-start = ((bf16[4,6,64,1024]{3,0,1,2:T(4,128)(2,1)}), bf16[4,6,64,1024]{3,0,1,2:T(4,128)(2,1)S(1)}, u32[]{:S(2)}, u32[]{:S(2)}) async-start(bf16[4,6,64,1024]{3,0,1,2:T(4,128)(2,1)} %pad_maximum_fusion), calls=%async_computation | async-start | bytes 6291456 | tf_op jit(solution)/shard_map/all_to_all | solution.py:162
  58.9 24.3 %shard_map.85 = (bf16[384,1024]{1,0:T(8,128)(2,1)}, bf16[2,384,1024]{2,1,0:T(8,128)(2,1)}, f32[2,384,1024]{2,1,0:T(8,128)}, bf16[2,384,1024]{2,1,0:T(8,128)(2,1)}) custom-call(bf16[384,2048]{1,0:T(8,128)(2,1)} %bitcast.58, bf16[384,2048]{1,0:T(8,128)(2,1)} %bitcast.56, bf16[2,384,1024]{2,1,0:T(8,128)(2,1)} %collective-permute-done.kp_ref.vp_ref, ...), custom_call_target="tpu_custom_call" | custom-call | tf_op jit(solution)/shard_map/pallas_call | solution.py:97
  83.2 45.1 %all-to-all-done = bf16[4,6,64,1024]{3,0,1,2:T(4,128)(2,1)S(1)} async-done(((bf16[4,6,64,1024]{3,0,1,2:T(4,128)(2,1)}), bf16[4,6,64,1024]{3,0,1,2:T(4,128)(2,1)S(1)}, u32[]{:S(2)}, u32[]{:S(2)}) %all-to-all-start) | async-done | bytes 3145760 | tf_op jit(solution)/shard_map/all_to_all | solution.py:162
  128.3 5.4 %collective-permute-start.2 = (bf16[2,384,1024]{2,1,0:T(8,128)(2,1)}, bf16[2,384,1024]{2,1,0:T(8,128)(2,1)}, u32[]{:S(2)}, u32[]{:S(2)}) collective-permute-start(bf16[2,384,1024]{2,1,0:T(8,128)(2,1)} %get-tuple-element.31), channel_id=1, source_target_pairs={{0,63},{1,0},{2,1},{3,2},{4,3},{5,4},{6,5},{7,6},{8,7},{9,8},{10,9... | collective-permute-start | bytes 4718600 | tf_op jit(solution)/shard_map/ppermute | solution.py:20
  135.1 2.7 copy.53.q_ref.k_ref.v_ref.do_ref
  137.7 10.7 %shard_map.86 = bf16[3,384,1024]{2,1,0:T(8,128)(2,1)} custom-call(bf16[4,384,1024]{2,1,0:T(8,128)(2,1)} %copy.53.q_ref.k_ref.v_ref.do_ref, bf16[4,384,1024]{2,1,0:T(8,128)(2,1)} %copy.53.q_ref.k_ref.v_ref.do_ref, bf16[4,384,1024]{2,1,0:T(8,128)(2,1)} %copy.53.q_ref.k_ref.v_ref.do_ref, bf16[4,384,1024]{2,1,0:T(8,128)(2,1)} %copy.53.q_ref.k_ref.v_ref.do_ref, ...), custom_call_target="tpu_custom_call" | custom-call | tf_op jit(solution)/shard_map/pallas_call | solution.py:130
  148.5 3.6 %reshape.257 = bf16[3,64,6,1,1024]{4,2,1,0,3:T(8,128)(2,1)S(1)} reshape(bf16[3,384,1024]{2,1,0:T(8,128)(2,1)} %shard_map.86) | data formatting | bytes 4718592 | tf_op jit(solution)/shard_map/reshape | solution.py:191
  152.0 1.3 fusion.14
  153.4 11.7 %collective-permute-done.2 = bf16[2,384,1024]{2,1,0:T(8,128)(2,1)} collective-permute-done((bf16[2,384,1024]{2,1,0:T(8,128)(2,1)}, bf16[2,384,1024]{2,1,0:T(8,128)(2,1)}, u32[]{:S(2)}, u32[]{:S(2)}) %collective-permute-start.2) | collective-permute-done | bytes 1572896 | tf_op jit(solution)/shard_map/ppermute | solution.py:20
  165.0 7.6 %collective-permute-done.3 = bf16[2,384,1024]{2,1,0:T(8,128)(2,1)} collective-permute-done((bf16[2,384,1024]{2,1,0:T(8,128)(2,1)}, bf16[2,384,1024]{2,1,0:T(8,128)(2,1)}, u32[]{:S(2)}, u32[]{:S(2)}) %collective-permute-start.3) | collective-permute-done | bytes 1572896 | tf_op jit(solution)/shard_map/ppermute | solution.py:20
  172.7 1.2 copy.58
  173.9 5.5 %all-to-all-start.1 = ((bf16[3,64,6,1,512]{4,2,0,3,1:T(8,128)(2,1)}), bf16[3,64,6,1,512]{4,2,0,3,1:T(8,128)(2,1)S(1)}, u32[]{:S(2)}, u32[]{:S(2)}) async-start(bf16[3,64,6,1,512]{4,2,0,3,1:T(8,128)(2,1)} %copy.58), calls=%async_computation.1 | async-start | bytes 3145728 | tf_op jit(solution)/shard_map/all_to_all | solution.py:204
  179.8 3.9 %collective-permute-start.5 = (bf16[3,64,6,1,512]{4,1,3,2,0:T(8,128)(2,1)S(1)}, bf16[3,64,6,1,512]{4,1,3,2,0:T(8,128)(2,1)S(1)}, u32[]{:S(2)}, u32[]{:S(2)}) collective-permute-start(bf16[3,64,6,1,512]{4,1,3,2,0:T(8,128)(2,1)S(1)} %copy.57), channel_id=1, source_target_pairs={{0,192},{64,0},{128,64},{192,128},{1,193},{65,1},{129,65},{193,129... | collective-permute-start | bytes 3538952 | tf_op jit(solution)/shard_map/ppermute | solution.py:20
  183.7 3.7 %add_convert_fusion = bf16[2,384,1024]{2,1,0:T(8,128)(2,1)S(1)} fusion(bf16[2,384,1024]{2,1,0:T(8,128)(2,1)} %collective-permute-done.2, f32[2,384,1024]{2,1,0:T(8,128)} %get-tuple-element.29, bf16[2,384,1024]{2,1,0:T(8,128)(2,1)} %collective-permute-done.3), kind=kLoop, calls=%fused_computation.1 | loop fusion | flops 3932160 | bytes 7864320 | tf_op jit(solution)/shard_map/convert_element_type | solution.py:198
  187.4 1.6 pad_maximum_fusion.1
  189.1 20.3 %collective-permute-done.5 = bf16[3,64,6,1,512]{4,1,3,2,0:T(8,128)(2,1)S(1)} collective-permute-done((bf16[3,64,6,1,512]{4,1,3,2,0:T(8,128)(2,1)S(1)}, bf16[3,64,6,1,512]{4,1,3,2,0:T(8,128)(2,1)S(1)}, u32[]{:S(2)}, u32[]{:S(2)}) %collective-permute-start.5) | collective-permute-done | bytes 1179680 | tf_op jit(solution)/shard_map/ppermute | solution.py:20
  209.4 6.7 %all-to-all-done.1 = bf16[3,64,6,1,512]{4,2,0,3,1:T(8,128)(2,1)S(1)} async-done(((bf16[3,64,6,1,512]{4,2,0,3,1:T(8,128)(2,1)}), bf16[3,64,6,1,512]{4,2,0,3,1:T(8,128)(2,1)S(1)}, u32[]{:S(2)}, u32[]{:S(2)}) %all-to-all-start.1) | async-done | bytes 1179680 | tf_op jit(solution)/shard_map/all_to_all | solution.py:204
  216.1 1.8 copy.59
  217.9 7.7 %all-to-all-start.2 = ((bf16[3,64,6,1,512]{4,2,0,3,1:T(8,128)(2,1)}), bf16[3,64,6,1,512]{4,2,0,3,1:T(8,128)(2,1)S(1)}, u32[]{:S(2)}, u32[]{:S(2)}) async-start(bf16[3,64,6,1,512]{4,2,0,3,1:T(8,128)(2,1)} %copy.59), calls=%async_computation.2 | async-start | bytes 3145728 | tf_op jit(solution)/shard_map/all_to_all | solution.py:207
  226.0 4.2 %collective-permute-start.6 = (bf16[3,1,6,64,512]{4,3,2,1,0:T(8,128)(2,1)S(1)}, bf16[3,1,6,64,512]{4,3,2,1,0:T(8,128)(2,1)S(1)}, u32[]{:S(2)}, u32[]{:S(2)}) collective-permute-start(bf16[3,1,6,64,512]{4,3,2,1,0:T(8,128)(2,1)S(1)} %copy.61), channel_id=1, source_target_pairs={{0,192},{64,0},{128,64},{192,128},{1,193},{65,1},{129,65},{193,129... | collective-permute-start | bytes 3538952 | tf_op jit(solution)/shard_map/ppermute | solution.py:20
  230.2 17.3 %collective-permute-done.4 = bf16[3,384,1024]{2,1,0:T(8,128)(2,1)} collective-permute-done((bf16[3,384,1024]{2,1,0:T(8,128)(2,1)}, bf16[3,384,1024]{2,1,0:T(8,128)(2,1)}, u32[]{:S(2)}, u32[]{:S(2)}) %collective-permute-start.4) | collective-permute-done | bytes 2359328 | tf_op jit(solution)/shard_map/ppermute | solution.py:20
  247.4 2.7 %slice_bitcast_fusion = (bf16[384,1024]{1,0:T(8,128)(2,1)S(1)}, bf16[384,1024]{1,0:T(8,128)(2,1)S(1)}, bf16[384,1024]{1,0:T(8,128)(2,1)}) fusion(bf16[3,384,1024]{2,1,0:T(8,128)(2,1)} %collective-permute-done.4), kind=kLoop, calls=%fused_computation.8 | loop fusion | bytes 4718592 | tf_op jit(solution)/shard_map/squeeze | solution.py:212
  250.2 17.1 %collective-permute-done.6 = bf16[3,1,6,64,512]{4,3,2,1,0:T(8,128)(2,1)S(1)} collective-permute-done((bf16[3,1,6,64,512]{4,3,2,1,0:T(8,128)(2,1)S(1)}, bf16[3,1,6,64,512]{4,3,2,1,0:T(8,128)(2,1)S(1)}, u32[]{:S(2)}, u32[]{:S(2)}) %collective-permute-start.6) | collective-permute-done | bytes 1179680 | tf_op jit(solution)/shard_map/ppermute | solution.py:20
  269.7 1.3 maximum_bitcast_fusion
  271.0 1.3 maximum_bitcast_fusion.1
  272.3 1.3 maximum_bitcast_fusion.2
  (51 shorter events, 9.5 us)
Async XLA Ops:
  2.8 11.6 %copy-start.1 = (bf16[1,384,2048]{2,1,0:T(8,128)(2,1)S(1)}, bf16[1,384,2048]{2,1,0:T(8,128)(2,1)}, u32[]{:S(2)}) copy-start(bf16[1,384,2048]{2,1,0:T(8,128)(2,1)} %param.9) | copy-start | bytes 4718596
  3.0 45.5 %collective-permute-start = (bf16[2,384,1024]{2,1,0:T(8,128)(2,1)S(1)}, bf16[2,384,1024]{2,1,0:T(8,128)(2,1)}, u32[]{:S(2)}, u32[]{:S(2)}) collective-permute-start(bf16[2,384,1024]{2,1,0:T(8,128)(2,1)S(1)} %pad_maximum_fusion.2), channel_id=1, source_target_pairs={{0,1},{1,2},{2,3},{3,4},{4,5},{5,6},{6,7},{7,8},{8,9},{9,10},{10,1... | collective-permute-start | bytes 4718600 | tf_op jit(solution)/shard_map/ppermute | solution.py:20
  5.1 43.4 %collective-permute-start.1 = (bf16[2,384,1024]{2,1,0:T(8,128)(2,1)S(1)}, bf16[2,384,1024]{2,1,0:T(8,128)(2,1)}, u32[]{:S(2)}, u32[]{:S(2)}) collective-permute-start(bf16[2,384,1024]{2,1,0:T(8,128)(2,1)S(1)} %pad_maximum_fusion.2), channel_id=1, source_target_pairs={{0,63},{1,0},{2,1},{3,2},{4,3},{5,4},{6,5},{7,6},{8,7},{9,8},{10,9... | collective-permute-start | bytes 4718600 | tf_op jit(solution)/shard_map/ppermute | solution.py:20
  16.9 1.4 copy-start.2
  28.0 30.0 %copy-start.7 = (s32[3,5]{1,0:T(4,128)S(1)}, s32[3,5]{1,0:T(4,128)}, u32[]{:S(2)}) copy-start(s32[3,5]{1,0:T(4,128)} %param.10) | copy-start | bytes 184
  48.5 79.8 %all-to-all-start = ((bf16[4,6,64,1024]{3,0,1,2:T(4,128)(2,1)}), bf16[4,6,64,1024]{3,0,1,2:T(4,128)(2,1)S(1)}, u32[]{:S(2)}, u32[]{:S(2)}) async-start(bf16[4,6,64,1024]{3,0,1,2:T(4,128)(2,1)} %pad_maximum_fusion), calls=%async_computation | async-start | bytes 6291456 | tf_op jit(solution)/shard_map/all_to_all | solution.py:162
  58.9 74.8 %copy-start.8 = (s32[3,2]{0,1:T(2,128)S(1)}, s32[3,2]{0,1:T(2,128)}, u32[]{:S(2)}) copy-start(s32[3,2]{0,1:T(2,128)} %param.11) | copy-start | bytes 76
  128.3 36.7 %collective-permute-start.2 = (bf16[2,384,1024]{2,1,0:T(8,128)(2,1)}, bf16[2,384,1024]{2,1,0:T(8,128)(2,1)}, u32[]{:S(2)}, u32[]{:S(2)}) collective-permute-start(bf16[2,384,1024]{2,1,0:T(8,128)(2,1)} %get-tuple-element.31), channel_id=1, source_target_pairs={{0,63},{1,0},{2,1},{3,2},{4,3},{5,4},{6,5},{7,6},{8,7},{9,8},{10,9... | collective-permute-start | bytes 4718600 | tf_op jit(solution)/shard_map/ppermute | solution.py:20
  133.7 39.0 %collective-permute-start.3 = (bf16[2,384,1024]{2,1,0:T(8,128)(2,1)}, bf16[2,384,1024]{2,1,0:T(8,128)(2,1)}, u32[]{:S(2)}, u32[]{:S(2)}) collective-permute-start(bf16[2,384,1024]{2,1,0:T(8,128)(2,1)} %get-tuple-element.32), channel_id=1, source_target_pairs={{0,1},{1,2},{2,3},{3,4},{4,5},{5,6},{6,7},{7,8},{8,9},{9,10},{10,1... | collective-permute-start | bytes 4718600 | tf_op jit(solution)/shard_map/ppermute | solution.py:20
  173.9 5.5 %copy-start = (bf16[3,64,6,1,512]{4,2,1,0,3:T(8,128)(2,1)S(1)}, bf16[3,64,6,1,512]{4,2,1,0,3:T(8,128)(2,1)}, u32[]{:S(2)}) copy-start(bf16[3,64,6,1,512]{4,2,1,0,3:T(8,128)(2,1)} %get-tuple-element.35) | copy-start | bytes 3538948
  173.9 42.1 %all-to-all-start.1 = ((bf16[3,64,6,1,512]{4,2,0,3,1:T(8,128)(2,1)}), bf16[3,64,6,1,512]{4,2,0,3,1:T(8,128)(2,1)S(1)}, u32[]{:S(2)}, u32[]{:S(2)}) async-start(bf16[3,64,6,1,512]{4,2,0,3,1:T(8,128)(2,1)} %copy.58), calls=%async_computation.1 | async-start | bytes 3145728 | tf_op jit(solution)/shard_map/all_to_all | solution.py:204
  179.8 7.5 %copy-start.6 = (bf16[384,1024]{1,0:T(8,128)(2,1)S(1)}, bf16[384,1024]{1,0:T(8,128)(2,1)}, u32[]{:S(2)}) copy-start(bf16[384,1024]{1,0:T(8,128)(2,1)} %get-tuple-element.28) | copy-start | bytes 2359300
  179.8 29.5 %collective-permute-start.5 = (bf16[3,64,6,1,512]{4,1,3,2,0:T(8,128)(2,1)S(1)}, bf16[3,64,6,1,512]{4,1,3,2,0:T(8,128)(2,1)S(1)}, u32[]{:S(2)}, u32[]{:S(2)}) collective-permute-start(bf16[3,64,6,1,512]{4,1,3,2,0:T(8,128)(2,1)S(1)} %copy.57), channel_id=1, source_target_pairs={{0,192},{64,0},{128,64},{192,128},{1,193},{65,1},{129,65},{193,129... | collective-permute-start | bytes 3538952 | tf_op jit(solution)/shard_map/ppermute | solution.py:20
  189.0 58.4 %collective-permute-start.4 = (bf16[3,384,1024]{2,1,0:T(8,128)(2,1)}, bf16[3,384,1024]{2,1,0:T(8,128)(2,1)}, u32[]{:S(2)}, u32[]{:S(2)}) collective-permute-start(bf16[3,384,1024]{2,1,0:T(8,128)(2,1)} %pad_maximum_fusion.1), channel_id=1, source_target_pairs={{0,192},{64,0},{128,64},{192,128},{1,193},{65,1},{129,65},{193,129... | collective-permute-start | bytes 7077896 | tf_op jit(solution)/shard_map/ppermute | solution.py:20
  217.9 50.4 %all-to-all-start.2 = ((bf16[3,64,6,1,512]{4,2,0,3,1:T(8,128)(2,1)}), bf16[3,64,6,1,512]{4,2,0,3,1:T(8,128)(2,1)S(1)}, u32[]{:S(2)}, u32[]{:S(2)}) async-start(bf16[3,64,6,1,512]{4,2,0,3,1:T(8,128)(2,1)} %copy.59), calls=%async_computation.2 | async-start | bytes 3145728 | tf_op jit(solution)/shard_map/all_to_all | solution.py:207
  226.0 41.4 %collective-permute-start.6 = (bf16[3,1,6,64,512]{4,3,2,1,0:T(8,128)(2,1)S(1)}, bf16[3,1,6,64,512]{4,3,2,1,0:T(8,128)(2,1)S(1)}, u32[]{:S(2)}, u32[]{:S(2)}) collective-permute-start(bf16[3,1,6,64,512]{4,3,2,1,0:T(8,128)(2,1)S(1)} %copy.61), channel_id=1, source_target_pairs={{0,192},{64,0},{128,64},{192,128},{1,193},{65,1},{129,65},{193,129... | collective-permute-start | bytes 3538952 | tf_op jit(solution)/shard_map/ppermute | solution.py:20
  268.4 1.1 copy-start.3
  268.4 1.2 copy-start.5
  269.7 1.3 copy-start.4

commit v13 on v11

--- a/solution.py
+++ b/solution.py
@@ -203,7 +203,6 @@
     early = shifted(early, "pipe", -1)
     late = lax.all_to_all(late, "seq", split_axis=1, concat_axis=3, tiled=True)
 
-    early, late = lax.optimization_barrier((early, late))
     early = lax.all_to_all(early, "seq", split_axis=1, concat_axis=3, tiled=True)
     late = shifted(late, "pipe", -1)
     col_handed = jnp.concatenate(

time: 272 us -> 272 us (level)
    all_to_all x1, waiting for transfers between devices: 30.3 us -> 34.3 us  [body(): lax.all_to_all(early, 'seq', split_axis=1, concat_axis=3, tiled=True)]
    optimization_barrier x2 -> x0, local copies, waits for them, and re-layouts: 3.2 us -> none  [body(): early, late = lax.optimization_barrier((early, late))]
where the time goes in v13:
time: 272 us
  waiting for transfers between devices  148 us (54%)
  starting transfers between devices  47.4 us (17%)
  Pallas kernels  35 us (13%)
  local copies, waits for them, and re-layouts  23.4 us (9%)
  other arithmetic  17.2 us (6%)
    ppermute x7, waiting for transfers between devices, shifted(): return lax.ppermute(value, axis, pairs)  63.3 us
    all_to_all x1, waiting for transfers between devices, body(): lax.all_to_all(sent, 'seq', split_axis=2, concat_axis=1, tiled=True)  45.1 us
    all_to_all x1, waiting for transfers between devices, body(): lax.all_to_all(early, 'seq', split_axis=1, concat_axis=3, tiled=True)  34.3 us
    pallas_call x1, Pallas kernels, row_side(): pl.pallas_call(row_kernel, grid=(HEADS_ROW,), in_specs=[plain, plain, sta...  24.3 us
    ppermute x7, starting transfers between devices, shifted(): return lax.ppermute(value, axis, pairs)  23 us
    pallas_call x1, Pallas kernels, col_side(): pl.pallas_call(col_kernel, grid=(HEADS_COL,), in_specs=[part_block(0), pa...  10.7 us
    all_to_all x1, starting transfers between devices, body(): lax.all_to_all(early, 'seq', split_axis=1, concat_axis=3, tiled=True)  9.49 us
    all_to_all x1, starting transfers between devices, body(): lax.all_to_all(sent, 'seq', split_axis=2, concat_axis=1, tiled=True)  9.46 us
  transfers between devices with their start and end apart: 10, of which 8 were waited for; matrix products, arithmetic and copies ran while one was open for 12% of the time, Pallas kernels for 13%

profile of v13, /device:TPU:1, one launch (start us, length us, event | category | flops | bytes accessed | tf_op | source)
XLA Modules:
  0.0 271.6 jit_solution(4692005295289242380)
XLA Ops:
  0.6 2.2 slice_bitcast_fusion
  3.0 2.1 collective-permute-start
  5.1 9.3 %collective-permute-start.1 = (bf16[2,384,1024]{2,1,0:T(8,128)(2,1)S(1)}, bf16[2,384,1024]{2,1,0:T(8,128)(2,1)}, u32[]{:S(2)}, u32[]{:S(2)}) collective-permute-start(bf16[2,384,1024]{2,1,0:T(8,128)(2,1)S(1)} %pad_maximum_fusion.3), channel_id=1, source_target_pairs={{0,63},{1,0},{2,1},{3,2},{4,3},{5,4},{6,5},{7,6},{8,7},{9,8},{10,9... | collective-permute-start | bytes 4718600 | tf_op jit(solution)/shard_map/ppermute | solution.py:20
  15.7 1.2 copy.40
  18.4 1.2 copy.38
  19.6 8.5 %pad_maximum_fusion.1 = bf16[4,6,64,1024]{3,0,1,2:T(4,128)(2,1)} fusion(bf16[1,6,64,1024]{3,0,1,2:T(2,128)(2,1)S(1)} %copy.41, bf16[1,6,64,1024]{3,0,1,2:T(2,128)(2,1)S(1)} %copy.40, bf16[1,6,64,1024]{3,0,1,2:T(2,128)(2,1)S(1)} %copy.39, bf16[1,6,64,1024]{3,0,1,2:T(2,128)(2,1)S(1)} %copy.38), kind=kLoop, calls=%fused_computation.1 | loop fusion | flops 12582912 | bytes 6291456 | tf_op jit(solution)/shard_map/stack | solution.py:158
  28.1 20.4 %collective-permute-done.kp_ref.vp_ref = bf16[2,384,1024]{2,1,0:T(8,128)(2,1)} collective-permute-done((bf16[2,384,1024]{2,1,0:T(8,128)(2,1)S(1)}, bf16[2,384,1024]{2,1,0:T(8,128)(2,1)}, u32[]{:S(2)}, u32[]{:S(2)}) %collective-permute-start) | collective-permute-done | bytes 1572896 | tf_op jit(solution)/shard_map/ppermute | solution.py:20
  48.5 9.5 %all-to-all-start = ((bf16[4,6,64,1024]{3,0,1,2:T(4,128)(2,1)}), bf16[4,6,64,1024]{3,0,1,2:T(4,128)(2,1)S(1)}, u32[]{:S(2)}, u32[]{:S(2)}) async-start(bf16[4,6,64,1024]{3,0,1,2:T(4,128)(2,1)} %pad_maximum_fusion.1), calls=%async_computation | async-start | bytes 6291456 | tf_op jit(solution)/shard_map/all_to_all | solution.py:162
  58.9 24.3 %shard_map.85 = (bf16[384,1024]{1,0:T(8,128)(2,1)}, bf16[2,384,1024]{2,1,0:T(8,128)(2,1)}, f32[2,384,1024]{2,1,0:T(8,128)}, bf16[2,384,1024]{2,1,0:T(8,128)(2,1)}) custom-call(bf16[384,2048]{1,0:T(8,128)(2,1)} %bitcast.43, bf16[384,2048]{1,0:T(8,128)(2,1)} %bitcast.41, bf16[2,384,1024]{2,1,0:T(8,128)(2,1)} %collective-permute-done.kp_ref.vp_ref, ...), custom_call_target="tpu_custom_call" | custom-call | tf_op jit(solution)/shard_map/pallas_call | solution.py:97
  83.2 45.1 %all-to-all-done = bf16[4,6,64,1024]{3,0,1,2:T(4,128)(2,1)S(1)} async-done(((bf16[4,6,64,1024]{3,0,1,2:T(4,128)(2,1)}), bf16[4,6,64,1024]{3,0,1,2:T(4,128)(2,1)S(1)}, u32[]{:S(2)}, u32[]{:S(2)}) %all-to-all-start) | async-done | bytes 3145760 | tf_op jit(solution)/shard_map/all_to_all | solution.py:162
  128.3 5.4 %collective-permute-start.2 = (bf16[2,384,1024]{2,1,0:T(8,128)(2,1)}, bf16[2,384,1024]{2,1,0:T(8,128)(2,1)}, u32[]{:S(2)}, u32[]{:S(2)}) collective-permute-start(bf16[2,384,1024]{2,1,0:T(8,128)(2,1)} %get-tuple-element.29), channel_id=1, source_target_pairs={{0,63},{1,0},{2,1},{3,2},{4,3},{5,4},{6,5},{7,6},{8,7},{9,8},{10,9... | collective-permute-start | bytes 4718600 | tf_op jit(solution)/shard_map/ppermute | solution.py:20
  135.1 2.7 copy.43.q_ref.k_ref.v_ref.do_ref
  137.7 10.7 %shard_map.86 = bf16[3,384,1024]{2,1,0:T(8,128)(2,1)} custom-call(bf16[4,384,1024]{2,1,0:T(8,128)(2,1)} %copy.43.q_ref.k_ref.v_ref.do_ref, bf16[4,384,1024]{2,1,0:T(8,128)(2,1)} %copy.43.q_ref.k_ref.v_ref.do_ref, bf16[4,384,1024]{2,1,0:T(8,128)(2,1)} %copy.43.q_ref.k_ref.v_ref.do_ref, bf16[4,384,1024]{2,1,0:T(8,128)(2,1)} %copy.43.q_ref.k_ref.v_ref.do_ref, ...), custom_call_target="tpu_custom_call" | custom-call | tf_op jit(solution)/shard_map/pallas_call | solution.py:130
  148.5 3.6 %reshape.249 = bf16[3,64,6,1,1024]{4,2,1,0,3:T(8,128)(2,1)S(1)} reshape(bf16[3,384,1024]{2,1,0:T(8,128)(2,1)} %shard_map.86) | data formatting | bytes 4718592 | tf_op jit(solution)/shard_map/reshape | solution.py:191
  152.1 1.3 fusion.15
  153.4 11.6 %collective-permute-done.2 = bf16[2,384,1024]{2,1,0:T(8,128)(2,1)} collective-permute-done((bf16[2,384,1024]{2,1,0:T(8,128)(2,1)}, bf16[2,384,1024]{2,1,0:T(8,128)(2,1)}, u32[]{:S(2)}, u32[]{:S(2)}) %collective-permute-start.2) | collective-permute-done | bytes 1572896 | tf_op jit(solution)/shard_map/ppermute | solution.py:20
  165.0 7.6 %collective-permute-done.3 = bf16[2,384,1024]{2,1,0:T(8,128)(2,1)} collective-permute-done((bf16[2,384,1024]{2,1,0:T(8,128)(2,1)}, bf16[2,384,1024]{2,1,0:T(8,128)(2,1)}, u32[]{:S(2)}, u32[]{:S(2)}) %collective-permute-start.3) | collective-permute-done | bytes 1572896 | tf_op jit(solution)/shard_map/ppermute | solution.py:20
  172.7 1.2 copy.50
  173.9 5.5 %all-to-all-start.2 = ((bf16[3,64,6,1,512]{4,2,0,3,1:T(8,128)(2,1)}), bf16[3,64,6,1,512]{4,2,0,3,1:T(8,128)(2,1)S(1)}, u32[]{:S(2)}, u32[]{:S(2)}) async-start(bf16[3,64,6,1,512]{4,2,0,3,1:T(8,128)(2,1)} %copy.50), calls=%async_computation.2 | async-start | bytes 3145728 | tf_op jit(solution)/shard_map/all_to_all | solution.py:204
  179.8 3.9 %collective-permute-start.5 = (bf16[3,64,6,1,512]{4,1,3,2,0:T(8,128)(2,1)S(1)}, bf16[3,64,6,1,512]{4,1,3,2,0:T(8,128)(2,1)S(1)}, u32[]{:S(2)}, u32[]{:S(2)}) collective-permute-start(bf16[3,64,6,1,512]{4,1,3,2,0:T(8,128)(2,1)S(1)} %copy.47), channel_id=1, source_target_pairs={{0,192},{64,0},{128,64},{192,128},{1,193},{65,1},{129,65},{193,129... | collective-permute-start | bytes 3538952 | tf_op jit(solution)/shard_map/ppermute | solution.py:20
  183.7 3.7 %add_convert_fusion = bf16[2,384,1024]{2,1,0:T(8,128)(2,1)S(1)} fusion(bf16[2,384,1024]{2,1,0:T(8,128)(2,1)} %collective-permute-done.2, f32[2,384,1024]{2,1,0:T(8,128)} %get-tuple-element.27, bf16[2,384,1024]{2,1,0:T(8,128)(2,1)} %collective-permute-done.3), kind=kLoop, calls=%fused_computation.2 | loop fusion | flops 3932160 | bytes 7864320 | tf_op jit(solution)/shard_map/convert_element_type | solution.py:198
  187.4 1.6 pad_maximum_fusion.2
  189.1 20.3 %collective-permute-done.5 = bf16[3,64,6,1,512]{4,1,3,2,0:T(8,128)(2,1)S(1)} collective-permute-done((bf16[3,64,6,1,512]{4,1,3,2,0:T(8,128)(2,1)S(1)}, bf16[3,64,6,1,512]{4,1,3,2,0:T(8,128)(2,1)S(1)}, u32[]{:S(2)}, u32[]{:S(2)}) %collective-permute-start.5) | collective-permute-done | bytes 1179680 | tf_op jit(solution)/shard_map/ppermute | solution.py:20
  209.4 1.8 copy.48
  211.2 4.9 %all-to-all-done.2 = bf16[3,64,6,1,512]{4,2,0,3,1:T(8,128)(2,1)S(1)} async-done(((bf16[3,64,6,1,512]{4,2,0,3,1:T(8,128)(2,1)}), bf16[3,64,6,1,512]{4,2,0,3,1:T(8,128)(2,1)S(1)}, u32[]{:S(2)}, u32[]{:S(2)}) %all-to-all-start.2) | async-done | bytes 1179680 | tf_op jit(solution)/shard_map/all_to_all | solution.py:204
  216.1 9.5 %all-to-all-start.1 = ((bf16[3,64,6,1,512]{4,2,0,3,1:T(8,128)(2,1)}), bf16[3,64,6,1,512]{4,2,0,3,1:T(8,128)(2,1)S(1)}, u32[]{:S(2)}, u32[]{:S(2)}) async-start(bf16[3,64,6,1,512]{4,2,0,3,1:T(8,128)(2,1)} %copy.48), calls=%async_computation.1 | async-start | bytes 3145728 | tf_op jit(solution)/shard_map/all_to_all | solution.py:206
  225.6 1.4 copy.51
  227.0 2.3 collective-permute-start.6
  229.3 34.3 %all-to-all-done.1 = bf16[3,64,6,1,512]{4,2,0,3,1:T(8,128)(2,1)S(1)} async-done(((bf16[3,64,6,1,512]{4,2,0,3,1:T(8,128)(2,1)}), bf16[3,64,6,1,512]{4,2,0,3,1:T(8,128)(2,1)S(1)}, u32[]{:S(2)}, u32[]{:S(2)}) %all-to-all-start.1) | async-done | bytes 1179680 | tf_op jit(solution)/shard_map/all_to_all | solution.py:206
  264.0 3.3 %collective-permute-done.6 = bf16[3,1,6,64,512]{4,3,2,1,0:T(8,128)(2,1)S(1)} collective-permute-done((bf16[3,1,6,64,512]{4,3,2,1,0:T(8,128)(2,1)}, bf16[3,1,6,64,512]{4,3,2,1,0:T(8,128)(2,1)S(1)}, u32[]{:S(2)}, u32[]{:S(2)}) %collective-permute-start.6) | collective-permute-done | bytes 1179680 | tf_op jit(solution)/shard_map/ppermute | solution.py:20
  267.3 1.9 pad_maximum_fusion
  269.2 2.4 fusion.14
  (39 shorter events, 6.0 us)
Async XLA Ops:
  2.8 11.6 %copy-start.1 = (bf16[1,384,2048]{2,1,0:T(8,128)(2,1)S(1)}, bf16[1,384,2048]{2,1,0:T(8,128)(2,1)}, u32[]{:S(2)}) copy-start(bf16[1,384,2048]{2,1,0:T(8,128)(2,1)} %param.9) | copy-start | bytes 4718596
  3.0 45.5 %collective-permute-start = (bf16[2,384,1024]{2,1,0:T(8,128)(2,1)S(1)}, bf16[2,384,1024]{2,1,0:T(8,128)(2,1)}, u32[]{:S(2)}, u32[]{:S(2)}) collective-permute-start(bf16[2,384,1024]{2,1,0:T(8,128)(2,1)S(1)} %pad_maximum_fusion.3), channel_id=1, source_target_pairs={{0,1},{1,2},{2,3},{3,4},{4,5},{5,6},{6,7},{7,8},{8,9},{9,10},{10,1... | collective-permute-start | bytes 4718600 | tf_op jit(solution)/shard_map/ppermute | solution.py:20
  5.1 43.4 %collective-permute-start.1 = (bf16[2,384,1024]{2,1,0:T(8,128)(2,1)S(1)}, bf16[2,384,1024]{2,1,0:T(8,128)(2,1)}, u32[]{:S(2)}, u32[]{:S(2)}) collective-permute-start(bf16[2,384,1024]{2,1,0:T(8,128)(2,1)S(1)} %pad_maximum_fusion.3), channel_id=1, source_target_pairs={{0,63},{1,0},{2,1},{3,2},{4,3},{5,4},{6,5},{7,6},{8,7},{9,8},{10,9... | collective-permute-start | bytes 4718600 | tf_op jit(solution)/shard_map/ppermute | solution.py:20
  16.9 1.4 copy-start.2
  28.1 29.9 %copy-start.4 = (s32[3,5]{1,0:T(4,128)S(1)}, s32[3,5]{1,0:T(4,128)}, u32[]{:S(2)}) copy-start(s32[3,5]{1,0:T(4,128)} %param.10) | copy-start | bytes 184
  48.5 79.8 %all-to-all-start = ((bf16[4,6,64,1024]{3,0,1,2:T(4,128)(2,1)}), bf16[4,6,64,1024]{3,0,1,2:T(4,128)(2,1)S(1)}, u32[]{:S(2)}, u32[]{:S(2)}) async-start(bf16[4,6,64,1024]{3,0,1,2:T(4,128)(2,1)} %pad_maximum_fusion.1), calls=%async_computation | async-start | bytes 6291456 | tf_op jit(solution)/shard_map/all_to_all | solution.py:162
  58.9 74.8 %copy-start.5 = (s32[3,2]{0,1:T(2,128)S(1)}, s32[3,2]{0,1:T(2,128)}, u32[]{:S(2)}) copy-start(s32[3,2]{0,1:T(2,128)} %param.11) | copy-start | bytes 76
  128.3 36.7 %collective-permute-start.2 = (bf16[2,384,1024]{2,1,0:T(8,128)(2,1)}, bf16[2,384,1024]{2,1,0:T(8,128)(2,1)}, u32[]{:S(2)}, u32[]{:S(2)}) collective-permute-start(bf16[2,384,1024]{2,1,0:T(8,128)(2,1)} %get-tuple-element.29), channel_id=1, source_target_pairs={{0,63},{1,0},{2,1},{3,2},{4,3},{5,4},{6,5},{7,6},{8,7},{9,8},{10,9... | collective-permute-start | bytes 4718600 | tf_op jit(solution)/shard_map/ppermute | solution.py:20
  133.7 39.0 %collective-permute-start.3 = (bf16[2,384,1024]{2,1,0:T(8,128)(2,1)}, bf16[2,384,1024]{2,1,0:T(8,128)(2,1)}, u32[]{:S(2)}, u32[]{:S(2)}) collective-permute-start(bf16[2,384,1024]{2,1,0:T(8,128)(2,1)} %get-tuple-element.30), channel_id=1, source_target_pairs={{0,1},{1,2},{2,3},{3,4},{4,5},{5,6},{6,7},{7,8},{8,9},{9,10},{10,1... | collective-permute-start | bytes 4718600 | tf_op jit(solution)/shard_map/ppermute | solution.py:20
  173.9 5.5 %copy-start = (bf16[3,64,6,1,512]{4,2,1,0,3:T(8,128)(2,1)S(1)}, bf16[3,64,6,1,512]{4,2,1,0,3:T(8,128)(2,1)}, u32[]{:S(2)}) copy-start(bf16[3,64,6,1,512]{4,2,1,0,3:T(8,128)(2,1)} %get-tuple-element.33) | copy-start | bytes 3538948
  173.9 42.1 %all-to-all-start.2 = ((bf16[3,64,6,1,512]{4,2,0,3,1:T(8,128)(2,1)}), bf16[3,64,6,1,512]{4,2,0,3,1:T(8,128)(2,1)S(1)}, u32[]{:S(2)}, u32[]{:S(2)}) async-start(bf16[3,64,6,1,512]{4,2,0,3,1:T(8,128)(2,1)} %copy.50), calls=%async_computation.2 | async-start | bytes 3145728 | tf_op jit(solution)/shard_map/all_to_all | solution.py:204
  179.8 7.5 %copy-start.3 = (bf16[384,1024]{1,0:T(8,128)(2,1)S(1)}, bf16[384,1024]{1,0:T(8,128)(2,1)}, u32[]{:S(2)}) copy-start(bf16[384,1024]{1,0:T(8,128)(2,1)} %get-tuple-element.26) | copy-start | bytes 2359300
  179.8 29.5 %collective-permute-start.5 = (bf16[3,64,6,1,512]{4,1,3,2,0:T(8,128)(2,1)S(1)}, bf16[3,64,6,1,512]{4,1,3,2,0:T(8,128)(2,1)S(1)}, u32[]{:S(2)}, u32[]{:S(2)}) collective-permute-start(bf16[3,64,6,1,512]{4,1,3,2,0:T(8,128)(2,1)S(1)} %copy.47), channel_id=1, source_target_pairs={{0,192},{64,0},{128,64},{192,128},{1,193},{65,1},{129,65},{193,129... | collective-permute-start | bytes 3538952 | tf_op jit(solution)/shard_map/ppermute | solution.py:20
  189.0 75.0 %collective-permute-start.4 = (bf16[3,384,1024]{2,1,0:T(8,128)(2,1)}, bf16[3,384,1024]{2,1,0:T(8,128)(2,1)}, u32[]{:S(2)}, u32[]{:S(2)}) collective-permute-start(bf16[3,384,1024]{2,1,0:T(8,128)(2,1)} %pad_maximum_fusion.2), channel_id=1, source_target_pairs={{0,192},{64,0},{128,64},{192,128},{1,193},{65,1},{129,65},{193,129... | collective-permute-start | bytes 7077896 | tf_op jit(solution)/shard_map/ppermute | solution.py:20
  216.1 47.5 %all-to-all-start.1 = ((bf16[3,64,6,1,512]{4,2,0,3,1:T(8,128)(2,1)}), bf16[3,64,6,1,512]{4,2,0,3,1:T(8,128)(2,1)S(1)}, u32[]{:S(2)}, u32[]{:S(2)}) async-start(bf16[3,64,6,1,512]{4,2,0,3,1:T(8,128)(2,1)} %copy.48), calls=%async_computation.1 | async-start | bytes 3145728 | tf_op jit(solution)/shard_map/all_to_all | solution.py:206
  227.0 40.4 %collective-permute-start.6 = (bf16[3,1,6,64,512]{4,3,2,1,0:T(8,128)(2,1)}, bf16[3,1,6,64,512]{4,3,2,1,0:T(8,128)(2,1)S(1)}, u32[]{:S(2)}, u32[]{:S(2)}) collective-permute-start(bf16[3,1,6,64,512]{4,3,2,1,0:T(8,128)(2,1)} %copy.51), channel_id=1, source_target_pairs={{0,192},{64,0},{128,64},{192,128},{1,193},{65,1},{129,65},{193,129... | collective-permute-start | bytes 3538952 | tf_op jit(solution)/shard_map/ppermute | solution.py:20
